TPU v7x, 128 devices: a whole 4x4x4 slice. The times are simulated.
128 devices in a mesh: prow: 4 (over y), pcol: 32 (over z, x, core).
Axes of the slice: x: 4, y: 4, z: 4, core: 2. Of those that a mesh axis runs over, the one named last changes fastest.
Arguments:
- diag_blocks: float32 [2, 64, 64], P(None, 'prow')
- panel_rows: float32 [2, 64, 8192], P(None, None, ('prow', 'pcol')), may hold values from -18 to 18
- child_map: int32 [2, 128], replicated, may hold values from 0 to 255, as said below
- front: float32 [16384, 16384], P('prow', 'pcol'), may hold values from -6 to 6
Outputs:
- updated_front: float32 [16384, 16384], P('prow', 'pcol')
Inputs may be any that keep to these rules, and one draw needn't show every extreme that they name: `child_map`: for each panel and each g below 4, the child blocks 32 * g to 32 * g + 31 map, in rising order, to distinct block rows from g * 64 to g * 64 + 63, the first and the last of these always among them.
All inputs are finite; a program needn't handle non-finite values.
Results may differ from a plain program's by a relative error of at most 0.0003.
Values sent between devices are 32-bit elements; how exact they have to be, the bound alone decides.
No kernel may reach another device: no remote copies, remote signals or barrier semaphores. Data moves between devices by JAX's collectives and lax.ppermute only.
A program may use at most 64 MiB of HBM per device.

v0:
```python
import jax
import jax.numpy as jnp
from jax import lax
from jax.sharding import PartitionSpec as P


def expand(group, group_map, first_block, block_count):
    width = group.shape[1]
    child_count = group_map.shape[1]
    targets = first_block + jnp.arange(block_count, dtype=jnp.int32)
    select = (group_map[:, :, None] == targets[None, None, :]).astype(jnp.float32)
    blocks = group.reshape(2, width, child_count, width)
    picked = jnp.einsum(
        "pacb,pct->patb",
        blocks,
        select,
        precision=lax.Precision.HIGHEST,
        preferred_element_type=jnp.float32,
    )
    return picked.reshape(2, width, block_count * width)


def per_device(diag_blocks, panel_rows, child_map, front):
    width = panel_rows.shape[1]
    whole_diag = lax.all_gather(diag_blocks, "prow", axis=1, tiled=True)
    factored = jnp.stack(
        [
            lax.linalg.triangular_solve(
                jnp.linalg.cholesky(whole_diag[panel]),
                panel_rows[panel],
                left_side=True,
                lower=True,
            )
            for panel in range(2)
        ]
    )
    row_index = lax.axis_index("prow")
    col_index = lax.axis_index("pcol")
    col_count = lax.axis_size("pcol")
    row_blocks = front.shape[0] // width
    col_blocks = front.shape[1] // width
    first_col = col_index * col_blocks
    span = col_count * width
    own_map = lax.dynamic_slice_in_dim(child_map, row_index * col_count, col_count, 1)
    every_row = lax.all_gather(factored, ("prow", "pcol"), axis=2, tiled=True)
    own_group = lax.dynamic_slice_in_dim(every_row, row_index * span, span, 2)
    left = expand(own_group, own_map, row_index * row_blocks, row_blocks)
    right = expand(every_row, child_map, first_col, col_blocks)
    update = lax.dot_general(
        left.reshape(2 * width, -1),
        right.reshape(2 * width, -1),
        (((0,), (0,)), ((), ())),
        precision=lax.Precision.HIGHEST,
        preferred_element_type=jnp.float32,
    )
    block_row = row_index * row_blocks + jnp.arange(front.shape[0], dtype=jnp.int32) // width
    block_col = first_col + jnp.arange(front.shape[1], dtype=jnp.int32) // width
    lower = block_row[:, None] >= block_col[None, :]
    return front - jnp.where(lower, update, 0.0)


def solution(mesh):
    return jax.shard_map(
        per_device,
        mesh=mesh,
        in_specs=(P(None, "prow", None), P(None, None, ("prow", "pcol")), P(), P("prow", "pcol")),
        out_specs=P("prow", "pcol"),
        check_vma=False,
    )
```

profile of v0, /device:TPU:1, one launch (start us, length us, event | category | flops | bytes accessed | tf_op | source)
XLA Modules:
  0.0 169.4 jit_solution(14358593414488060114)
XLA Ops:
  6.5 0.0 all-gather.2.cloned.1.call-start
  6.5 0.7 copy.13
  7.3 10.4 %all_gather.6 = f32[2,64,64]{2,0,1:T(2,128)S(1)} all-gather(f32[2,16,64]{2,0,1:T(2,128)S(1)} %copy.13), channel_id=1, replica_groups=mesh['prow'=4,'pcol'=32] {'prow'}, dimensions={1}, use_global_device_ids=true | all-gather | bytes 40960 | tf_op jit(solution)/shard_map/all_gather | solution.py:25
  17.6 0.1 fusion.26
  17.7 0.1 copy.29
  17.8 5.8 %cholesky.44 = f32[64,64]{1,0:T(8,128)S(1)} custom-call(f32[64,64]{1,0:T(8,128)S(1)} %fusion.3), custom_call_target="Cholesky" | custom-call | tf_op jit(solution)/shard_map/jit(cholesky)/cholesky | solution.py:29
  23.7 0.6 compare_reduce_fusion.1
  24.3 0.7 fusion
  25.0 4.9 %custom-call.6 = f32[1,64,64]{1,2,0:T(8,128)S(1)} custom-call(f32[1,64,64]{2,1,0:T(8,128)S(1)} %fusion), custom_call_target="InvertDiagBlocksLowerTriangular" | custom-call | tf_op jit(solution)/shard_map/triangular_solve/custom-call.0 | solution.py:28
  29.9 0.1 copy.30
  30.0 5.8 %cholesky.55 = f32[64,64]{1,0:T(8,128)S(1)} custom-call(f32[64,64]{1,0:T(8,128)S(1)} %fusion.2), custom_call_target="Cholesky" | custom-call | tf_op jit(solution)/shard_map/jit(cholesky)/cholesky | solution.py:29
  35.9 0.6 compare_reduce_fusion
  36.5 0.7 fusion.1
  37.2 4.9 %custom-call.7 = f32[1,64,64]{1,2,0:T(8,128)S(1)} custom-call(f32[1,64,64]{2,1,0:T(8,128)S(1)} %fusion.1), custom_call_target="InvertDiagBlocksLowerTriangular" | custom-call | tf_op jit(solution)/shard_map/triangular_solve/custom-call.0 | solution.py:28
  42.1 1.0 convolution_bitcast_fusion.3
  43.1 1.0 convolution_bitcast_fusion.2
  44.1 0.7 copy.18
  44.8 0.0 all-gather.2.cloned.1.call-update
  44.9 0.8 constant_dynamic-slice_fusion.1
  45.6 73.9 %all-gather.2.cloned.1.call-done = f32[2,64,8192]{1,0,2:T(2,128)} async-done(((f32[2,64,64]{1,0,2:T(2,128)}), f32[2,64,8192]{1,0,2:T(2,128)}) %all-gather.2.cloned.1.call-update) | async-done | bytes 4194320 | tf_op jit(solution)/shard_map/all_gather | solution.py:45
  119.5 2.6 %constant_dynamic-slice_fusion = f32[2,64,2048]{1,0,2:T(2,128)} fusion(f32[2,64,8192]{1,0,2:T(2,128)} %all-gather.2.cloned.1.call-done, s32[]{:T(128)S(6)} %select_n.34), kind=kLoop, calls=%fused_computation.52 | loop fusion | bytes 2097156 | tf_op jit(solution)/shard_map/dynamic_slice | solution.py:46
  122.2 2.9 %copy.25 = f32[2,64,32,64]{3,2,1,0:T(8,128)S(1)} copy(f32[2,64,32,64]{1,0,3,2:T(2,128)} %bitcast.63) | data formatting | bytes 2097152 | tf_op jit(solution)/shard_map/reshape | solution.py:12
  125.1 3.9 %convolution_bitcast_fusion = f32[2,64,64,64]{3,2,1,0:T(8,128)} fusion(f32[2,64,32,64]{3,2,1,0:T(8,128)S(1)} %copy.25, s32[64]{0:T(128)S(1)} %iota_add_fusion.1, s32[2,32]{1,0:T(2,128)S(1)} %constant_dynamic-slice_fusion.1), kind=kOutput, calls=%fused_computation.1 | convolution fusion | flops 201330688 | bytes 3146240 | tf_op jit(solution)/shard_map/pacb,pct->patb/dot_general | solution.py:13
  129.0 3.5 %reshape_reshape.6 = f32[128,4096]{1,0:T(8,128)S(1)} reshape(f32[2,64,64,64]{3,2,1,0:T(8,128)} %convolution_bitcast_fusion) | data formatting | bytes 4194304 | tf_op jit(solution)/shard_map/reshape;reshape | solution.py:50
  132.5 0.0 copy-start
  132.5 13.1 %copy.24 = f32[2,64,128,64]{3,2,1,0:T(8,128)} copy(f32[2,64,128,64]{1,0,3,2:T(2,128)} %bitcast.62) | data formatting | bytes 8388608 | tf_op jit(solution)/shard_map/reshape | solution.py:12
  145.6 0.0 copy-done
  145.6 5.1 %convolution_bitcast_fusion.1 = f32[2,64,8,64]{3,2,1,0:T(8,128)S(1)} fusion(f32[2,64,128,64]{3,2,1,0:T(8,128)} %copy.24, s32[2,128]{1,0:T(2,128)S(1)} %copy-done, s32[8]{0:T(128)S(1)} %iota_add_fusion), kind=kOutput, calls=%fused_computation.2 | convolution fusion | flops 100665344 | bytes 4457504 | tf_op jit(solution)/shard_map/pacb,pct->patb/dot_general | solution.py:13
  150.8 0.1 reshape_reshape.7
  150.9 11.6 %select_subtract_fusion = f32[4096,512]{1,0:T(8,128)} fusion(f32[4096,512]{1,0:T(8,128)} %param.10, f32[128,4096]{1,0:T(8,128)S(1)} %reshape_reshape.6, f32[128,512]{1,0:T(8,128)S(1)} %reshape_reshape.7, s32[512]{0:T(512)S(1)} %fusion.22, s32[4096]{0:T(1024)S(1)} %fusion.12), kind=kOutput, calls=%fused_computation | convolution fusion | flops 3227516928 | bytes 19154944 | tf_op jit(solution)/shard_map/dot_general | solution.py:49
  (9 shorter events, 0.1 us)
Async XLA Ops:
  6.5 113.0 %all-gather.2.cloned.1.call-start = ((), (), s32[]{:S(2)}) async-start(), calls=%async_computation | async-start | bytes 8454144 | tf_op jit(solution)/shard_map/all_gather | solution.py:45
  132.5 13.1 %copy-start = (s32[2,128]{1,0:T(2,128)S(1)}, s32[2,128]{1,0:T(2,128)}, u32[]{:S(2)}) copy-start(s32[2,128]{1,0:T(2,128)} %param.9) | copy-start | bytes 3076
Sparse Core Ops, SparseCore 0:
  45.0 74.5 all-gather.1
where the time goes:
time: 170 us; the launch traced here: 169 us
  waiting for transfers between devices  73.9 us (43%)
  local copies, waits for them, and re-layouts  24.7 us (15%)
  other arithmetic  24.2 us (14%)
  matrix products  22.7 us (13%)
  between operations  13.5 us (8%)
  blocking collectives  10.4 us (6%)
    all_gather x1, waiting for transfers between devices, per_device(): every_row = lax.all_gather(factored, ('prow', 'pcol'), axis=2, tiled=True)  73.9 us
    reshape x2, local copies, waits for them, and re-layouts, expand(): blocks = group.reshape(2, width, child_count, width)  16 us
    another operation x6, other arithmetic, per_device(): jnp.linalg.cholesky(whole_diag[panel])  13 us
    dot_general x1, matrix products, per_device(): lax.dot_general(left.reshape(2 * width, -1), right.reshape(2 * width, -1)...  11.6 us
    another operation x4, other arithmetic, per_device(): lax.linalg.triangular_solve(jnp.linalg.cholesky(whole_diag[panel]), panel...  11.1 us
    all_gather x1, blocking collectives, per_device(): whole_diag = lax.all_gather(diag_blocks, 'prow', axis=1, tiled=True)  10.4 us
    dot_general x2, matrix products, expand(): jnp.einsum('pacb,pct->patb', blocks, select, precision=lax.Precision.HIGH...  9.05 us
    another operation x1, local copies, waits for them, and re-layouts, per_device(): left.reshape(2 * width, -1)  3.52 us
  transfers between devices with their start and end apart: 1, of which 1 were waited for; matrix products, arithmetic and copies ran while one was open for 0% of the time, Pallas kernels for 0%

commit v1 on v0

v1 whole, which is shorter than its diff:
```python
import functools

import jax
import jax.numpy as jnp
from jax import lax
from jax.experimental import pallas as pl
from jax.experimental.pallas import tpu as pltpu
from jax.sharding import PartitionSpec as P

HIGHEST = lax.Precision.HIGHEST
TILE_ROWS = 512


def front_kernel(width, row_blocks, col_blocks, table_ref, place_ref,
                 group_ref, right_ref, front_ref, out_ref, left_ref):
    step = pl.program_id(0)
    tile_rows, cols = front_ref.shape
    per_tile = tile_rows // width
    lane = lax.broadcasted_iota(jnp.int32, (width, 2 * width), 1)
    for local in range(per_tile):
        block = step * per_tile + local
        first = table_ref[0, block]
        second = table_ref[1, block]
        from_first = group_ref[jnp.maximum(first, 0)]
        from_second = group_ref[jnp.maximum(second, 0)]
        left_ref[local * width:(local + 1) * width, :] = jnp.where(
            lane < width,
            jnp.where(first >= 0, from_first, 0.0),
            jnp.where(second >= 0, from_second, 0.0),
        )
    update = jnp.dot(left_ref[...], right_ref[...], precision=HIGHEST,
                     preferred_element_type=jnp.float32)
    row0 = place_ref[0] * (row_blocks * width) + step * tile_rows
    col0 = place_ref[1] * (col_blocks * width)
    rows = row0 + lax.broadcasted_iota(jnp.int32, (tile_rows, cols), 0)
    cols_at = col0 + lax.broadcasted_iota(jnp.int32, (tile_rows, cols), 1)
    lower = rows >= jnp.bitwise_and(cols_at, -width)
    out_ref[...] = front_ref[...] - jnp.where(lower, update, 0.0)


def apply_update(table, place, group, right, front, width, row_blocks, col_blocks):
    rows, cols = front.shape
    tiles = rows // TILE_ROWS
    kernel = functools.partial(front_kernel, width, row_blocks, col_blocks)
    return pl.pallas_call(
        kernel,
        out_shape=jax.ShapeDtypeStruct(front.shape, front.dtype),
        grid_spec=pltpu.PrefetchScalarGridSpec(
            num_scalar_prefetch=2,
            grid=(tiles,),
            in_specs=[
                pl.BlockSpec(group.shape, lambda i, t, p: (0, 0, 0)),
                pl.BlockSpec(right.shape, lambda i, t, p: (0, 0)),
                pl.BlockSpec((TILE_ROWS, cols), lambda i, t, p: (i, 0)),
            ],
            out_specs=pl.BlockSpec((TILE_ROWS, cols), lambda i, t, p: (i, 0)),
            scratch_shapes=[pltpu.VMEM((TILE_ROWS, 2 * width), jnp.float32)],
        ),
        cost_estimate=pl.CostEstimate(
            flops=2 * rows * cols * 2 * width,
            bytes_accessed=2 * rows * cols * 4 + group.size * 4 + right.size * 4,
            transcendentals=0,
        ),
    )(table, place, group, right, front)


def first_match(mapping, targets):
    hit = mapping[:, :, None] == targets[None, None, :]
    index = jnp.argmax(hit, axis=1).astype(jnp.int32)
    return jnp.where(jnp.any(hit, axis=1), index, -1)


def per_device(diag_blocks, panel_rows, child_map, front):
    width = panel_rows.shape[1]
    row_index = lax.axis_index("prow")
    col_index = lax.axis_index("pcol")
    col_count = lax.axis_size("pcol")
    row_blocks = front.shape[0] // width
    col_blocks = front.shape[1] // width

    local = jnp.transpose(panel_rows, (2, 0, 1)).reshape(width, 2 * width)
    group = lax.all_gather(local, "pcol", axis=0)

    whole_diag = lax.all_gather(diag_blocks, "prow", axis=1, tiled=True)
    lower_factor = jnp.linalg.cholesky(whole_diag)
    eye = jnp.broadcast_to(jnp.eye(width, dtype=jnp.float32), whole_diag.shape)
    inverse_factor = lax.linalg.triangular_solve(
        lower_factor, eye, left_side=True, lower=True)
    inverse = jnp.einsum("pca,pcb->pab", inverse_factor, inverse_factor,
                         precision=HIGHEST)

    own_map = lax.dynamic_slice_in_dim(child_map, row_index * col_count, col_count, 1)
    table = first_match(own_map - row_index * row_blocks,
                        jnp.arange(row_blocks, dtype=jnp.int32))

    first_col = col_index * col_blocks
    source = first_col // row_blocks
    source_map = lax.dynamic_slice_in_dim(child_map, source * col_count, col_count, 1)
    picks = first_match(source_map, first_col + jnp.arange(col_blocks, dtype=jnp.int32))
    keep = (picks >= 0) & (row_index == source)
    select = (picks[:, :, None] == jnp.arange(col_count, dtype=jnp.int32)) & keep[:, :, None]
    window = jnp.einsum("pjk,kbpa->pjba", select.astype(jnp.float32),
                        group.reshape(col_count, width, 2, width), precision=HIGHEST)
    window = lax.psum(window, "prow")
    right = jnp.einsum("pxa,pjba->pxjb", inverse, window, precision=HIGHEST)
    right = right.reshape(2 * width, col_blocks * width)

    place = jnp.stack([row_index, col_index]).astype(jnp.int32)
    return apply_update(table, place, group, right, front, width, row_blocks, col_blocks)


def solution(mesh):
    return jax.shard_map(
        per_device,
        mesh=mesh,
        in_specs=(P(None, "prow", None), P(None, None, ("prow", "pcol")), P(), P("prow", "pcol")),
        out_specs=P("prow", "pcol"),
        check_vma=False,
    )
```

time: 170 us -> 127 us (0.75)
  the two profiles are of different devices: /device:TPU:1 before, /device:TPU:14 now
where the time goes in v1:
time: 127 us; the launch traced here: 126 us
  waiting for transfers between devices  49 us (39%)
  other arithmetic  25.6 us (20%)
  between operations  13.5 us (11%)
  Pallas kernels  13.3 us (10%)
  blocking collectives  12.1 us (10%)
  local copies, waits for them, and re-layouts  6.03 us (5%)
  matrix products  6.01 us (5%)
    psum x1, waiting for transfers between devices, per_device(): window = lax.psum(window, 'prow')  40.5 us
    pallas_call x1, Pallas kernels, apply_update(): pl.pallas_call(kernel, out_shape=jax.ShapeDtypeStruct(front.shape, front....  13.3 us
    all_gather x1, blocking collectives, per_device(): whole_diag = lax.all_gather(diag_blocks, 'prow', axis=1, tiled=True)  12.1 us
    another operation x4, other arithmetic, per_device(): lower_factor = jnp.linalg.cholesky(whole_diag)  11.9 us
    another operation x3, other arithmetic, per_device(): lax.linalg.triangular_solve(lower_factor, eye, left_side=True, lower=True)  9.92 us
    all_gather x1, waiting for transfers between devices, per_device(): group = lax.all_gather(local, 'pcol', axis=0)  8.43 us
    dot_general x1, matrix products, per_device(): jnp.einsum('pjk,kbpa->pjba', select.astype(jnp.float32), group.reshape(co...  2.75 us
    dot_general x1, matrix products, per_device(): right = jnp.einsum('pxa,pjba->pxjb', inverse, window, precision=HIGHEST)  2.67 us
  transfers between devices with their start and end apart: 2, of which 2 were waited for; matrix products, arithmetic and copies ran while one was open for 22% of the time, Pallas kernels for 0%

profile of v1, /device:TPU:14, one launch (start us, length us, event | category | flops | bytes accessed | tf_op | source)
XLA Modules:
  0.0 125.5 jit_solution(2385072503376402186)
XLA Ops:
  6.5 0.0 all-gather.2.cloned.1.call-start
  6.5 1.5 %copy.35 = f32[1,64,128]{2,1,0:T(8,128)} copy(f32[1,64,128]{1,2,0:T(8,128)} %bitcast.28) | data formatting | bytes 65536 | tf_op jit(solution)/shard_map/all_gather;reshape | solution.py:82
  8.1 0.0 all-gather.2.cloned.1.call-update
  8.1 0.0 all-reduce.2.cloned.1.call-start
  8.2 0.7 copy.23
  8.9 12.1 %all_gather.7 = f32[2,64,64]{2,0,1:T(2,128)S(1)} all-gather(f32[2,16,64]{2,0,1:T(2,128)S(1)} %copy.23), channel_id=1, replica_groups=mesh['prow'=4,'pcol'=32] {'prow'}, dimensions={1}, use_global_device_ids=true | all-gather | bytes 40960 | tf_op jit(solution)/shard_map/all_gather | solution.py:84
  21.0 0.1 copy.24
  21.1 11.7 %custom-call.7 = f32[2,64,64]{2,1,0:T(8,128)S(1)} custom-call(f32[2,64,64]{2,1,0:T(8,128)S(1)} %fusion.6), custom_call_target="Cholesky" | custom-call | tf_op jit(solution)/shard_map/jit(cholesky)/cholesky | solution.py:85
  32.9 0.1 compare_reduce_fusion.2
  33.0 0.1 select_bitcast_fusion
  33.1 9.8 %custom-call.8 = f32[2,1,64,64]{2,3,1,0:T(8,128)S(1)} custom-call(f32[2,1,64,64]{3,2,1,0:T(8,128)S(1)} %select_bitcast_fusion), custom_call_target="InvertDiagBlocksLowerTriangular" | custom-call | tf_op jit(solution)/shard_map/triangular_solve | solution.py:87
  42.9 0.8 constant_dynamic-slice_fusion
  43.8 0.1 fusion.8
  43.9 0.2 compare_reduce_fusion.1
  44.1 0.3 fusion.4
  44.4 0.3 convolution_bitcast_fusion
  44.7 0.8 compare_reduce_fusion
  45.5 0.7 iota_reduce_fusion
  46.1 8.4 %all-gather.2.cloned.1.call-done.group_ref = f32[32,64,128]{2,1,0:T(8,128)} async-done(((f32[1,64,128]{2,1,0:T(8,128)}), f32[32,64,128]{2,1,0:T(8,128)}) %all-gather.2.cloned.1.call-update) | async-done | bytes 1048592 | tf_op jit(solution)/shard_map/all_gather | solution.py:82
  54.6 2.5 %reshape.24 = f32[32,64,2,64]{3,2,1,0:T(2,128)S(1)} reshape(f32[32,64,128]{2,1,0:T(8,128)} %all-gather.2.cloned.1.call-done.group_ref) | data formatting | bytes 2097152 | tf_op jit(solution)/shard_map/reshape | solution.py:103
  57.1 2.8 %fusion = f32[2,8,64,64]{3,1,2,0:T(8,128)} fusion(f32[32,64,2,64]{3,2,1,0:T(2,128)S(1)} %reshape.24, s32[2,8]{1,0:T(2,128)S(1)} %get-tuple-element.10, pred[2,8]{1,0:T(4,128)(4,1)S(1)} %get-tuple-element.9), kind=kOutput, calls=%fused_computation | convolution fusion | flops 25166848 | bytes 1310800 | tf_op jit(solution)/shard_map/pjk,kbpa->pjba/dot_general | solution.py:102
  59.8 0.0 all-reduce.2.cloned.1.call-update
  59.8 0.6 pad_add_fusion.place_ref
  60.4 0.6 broadcast_select_fusion.1.table_ref
  61.0 40.5 %all-reduce.2.cloned.1.call-done = f32[2,8,64,64]{3,1,2,0:T(8,128)} async-done(((f32[2,8,64,64]{3,1,2,0:T(8,128)}), f32[2,8,64,64]{3,1,2,0:T(8,128)}) %all-reduce.2.cloned.1.call-update) | async-done | bytes 262160 | tf_op jit(solution)/shard_map/psum | solution.py:104
  101.6 2.7 %fusion.2 = f32[2,64,8,64]{3,1,2,0:T(8,128)S(1)} fusion(f32[2,64,64,1]{2,1,3,0:T(8,128)S(1)} %convolution_bitcast_fusion, f32[2,8,64,64]{3,1,2,0:T(8,128)} %all-reduce.2.cloned.1.call-done), kind=kOutput, calls=%fused_computation.3 | convolution fusion | flops 50331648 | bytes 557056 | tf_op jit(solution)/shard_map/pxa,pjba->pxjb/dot_general | solution.py:105
  104.2 0.3 copy.30
  104.5 0.9 reshape.25.right_ref
  105.4 13.3 %shard_map.46 = f32[4096,512]{1,0:T(8,128)} custom-call(s32[2,64]{1,0:T(2,128)} %broadcast_select_fusion.1.table_ref, s32[2]{0:T(128)} %pad_add_fusion.place_ref, f32[32,64,128]{2,1,0:T(8,128)} %all-gather.2.cloned.1.call-done.group_ref, f32[128,512]{1,0:T(8,128)} %reshape.25.right_ref, f32[4096,512]{1,0:T(8,128)} %front_ref.1), custom_call_target="tpu_custom_call" | custom-call | flops 536870912 | bytes 18087936 | tf_op jit(solution)/shard_map/pallas_call | solution.py:45
  (7 shorter events, 0.1 us)
Async XLA Ops:
  6.5 48.0 %all-gather.2.cloned.1.call-start = ((), (), s32[]{:S(2)}) async-start(), calls=%async_computation | async-start | bytes 1081344 | tf_op jit(solution)/shard_map/all_gather | solution.py:82
  8.1 93.5 %all-reduce.2.cloned.1.call-start = ((), (), s32[]{:S(2)}) async-start(), calls=%async_computation.1 | async-start | bytes 1048576 | tf_op jit(solution)/shard_map/psum | solution.py:104
Sparse Core Ops, SparseCore 0:
  9.6 44.9 all-gather.1
  60.0 41.5 all-reduce.1

commit v2 on v1

--- a/solution.py
+++ b/solution.py
@@ -1,6 +1,7 @@
 import functools
 
 import jax
+import numpy as np
 import jax.numpy as jnp
 from jax import lax
 from jax.experimental import pallas as pl
@@ -11,8 +12,14 @@
 TILE_ROWS = 512
 
 
+def split_bf16(value):
+    scaled = value * 65537.0
+    high = scaled - (scaled - value)
+    return high.astype(jnp.bfloat16), (value - high).astype(jnp.bfloat16)
+
+
 def front_kernel(width, row_blocks, col_blocks, table_ref, place_ref,
-                 group_ref, right_ref, front_ref, out_ref, left_ref):
+                 group_ref, high_ref, low_ref, front_ref, out_ref, left_ref):
     step = pl.program_id(0)
     tile_rows, cols = front_ref.shape
     per_tile = tile_rows // width
@@ -28,8 +35,11 @@
             jnp.where(first >= 0, from_first, 0.0),
             jnp.where(second >= 0, from_second, 0.0),
         )
-    update = jnp.dot(left_ref[...], right_ref[...], precision=HIGHEST,
-                     preferred_element_type=jnp.float32)
+    left_high, left_low = split_bf16(left_ref[...])
+    right_high = high_ref[...]
+    update = jnp.dot(left_high, right_high, preferred_element_type=jnp.float32)
+    update += jnp.dot(left_high, low_ref[...], preferred_element_type=jnp.float32)
+    update += jnp.dot(left_low, right_high, preferred_element_type=jnp.float32)
     row0 = place_ref[0] * (row_blocks * width) + step * tile_rows
     col0 = place_ref[1] * (col_blocks * width)
     rows = row0 + lax.broadcasted_iota(jnp.int32, (tile_rows, cols), 0)
@@ -40,6 +50,7 @@
 
 def apply_update(table, place, group, right, front, width, row_blocks, col_blocks):
     rows, cols = front.shape
+    high, low = split_bf16(right)
     tiles = rows // TILE_ROWS
     kernel = functools.partial(front_kernel, width, row_blocks, col_blocks)
     return pl.pallas_call(
@@ -51,17 +62,29 @@
             in_specs=[
                 pl.BlockSpec(group.shape, lambda i, t, p: (0, 0, 0)),
                 pl.BlockSpec(right.shape, lambda i, t, p: (0, 0)),
+                pl.BlockSpec(right.shape, lambda i, t, p: (0, 0)),
                 pl.BlockSpec((TILE_ROWS, cols), lambda i, t, p: (i, 0)),
             ],
             out_specs=pl.BlockSpec((TILE_ROWS, cols), lambda i, t, p: (i, 0)),
             scratch_shapes=[pltpu.VMEM((TILE_ROWS, 2 * width), jnp.float32)],
         ),
         cost_estimate=pl.CostEstimate(
-            flops=2 * rows * cols * 2 * width,
+            flops=3 * 2 * rows * cols * 2 * width,
             bytes_accessed=2 * rows * cols * 4 + group.size * 4 + right.size * 4,
             transcendentals=0,
         ),
-    )(table, place, group, right, front)
+    )(table, place, group, high, low, front)
+
+
+def doubling_gather(block, axis, count):
+    bits = count.bit_length() - 1
+    spread = [0]
+    for bit in reversed(range(bits)):
+        mask = 1 << bit
+        other = lax.ppermute(block, axis, [(i, i ^ mask) for i in range(count)])
+        block = jnp.concatenate([block, other], axis=0)
+        spread = spread + [s ^ mask for s in spread]
+    return block, spread
 
 
 def first_match(mapping, targets):
@@ -78,10 +101,23 @@
     row_blocks = front.shape[0] // width
     col_blocks = front.shape[1] // width
 
+    row_count = lax.axis_size("prow")
+
     local = jnp.transpose(panel_rows, (2, 0, 1)).reshape(width, 2 * width)
-    group = lax.all_gather(local, "pcol", axis=0)
+    group, spread = doubling_gather(local[None], "pcol", col_count)
+    child_at = jnp.bitwise_xor(col_index, jnp.asarray(spread, jnp.int32))
+    slot_of = jnp.bitwise_xor(col_index, jnp.arange(col_count, dtype=jnp.int32))
+    slot_of = jnp.take(jnp.asarray(np.argsort(spread), jnp.int32), slot_of)
 
-    whole_diag = lax.all_gather(diag_blocks, "prow", axis=1, tiled=True)
+    pieces = [diag_blocks] + [
+        lax.ppermute(diag_blocks, "prow", [(i, (i + k) % row_count) for i in range(row_count)])
+        for k in range(1, row_count)
+    ]
+    order = (row_index - jnp.arange(row_count, dtype=jnp.int32)) % row_count
+    whole_diag = sum(
+        jnp.where((order == k)[None, :, None, None], piece[:, None], 0.0)
+        for k, piece in enumerate(pieces)
+    ).reshape(diag_blocks.shape[0], -1, diag_blocks.shape[2])
     lower_factor = jnp.linalg.cholesky(whole_diag)
     eye = jnp.broadcast_to(jnp.eye(width, dtype=jnp.float32), whole_diag.shape)
     inverse_factor = lax.linalg.triangular_solve(
@@ -92,16 +128,24 @@
     own_map = lax.dynamic_slice_in_dim(child_map, row_index * col_count, col_count, 1)
     table = first_match(own_map - row_index * row_blocks,
                         jnp.arange(row_blocks, dtype=jnp.int32))
+    table = jnp.where(table >= 0, jnp.take(slot_of, jnp.maximum(table, 0)), -1)
 
     first_col = col_index * col_blocks
     source = first_col // row_blocks
     source_map = lax.dynamic_slice_in_dim(child_map, source * col_count, col_count, 1)
     picks = first_match(source_map, first_col + jnp.arange(col_blocks, dtype=jnp.int32))
     keep = (picks >= 0) & (row_index == source)
-    select = (picks[:, :, None] == jnp.arange(col_count, dtype=jnp.int32)) & keep[:, :, None]
+    select = (picks[:, :, None] == child_at) & keep[:, :, None]
     window = jnp.einsum("pjk,kbpa->pjba", select.astype(jnp.float32),
                         group.reshape(col_count, width, 2, width), precision=HIGHEST)
-    window = lax.psum(window, "prow")
+    owner = [(c * col_blocks) // row_blocks for c in range(col_count)]
+    window = window + sum(
+        lax.ppermute(window, ("prow", "pcol"), [
+            (owner[c] * col_count + c, (owner[c] + k) * col_count + c)
+            for c in range(col_count) if owner[c] + k < row_count
+        ])
+        for k in range(1, row_count)
+    )
     right = jnp.einsum("pxa,pjba->pxjb", inverse, window, precision=HIGHEST)
     right = right.reshape(2 * width, col_blocks * width)
 

time: 127 us -> 109 us (0.86)
  starting transfers between devices: 0.04 us -> 14.7 us
  between operations: 13.5 us -> 0.39 us
  blocking collectives: 12.1 us -> 0 us
  waiting for transfers between devices: 49 us -> 38.2 us
  local copies, waits for them, and re-layouts: 6.03 us -> 12.2 us
  matrix products: 6.01 us -> 3.02 us
  other arithmetic: 25.6 us -> 28.5 us
  Pallas kernels: 13.3 us -> 11.7 us
    psum x1 -> x0, waiting for transfers between devices: 40.5 us -> none  [per_device(): window = lax.psum(window, 'prow')]
    ppermute x0 -> x11, waiting for transfers between devices: none -> 38.2 us  [the longest x3 25.6 us: per_device(): lax.ppermute(window, ('prow', 'pcol'), [(owner[c] * col_count + c, (owner...]
    ppermute x0 -> x11, starting transfers between devices: none -> 14.7 us  [the longest x5 7.48 us: doubling_gather(): other = lax.ppermute(block, axis, [(i, i ^ mask) for i in range(count)])]
    all_gather x1 -> x0, blocking collectives: 12.1 us -> none  [per_device(): whole_diag = lax.all_gather(diag_blocks, 'prow', axis=1, tiled=True)]
    all_gather x1 -> x0, waiting for transfers between devices: 8.43 us -> none  [per_device(): group = lax.all_gather(local, 'pcol', axis=0)]
    concatenate x0 -> x13, local copies, waits for them, and re-layouts: none -> 6.63 us  [doubling_gather(): block = jnp.concatenate([block, other], axis=0)]
    gather x0 -> x3, local copies, waits for them, and re-layouts: none -> 2.67 us  [the longest x1 1.36 us: per_device(): slot_of = jnp.take(jnp.asarray(np.argsort(spread), jnp.int32), slot_of)]
    reshape x1 -> x0, local copies, waits for them, and re-layouts: 2.49 us -> none  [per_device(): group.reshape(col_count, width, 2, width)]
  transfers between devices with their start and end apart: 2 -> 11, of which waited for: 2 -> 4; matrix products, arithmetic and copies ran while one was open for 22% -> 33% of each run, Pallas kernels for 0% -> 0%
where the time goes in v2:
time: 109 us
  waiting for transfers between devices  38.2 us (35%)
  other arithmetic  28.5 us (26%)
  starting transfers between devices  14.7 us (13%)
  local copies, waits for them, and re-layouts  12.2 us (11%)
  Pallas kernels  11.7 us (11%)
  matrix products  3.02 us (3%)
    ppermute x3, waiting for transfers between devices, per_device(): lax.ppermute(window, ('prow', 'pcol'), [(owner[c] * col_count + c, (owner...  25.6 us
    ppermute x5, waiting for transfers between devices, doubling_gather(): other = lax.ppermute(block, axis, [(i, i ^ mask) for i in range(count)])  12.6 us
    another operation x4, other arithmetic, per_device(): lower_factor = jnp.linalg.cholesky(whole_diag)  11.9 us
    pallas_call x1, Pallas kernels, apply_update(): pl.pallas_call(kernel, out_shape=jax.ShapeDtypeStruct(front.shape, front....  11.7 us
    another operation x3, other arithmetic, per_device(): lax.linalg.triangular_solve(lower_factor, eye, left_side=True, lower=True)  10.6 us
    ppermute x5, starting transfers between devices, doubling_gather(): other = lax.ppermute(block, axis, [(i, i ^ mask) for i in range(count)])  7.48 us
    concatenate x13, local copies, waits for them, and re-layouts, doubling_gather(): block = jnp.concatenate([block, other], axis=0)  6.63 us
    ppermute x3, starting transfers between devices, per_device(): lax.ppermute(diag_blocks, 'prow', [(i, (i + k) % row_count) for i in rang...  4.32 us
  transfers between devices with their start and end apart: 11, of which 4 were waited for; matrix products, arithmetic and copies ran while one was open for 33% of the time, Pallas kernels for 0%

profile of v2, /device:TPU:14, one launch (start us, length us, event | category | flops | bytes accessed | tf_op | source)
XLA Modules:
  0.0 108.8 jit_solution(766120791408340794)
XLA Ops:
  0.0 1.6 %collective-permute-start.5 = (f32[2,16,64]{2,1,0:T(8,128)}, f32[2,16,64]{2,1,0:T(8,128)S(1)}, u32[]{:S(2)}, u32[]{:S(2)}) collective-permute-start(f32[2,16,64]{2,1,0:T(8,128)} %param.6), channel_id=1, source_target_pairs={{0,32},{32,64},{64,96},{96,0},{1,33},{33,65},{65,97},{97,1},{2,34}... | collective-permute-start | bytes 24584 | tf_op jit(solution)/shard_map/ppermute | solution.py:113
  2.0 2.3 %collective-permute-start.6 = (f32[2,16,64]{2,1,0:T(8,128)}, f32[2,16,64]{2,1,0:T(8,128)S(1)}, u32[]{:S(2)}, u32[]{:S(2)}) collective-permute-start(f32[2,16,64]{2,1,0:T(8,128)} %param.6), channel_id=1, source_target_pairs={{0,64},{32,96},{64,0},{96,32},{1,65},{33,97},{65,1},{97,33},{2,66}... | collective-permute-start | bytes 24584 | tf_op jit(solution)/shard_map/ppermute | solution.py:113
  4.3 0.9 copy.44
  5.2 4.0 %collective-permute-start = (f32[1,64,128]{2,1,0:T(8,128)S(1)}, f32[1,64,128]{2,1,0:T(8,128)S(1)}, u32[]{:S(2)}, u32[]{:S(2)}) collective-permute-start(f32[1,64,128]{2,1,0:T(8,128)S(1)} %copy.44), channel_id=1, source_target_pairs={{0,16},{1,17},{2,18},{3,19},{4,20},{5,21},{6,22},{7,23},{8,24},{9,... | collective-permute-start | bytes 98312 | tf_op jit(solution)/shard_map/ppermute | solution.py:84
  9.2 0.8 constant_dynamic-slice_fusion
  10.2 0.8 compare_reduce_fusion
  11.1 0.7 iota_reduce_fusion
  12.4 0.7 broadcast_xor_fusion
  13.2 1.4 %gather_fusion = s32[32]{0:T(128)S(1)} fusion(s32[32]{0:T(128)} %constant.140.clone, s32[1024]{0:T(1024)S(1)} %pad_clamp_fusion.1), kind=kCustom, calls=%fused_computation | custom fusion | bytes 384 | tf_op jit(solution)/shard_map/jit(_take)/gather | solution.py:110
  14.5 1.2 %gather_fusion.1 = s32[128]{0:T(128)S(1)} fusion(s32[32]{0:T(128)S(1)} %and_select_fusion.1, s32[1024]{0:T(1024)S(1)} %pad_clamp_fusion), kind=kCustom, calls=%fused_computation.1 | custom fusion | bytes 1536 | tf_op jit(solution)/shard_map/jit(_take)/gather | solution.py:131
  16.4 1.1 %collective-permute-start.1 = (f32[2,64,128]{2,1,0:T(8,128)S(1)}, f32[2,64,128]{2,1,0:T(8,128)S(1)}, u32[]{:S(2)}, u32[]{:S(2)}) collective-permute-start(f32[2,64,128]{2,1,0:T(8,128)S(1)} %pad_maximum_fusion.2), channel_id=1, source_target_pairs={{0,8},{1,9},{2,10},{3,11},{4,12},{5,13},{6,14},{7,15},{8,0},{9,1},... | collective-permute-start | bytes 196616 | tf_op jit(solution)/shard_map/ppermute | solution.py:84
  17.6 3.2 %collective-permute-done.1 = f32[2,64,128]{2,1,0:T(8,128)S(1)} collective-permute-done((f32[2,64,128]{2,1,0:T(8,128)S(1)}, f32[2,64,128]{2,1,0:T(8,128)S(1)}, u32[]{:S(2)}, u32[]{:S(2)}) %collective-permute-start.1) | collective-permute-done | bytes 65568 | tf_op jit(solution)/shard_map/ppermute | solution.py:84
  20.8 1.5 %collective-permute-start.2 = (f32[4,64,128]{2,1,0:T(8,128)S(1)}, f32[4,64,128]{2,1,0:T(8,128)S(1)}, u32[]{:S(2)}, u32[]{:S(2)}) collective-permute-start(f32[4,64,128]{2,1,0:T(8,128)S(1)} %pad_maximum_fusion.1), channel_id=1, source_target_pairs={{0,4},{1,5},{2,6},{3,7},{4,0},{5,1},{6,2},{7,3},{8,12},{9,13},{10,... | collective-permute-start | bytes 393224 | tf_op jit(solution)/shard_map/ppermute | solution.py:84
  22.9 0.7 copy.27
  24.5 3.8 %collective-permute-done.2 = f32[4,64,128]{2,1,0:T(8,128)S(1)} collective-permute-done((f32[4,64,128]{2,1,0:T(8,128)S(1)}, f32[4,64,128]{2,1,0:T(8,128)S(1)}, u32[]{:S(2)}, u32[]{:S(2)}) %collective-permute-start.2) | collective-permute-done | bytes 131104 | tf_op jit(solution)/shard_map/ppermute | solution.py:84
  28.4 0.9 collective-permute-start.3
  29.3 5.6 %collective-permute-done.3 = f32[8,64,128]{2,1,0:T(8,128)S(1)} collective-permute-done((f32[8,64,128]{2,1,0:T(8,128)S(1)}, f32[8,64,128]{2,1,0:T(8,128)S(1)}, u32[]{:S(2)}, u32[]{:S(2)}) %collective-permute-start.3) | collective-permute-done | bytes 262176 | tf_op jit(solution)/shard_map/ppermute | solution.py:84
  35.0 11.7 %custom-call.7 = f32[2,64,64]{2,1,0:T(8,128)S(1)} custom-call(f32[2,64,64]{2,1,0:T(8,128)S(1)} %fusion.7), custom_call_target="Cholesky" | custom-call | tf_op jit(solution)/shard_map/jit(cholesky)/cholesky | solution.py:121
  46.9 10.5 %custom-call.8 = f32[2,1,64,64]{2,3,1,0:T(8,128)} custom-call(f32[2,1,64,64]{3,2,1,0:T(8,128)S(1)} %select_bitcast_fusion), custom_call_target="InvertDiagBlocksLowerTriangular" | custom-call | tf_op jit(solution)/shard_map/triangular_solve | solution.py:123
  57.5 0.7 copy.32
  59.2 1.1 %copy.35 = f32[8,64,2,64]{3,0,1,2:T(8,128)} copy(f32[8,64,2,64]{3,2,1,0:T(2,128)S(1)} %concatenate.43) | data formatting | bytes 524288 | tf_op jit(solution)/shard_map/concatenate | solution.py:85
  60.3 0.6 concatenate.44
  60.9 0.6 copy.36
  61.5 2.5 %concatenate.45 = f32[32,64,2,64]{3,0,1,2:T(8,128)S(1)} concatenate(f32[1,64,2,64]{3,0,1,2:T(1,128)} %bitcast.54, f32[1,64,2,64]{3,0,1,2:T(1,128)} %copy.32, f32[2,64,2,64]{3,0,1,2:T(2,128)S(1)} %copy.33, f32[4,64,2,64]{3,0,1,2:T(4,128)S(1)} %copy.34, f32[8,64,2,64]{3,0,1,2:T(8,128)} %copy.35, f32[16,64,2,64]{3,0,1,2:T(8,128)S(1)} %copy.36), dimensions={0} | concatenate | bytes 2097152 | tf_op jit(solution)/shard_map/concatenate | solution.py:85
  64.1 0.8 fusion.14
  64.9 0.7 collective-permute-start.10
  65.6 0.7 collective-permute-start.9
  66.3 1.5 %collective-permute-start.8 = (f32[2,8,64,64]{3,1,2,0:T(8,128)S(1)}, f32[2,8,64,64]{3,1,2,0:T(8,128)S(1)}, u32[]{:S(2)}, u32[]{:S(2)}) collective-permute-start(f32[2,8,64,64]{3,1,2,0:T(8,128)S(1)} %fusion.14), channel_id=1, source_target_pairs={{0,32},{1,33},{2,34},{3,35},{4,36},{5,37},{6,38},{7,39},{40,72},{4... | collective-permute-start | bytes 786440 | tf_op jit(solution)/shard_map/ppermute | solution.py:143
  68.5 25.6 %collective-permute-done.8 = f32[2,8,64,64]{3,1,2,0:T(8,128)S(1)} collective-permute-done((f32[2,8,64,64]{3,1,2,0:T(8,128)S(1)}, f32[2,8,64,64]{3,1,2,0:T(8,128)S(1)}, u32[]{:S(2)}, u32[]{:S(2)}) %collective-permute-start.8) | collective-permute-done | bytes 262176 | tf_op jit(solution)/shard_map/ppermute | solution.py:143
  94.2 1.6 %fusion = f32[2,64,8,64]{3,1,2,0:T(8,128)S(1)} fusion(f32[2,64,64,1]{2,1,3,0:T(8,128)S(1)} %convolution_bitcast_fusion, f32[2,8,64,64]{3,1,2,0:T(8,128)S(1)} %add_add_fusion), kind=kOutput, calls=%fused_computation.3 | convolution fusion | flops 50331648 | bytes 557056 | tf_op jit(solution)/shard_map/pxa,pjba->pxjb/dot_general | solution.py:149
  96.3 0.8 fusion.4
  97.0 11.7 %shard_map.64 = f32[4096,512]{1,0:T(8,128)} custom-call(s32[2,64]{1,0:T(2,128)} %compare_select_fusion.5.table_ref, s32[2]{0:T(128)} %pad_add_fusion.place_ref, f32[32,64,128]{2,1,0:T(8,128)} %copy-done.4, bf16[128,512]{1,0:T(8,128)(2,1)} %get-tuple-element.12.high_ref, bf16[128,512]{1,0:T(8,128)(2,1)} %get-tuple-element.11.low_ref, f32[4096,512]{1,0:T(8,128)} %front_ref.1), custom_call_target="tpu_custom_call" | custom-call | flops 1610612736 | bytes 18087936 | tf_op jit(solution)/shard_map/pallas_call | solution.py:56
  (79 shorter events, 6.2 us)
Async XLA Ops:
  0.0 24.3 %copy-start.8 = (f32[2,16,64]{2,1,0:T(8,128)S(1)}, f32[2,16,64]{2,1,0:T(8,128)}, u32[]{:S(2)}) copy-start(f32[2,16,64]{2,1,0:T(8,128)} %param.6) | copy-start | bytes 24580
  0.0 22.9 %copy-start.5 = (f32[2,64,64]{2,1,0:T(8,128)S(1)}, f32[2,64,64]{2,1,0:T(8,128)}, u32[]{:S(2)}) copy-start(f32[2,64,64]{2,1,0:T(8,128)} %param.7) | copy-start | bytes 98308
  0.0 24.3 %collective-permute-start.5 = (f32[2,16,64]{2,1,0:T(8,128)}, f32[2,16,64]{2,1,0:T(8,128)S(1)}, u32[]{:S(2)}, u32[]{:S(2)}) collective-permute-start(f32[2,16,64]{2,1,0:T(8,128)} %param.6), channel_id=1, source_target_pairs={{0,32},{32,64},{64,96},{96,0},{1,33},{33,65},{65,97},{97,1},{2,34}... | collective-permute-start | bytes 24584 | tf_op jit(solution)/shard_map/ppermute | solution.py:113
  1.6 22.7 %collective-permute-start.7 = (f32[2,16,64]{2,1,0:T(8,128)}, f32[2,16,64]{2,1,0:T(8,128)S(1)}, u32[]{:S(2)}, u32[]{:S(2)}) collective-permute-start(f32[2,16,64]{2,1,0:T(8,128)} %param.6), channel_id=1, source_target_pairs={{0,96},{32,0},{64,32},{96,64},{1,97},{33,1},{65,33},{97,65},{2,98}... | collective-permute-start | bytes 24584 | tf_op jit(solution)/shard_map/ppermute | solution.py:113
  2.0 22.2 %collective-permute-start.6 = (f32[2,16,64]{2,1,0:T(8,128)}, f32[2,16,64]{2,1,0:T(8,128)S(1)}, u32[]{:S(2)}, u32[]{:S(2)}) collective-permute-start(f32[2,16,64]{2,1,0:T(8,128)} %param.6), channel_id=1, source_target_pairs={{0,64},{32,96},{64,0},{96,32},{1,65},{33,97},{65,1},{97,33},{2,66}... | collective-permute-start | bytes 24584 | tf_op jit(solution)/shard_map/ppermute | solution.py:113
  5.2 11.2 %collective-permute-start = (f32[1,64,128]{2,1,0:T(8,128)S(1)}, f32[1,64,128]{2,1,0:T(8,128)S(1)}, u32[]{:S(2)}, u32[]{:S(2)}) collective-permute-start(f32[1,64,128]{2,1,0:T(8,128)S(1)} %copy.44), channel_id=1, source_target_pairs={{0,16},{1,17},{2,18},{3,19},{4,20},{5,21},{6,22},{7,23},{8,24},{9,... | collective-permute-start | bytes 98312 | tf_op jit(solution)/shard_map/ppermute | solution.py:84
  16.4 4.3 %collective-permute-start.1 = (f32[2,64,128]{2,1,0:T(8,128)S(1)}, f32[2,64,128]{2,1,0:T(8,128)S(1)}, u32[]{:S(2)}, u32[]{:S(2)}) collective-permute-start(f32[2,64,128]{2,1,0:T(8,128)S(1)} %pad_maximum_fusion.2), channel_id=1, source_target_pairs={{0,8},{1,9},{2,10},{3,11},{4,12},{5,13},{6,14},{7,15},{8,0},{9,1},... | collective-permute-start | bytes 196616 | tf_op jit(solution)/shard_map/ppermute | solution.py:84
  20.8 7.5 %collective-permute-start.2 = (f32[4,64,128]{2,1,0:T(8,128)S(1)}, f32[4,64,128]{2,1,0:T(8,128)S(1)}, u32[]{:S(2)}, u32[]{:S(2)}) collective-permute-start(f32[4,64,128]{2,1,0:T(8,128)S(1)} %pad_maximum_fusion.1), channel_id=1, source_target_pairs={{0,4},{1,5},{2,6},{3,7},{4,0},{5,1},{6,2},{7,3},{8,12},{9,13},{10,... | collective-permute-start | bytes 393224 | tf_op jit(solution)/shard_map/ppermute | solution.py:84
  28.4 6.5 %collective-permute-start.3 = (f32[8,64,128]{2,1,0:T(8,128)S(1)}, f32[8,64,128]{2,1,0:T(8,128)S(1)}, u32[]{:S(2)}, u32[]{:S(2)}) collective-permute-start(f32[8,64,128]{2,1,0:T(8,128)S(1)} %pad_maximum_fusion), channel_id=1, source_target_pairs={{0,2},{1,3},{2,0},{3,1},{4,6},{5,7},{6,4},{7,5},{8,10},{9,11},{10,... | collective-permute-start | bytes 786440 | tf_op jit(solution)/shard_map/ppermute | solution.py:84
  34.9 23.8 %copy-start.2 = (f32[32,64,128]{2,1,0:T(8,128)}, f32[32,64,128]{2,1,0:T(8,128)S(1)}, u32[]{:S(2)}) copy-start(f32[32,64,128]{2,1,0:T(8,128)S(1)} %get-tuple-element.14) | copy-start | bytes 3145732
  34.9 25.4 %collective-permute-start.4 = (f32[16,64,128]{2,1,0:T(8,128)S(1)}, f32[16,64,128]{2,1,0:T(8,128)S(1)}, u32[]{:S(2)}, u32[]{:S(2)}) collective-permute-start(f32[16,64,128]{2,1,0:T(8,128)S(1)} %get-tuple-element.13), channel_id=1, source_target_pairs={{0,1},{1,0},{2,3},{3,2},{4,5},{5,4},{6,7},{7,6},{8,9},{9,8},{10,11... | collective-permute-start | bytes 1572872 | tf_op jit(solution)/shard_map/ppermute | solution.py:84
  60.3 1.2 %copy-start = (f32[16,64,128]{2,1,0:T(8,128)}, f32[16,64,128]{2,1,0:T(8,128)S(1)}, u32[]{:S(2)}) copy-start(f32[16,64,128]{2,1,0:T(8,128)S(1)} %collective-permute-done.4) | copy-start | bytes 1572868
  64.1 3.7 %copy-start.6 = (f32[64,64]{1,0:T(8,128)S(1)}, f32[64,64]{1,0:T(8,128)}, u32[]{:S(2)}) copy-start(f32[64,64]{1,0:T(8,128)} %fusion.13) | copy-start | bytes 49156
  64.1 3.7 %copy-start.7 = (f32[2,1,64,64]{2,3,1,0:T(8,128)S(1)}, f32[2,1,64,64]{2,3,1,0:T(8,128)}, u32[]{:S(2)}) copy-start(f32[2,1,64,64]{2,3,1,0:T(8,128)} %custom-call.8) | copy-start | bytes 98308
  64.1 4.3 %copy-start.1 = (f32[16,64,128]{2,1,0:T(8,128)S(1)}, f32[16,64,128]{2,1,0:T(8,128)}, u32[]{:S(2)}) copy-start(f32[16,64,128]{2,1,0:T(8,128)} %copy-done) | copy-start | bytes 1572868
  64.1 4.3 %copy-start.3 = (f32[32,64,128]{2,1,0:T(8,128)S(1)}, f32[32,64,128]{2,1,0:T(8,128)}, u32[]{:S(2)}) copy-start(f32[32,64,128]{2,1,0:T(8,128)} %copy-done.2) | copy-start | bytes 3145732
  64.9 3.6 %collective-permute-start.10 = (f32[2,8,64,64]{3,1,2,0:T(8,128)S(1)}, f32[2,8,64,64]{3,1,2,0:T(8,128)S(1)}, u32[]{:S(2)}, u32[]{:S(2)}) collective-permute-start(f32[2,8,64,64]{3,1,2,0:T(8,128)S(1)} %fusion.14), channel_id=1, source_target_pairs={{0,96},{1,97},{2,98},{3,99},{4,100},{5,101},{6,102},{7,103}} | collective-permute-start | bytes 786440 | tf_op jit(solution)/shard_map/ppermute | solution.py:143
  65.6 2.9 %collective-permute-start.9 = (f32[2,8,64,64]{3,1,2,0:T(8,128)S(1)}, f32[2,8,64,64]{3,1,2,0:T(8,128)S(1)}, u32[]{:S(2)}, u32[]{:S(2)}) collective-permute-start(f32[2,8,64,64]{3,1,2,0:T(8,128)S(1)} %fusion.14), channel_id=1, source_target_pairs={{0,64},{1,65},{2,66},{3,67},{4,68},{5,69},{6,70},{7,71},{40,104},{... | collective-permute-start | bytes 786440 | tf_op jit(solution)/shard_map/ppermute | solution.py:143
  66.3 27.8 %collective-permute-start.8 = (f32[2,8,64,64]{3,1,2,0:T(8,128)S(1)}, f32[2,8,64,64]{3,1,2,0:T(8,128)S(1)}, u32[]{:S(2)}, u32[]{:S(2)}) collective-permute-start(f32[2,8,64,64]{3,1,2,0:T(8,128)S(1)} %fusion.14), channel_id=1, source_target_pairs={{0,32},{1,33},{2,34},{3,35},{4,36},{5,37},{6,38},{7,39},{40,72},{4... | collective-permute-start | bytes 786440 | tf_op jit(solution)/shard_map/ppermute | solution.py:143
  68.5 27.7 %copy-start.4 = (f32[32,64,128]{2,1,0:T(8,128)}, f32[32,64,128]{2,1,0:T(8,128)S(1)}, u32[]{:S(2)}) copy-start(f32[32,64,128]{2,1,0:T(8,128)S(1)} %constant_dynamic-update-slice_fusion.5.group_ref) | copy-start | bytes 3145732

commit v3 on v2

--- a/solution.py
+++ b/solution.py
@@ -118,12 +118,6 @@
         jnp.where((order == k)[None, :, None, None], piece[:, None], 0.0)
         for k, piece in enumerate(pieces)
     ).reshape(diag_blocks.shape[0], -1, diag_blocks.shape[2])
-    lower_factor = jnp.linalg.cholesky(whole_diag)
-    eye = jnp.broadcast_to(jnp.eye(width, dtype=jnp.float32), whole_diag.shape)
-    inverse_factor = lax.linalg.triangular_solve(
-        lower_factor, eye, left_side=True, lower=True)
-    inverse = jnp.einsum("pca,pcb->pab", inverse_factor, inverse_factor,
-                         precision=HIGHEST)
 
     own_map = lax.dynamic_slice_in_dim(child_map, row_index * col_count, col_count, 1)
     table = first_match(own_map - row_index * row_blocks,
@@ -138,6 +132,13 @@
     select = (picks[:, :, None] == child_at) & keep[:, :, None]
     window = jnp.einsum("pjk,kbpa->pjba", select.astype(jnp.float32),
                         group.reshape(col_count, width, 2, width), precision=HIGHEST)
+    window, whole_diag = lax.optimization_barrier((window, whole_diag))
+    lower_factor = jnp.linalg.cholesky(whole_diag)
+    eye = jnp.broadcast_to(jnp.eye(width, dtype=jnp.float32), whole_diag.shape)
+    inverse_factor = lax.linalg.triangular_solve(
+        lower_factor, eye, left_side=True, lower=True)
+    inverse = jnp.einsum("pca,pcb->pab", inverse_factor, inverse_factor,
+                         precision=HIGHEST)
     owner = [(c * col_blocks) // row_blocks for c in range(col_count)]
     window = window + sum(
         lax.ppermute(window, ("prow", "pcol"), [

time: 109 us -> 91.1 us (0.84)
  the two profiles are of different devices: /device:TPU:14 before, /device:TPU:7 now
where the time goes in v3:
time: 91.1 us; the launch traced here: 90.5 us
  other arithmetic  28.5 us (31%)
  starting transfers between devices  22.5 us (25%)
  local copies, waits for them, and re-layouts  16.3 us (18%)
  Pallas kernels  11.7 us (13%)
  waiting for transfers between devices  7.42 us (8%)
  matrix products  3.75 us (4%)
    ppermute x5, starting transfers between devices, doubling_gather(): other = lax.ppermute(block, axis, [(i, i ^ mask) for i in range(count)])  12.5 us
    another operation x4, other arithmetic, per_device(): lower_factor = jnp.linalg.cholesky(whole_diag)  11.9 us
    pallas_call x1, Pallas kernels, apply_update(): pl.pallas_call(kernel, out_shape=jax.ShapeDtypeStruct(front.shape, front....  11.7 us
    another operation x3, other arithmetic, per_device(): lax.linalg.triangular_solve(lower_factor, eye, left_side=True, lower=True)  9.92 us
    concatenate x13, local copies, waits for them, and re-layouts, doubling_gather(): block = jnp.concatenate([block, other], axis=0)  8.88 us
    ppermute x5, waiting for transfers between devices, doubling_gather(): other = lax.ppermute(block, axis, [(i, i ^ mask) for i in range(count)])  7.4 us
    ppermute x3, starting transfers between devices, per_device(): lax.ppermute(window, ('prow', 'pcol'), [(owner[c] * col_count + c, (owner...  5.54 us
    ppermute x3, starting transfers between devices, per_device(): lax.ppermute(diag_blocks, 'prow', [(i, (i + k) % row_count) for i in rang...  4.38 us
  transfers between devices with their start and end apart: 11, of which 3 were waited for; matrix products, arithmetic and copies ran while one was open for 44% of the time, Pallas kernels for 0%

profile of v3, /device:TPU:7, one launch (start us, length us, event | category | flops | bytes accessed | tf_op | source)
XLA Modules:
  0.0 90.5 jit_solution(2970277545792168401)
XLA Ops:
  0.0 1.3 %collective-permute-start.5 = (f32[2,16,64]{2,1,0:T(8,128)}, f32[2,16,64]{2,1,0:T(8,128)S(1)}, u32[]{:S(2)}, u32[]{:S(2)}) collective-permute-start(f32[2,16,64]{2,1,0:T(8,128)} %param.6), channel_id=1, source_target_pairs={{0,32},{32,64},{64,96},{96,0},{1,33},{33,65},{65,97},{97,1},{2,34}... | collective-permute-start | bytes 24584 | tf_op jit(solution)/shard_map/ppermute | solution.py:113
  1.3 1.4 %collective-permute-start.7 = (f32[2,16,64]{2,1,0:T(8,128)}, f32[2,16,64]{2,1,0:T(8,128)S(1)}, u32[]{:S(2)}, u32[]{:S(2)}) collective-permute-start(f32[2,16,64]{2,1,0:T(8,128)} %param.6), channel_id=1, source_target_pairs={{0,96},{32,0},{64,32},{96,64},{1,97},{33,1},{65,33},{97,65},{2,98}... | collective-permute-start | bytes 24584 | tf_op jit(solution)/shard_map/ppermute | solution.py:113
  2.7 1.6 %collective-permute-start.6 = (f32[2,16,64]{2,1,0:T(8,128)}, f32[2,16,64]{2,1,0:T(8,128)S(1)}, u32[]{:S(2)}, u32[]{:S(2)}) collective-permute-start(f32[2,16,64]{2,1,0:T(8,128)} %param.6), channel_id=1, source_target_pairs={{0,64},{32,96},{64,0},{96,32},{1,65},{33,97},{65,1},{97,33},{2,66}... | collective-permute-start | bytes 24584 | tf_op jit(solution)/shard_map/ppermute | solution.py:113
  4.4 0.9 copy.44
  5.3 3.7 %collective-permute-start = (f32[1,64,128]{2,1,0:T(8,128)S(1)}, f32[1,64,128]{2,1,0:T(8,128)S(1)}, u32[]{:S(2)}, u32[]{:S(2)}) collective-permute-start(f32[1,64,128]{2,1,0:T(8,128)S(1)} %copy.44), channel_id=1, source_target_pairs={{0,16},{1,17},{2,18},{3,19},{4,20},{5,21},{6,22},{7,23},{8,24},{9,... | collective-permute-start | bytes 98312 | tf_op jit(solution)/shard_map/ppermute | solution.py:84
  9.0 0.8 constant_dynamic-slice_fusion
  10.0 0.8 compare_reduce_fusion
  10.9 0.7 iota_reduce_fusion
  12.3 1.4 %gather_fusion = s32[32]{0:T(128)S(1)} fusion(s32[32]{0:T(128)} %constant.140.clone, s32[1024]{0:T(1024)S(1)} %get-tuple-element.34), kind=kCustom, calls=%fused_computation | custom fusion | bytes 384 | tf_op jit(solution)/shard_map/jit(_take)/gather | solution.py:110
  14.3 0.8 collective-permute-start.1
  15.1 2.4 %collective-permute-done.1 = f32[2,64,128]{2,1,0:T(8,128)S(1)} collective-permute-done((f32[2,64,128]{2,1,0:T(8,128)S(1)}, f32[2,64,128]{2,1,0:T(8,128)S(1)}, u32[]{:S(2)}, u32[]{:S(2)}) %collective-permute-start.1) | collective-permute-done | bytes 65568 | tf_op jit(solution)/shard_map/ppermute | solution.py:84
  17.5 1.2 %collective-permute-start.2 = (f32[4,64,128]{2,1,0:T(8,128)S(1)}, f32[4,64,128]{2,1,0:T(8,128)S(1)}, u32[]{:S(2)}, u32[]{:S(2)}) collective-permute-start(f32[4,64,128]{2,1,0:T(8,128)S(1)} %pad_maximum_fusion.1), channel_id=1, source_target_pairs={{0,4},{1,5},{2,6},{3,7},{4,0},{5,1},{6,2},{7,3},{8,12},{9,13},{10,... | collective-permute-start | bytes 393224 | tf_op jit(solution)/shard_map/ppermute | solution.py:84
  18.7 1.2 %gather_fusion.1 = s32[128]{0:T(128)S(1)} fusion(s32[32]{0:T(128)S(1)} %and_select_fusion.1, s32[1024]{0:T(1024)S(1)} %get-tuple-element.33), kind=kCustom, calls=%fused_computation.1 | custom fusion | bytes 1536 | tf_op jit(solution)/shard_map/jit(_take)/gather | solution.py:125
  20.7 2.3 %collective-permute-done.2 = f32[4,64,128]{2,1,0:T(8,128)S(1)} collective-permute-done((f32[4,64,128]{2,1,0:T(8,128)S(1)}, f32[4,64,128]{2,1,0:T(8,128)S(1)}, u32[]{:S(2)}, u32[]{:S(2)}) %collective-permute-start.2) | collective-permute-done | bytes 131104 | tf_op jit(solution)/shard_map/ppermute | solution.py:84
  24.8 0.7 constant_dynamic-update-slice_fusion.1
  25.5 2.8 %collective-permute-done.3 = f32[8,64,128]{2,1,0:T(8,128)S(1)} collective-permute-done((f32[8,64,128]{2,1,0:T(8,128)S(1)}, f32[8,64,128]{2,1,0:T(8,128)S(1)}, u32[]{:S(2)}, u32[]{:S(2)}) %collective-permute-start.3) | collective-permute-done | bytes 262176 | tf_op jit(solution)/shard_map/ppermute | solution.py:84
  28.3 0.8 constant_dynamic-update-slice_fusion
  29.0 6.2 %collective-permute-start.4 = (f32[16,64,128]{2,1,0:T(8,128)S(1)}, f32[16,64,128]{2,1,0:T(8,128)S(1)}, u32[]{:S(2)}, u32[]{:S(2)}) collective-permute-start(f32[16,64,128]{2,1,0:T(8,128)S(1)} %get-tuple-element.17), channel_id=1, source_target_pairs={{0,1},{1,0},{2,3},{3,2},{4,5},{5,4},{6,7},{7,6},{8,9},{9,8},{10,11... | collective-permute-start | bytes 1572872 | tf_op jit(solution)/shard_map/ppermute | solution.py:84
  38.1 0.7 copy.29
  38.9 0.7 copy.30
  40.3 1.1 %copy.32 = f32[8,64,2,64]{3,0,1,2:T(8,128)} copy(f32[8,64,2,64]{3,2,1,0:T(2,128)S(1)} %concatenate.43) | data formatting | bytes 524288 | tf_op jit(solution)/shard_map/concatenate | solution.py:85
  42.7 2.6 %concatenate.45 = f32[32,64,2,64]{3,0,1,2:T(8,128)S(1)} concatenate(f32[1,64,2,64]{3,0,1,2:T(1,128)S(1)} %bitcast.54, f32[1,64,2,64]{3,0,1,2:T(1,128)} %copy.29, f32[2,64,2,64]{3,0,1,2:T(2,128)} %copy.30, f32[4,64,2,64]{3,0,1,2:T(4,128)S(1)} %copy.31, f32[8,64,2,64]{3,0,1,2:T(8,128)} %copy.32, f32[16,64,2,64]{3,0,1,2:T(8,128)S(1)} %copy.33), dimensions={0} | concatenate | bytes 2097152 | tf_op jit(solution)/shard_map/concatenate | solution.py:85
  45.3 1.5 %fusion.14 = f32[2,8,64,64]{3,1,2,0:T(8,128)S(1)} fusion(f32[32,64,2,64]{3,0,1,2:T(8,128)S(1)} %concatenate.45, s32[32]{0:T(128)} %broadcast_xor_fusion, s32[2,8]{1,0:T(2,128)} %get-tuple-element.14, pred[2,8]{1,0:T(4,128)(4,1)} %get-tuple-element.13), kind=kOutput, calls=%fused_computation.46 | convolution fusion | flops 25166848 | bytes 1310928 | tf_op jit(solution)/shard_map/pjk,kbpa->pjba/dot_general | solution.py:133
  46.9 2.7 %collective-permute-start.10 = (f32[2,8,64,64]{3,1,2,0:T(8,128)S(1)}, f32[2,8,64,64]{3,1,2,0:T(8,128)S(1)}, u32[]{:S(2)}, u32[]{:S(2)}) collective-permute-start(f32[2,8,64,64]{3,1,2,0:T(8,128)S(1)} %fusion.14), channel_id=1, source_target_pairs={{0,96},{1,97},{2,98},{3,99},{4,100},{5,101},{6,102},{7,103}} | collective-permute-start | bytes 786440 | tf_op jit(solution)/shard_map/ppermute | solution.py:144
  49.6 1.3 %collective-permute-start.9 = (f32[2,8,64,64]{3,1,2,0:T(8,128)S(1)}, f32[2,8,64,64]{3,1,2,0:T(8,128)S(1)}, u32[]{:S(2)}, u32[]{:S(2)}) collective-permute-start(f32[2,8,64,64]{3,1,2,0:T(8,128)S(1)} %fusion.14), channel_id=1, source_target_pairs={{0,64},{1,65},{2,66},{3,67},{4,68},{5,69},{6,70},{7,71},{40,104},{... | collective-permute-start | bytes 786440 | tf_op jit(solution)/shard_map/ppermute | solution.py:144
  50.9 1.5 %collective-permute-start.8 = (f32[2,8,64,64]{3,1,2,0:T(8,128)S(1)}, f32[2,8,64,64]{3,1,2,0:T(8,128)S(1)}, u32[]{:S(2)}, u32[]{:S(2)}) collective-permute-start(f32[2,8,64,64]{3,1,2,0:T(8,128)S(1)} %fusion.14), channel_id=1, source_target_pairs={{0,32},{1,33},{2,34},{3,35},{4,36},{5,37},{6,38},{7,39},{40,72},{4... | collective-permute-start | bytes 786440 | tf_op jit(solution)/shard_map/ppermute | solution.py:144
  52.5 11.7 %custom-call.7 = f32[2,64,64]{2,1,0:T(8,128)S(1)} custom-call(f32[2,64,64]{2,1,0:T(8,128)S(1)} %fusion.7), custom_call_target="Cholesky" | custom-call | tf_op jit(solution)/shard_map/jit(cholesky)/cholesky | solution.py:136
  64.5 9.8 %custom-call.8 = f32[2,1,64,64]{2,3,1,0:T(8,128)S(1)} custom-call(f32[2,1,64,64]{3,2,1,0:T(8,128)S(1)} %select_bitcast_fusion), custom_call_target="InvertDiagBlocksLowerTriangular" | custom-call | tf_op jit(solution)/shard_map/triangular_solve | solution.py:138
  75.0 0.8 constant_dynamic-update-slice_fusion.5.group_ref
  75.9 1.6 %fusion = f32[2,64,8,64]{3,1,2,0:T(8,128)S(1)} fusion(f32[2,64,64,1]{2,1,3,0:T(8,128)S(1)} %convolution_bitcast_fusion, f32[2,8,64,64]{3,1,2,0:T(8,128)S(1)} %add_add_fusion), kind=kOutput, calls=%fused_computation.3 | convolution fusion | flops 50331648 | bytes 557056 | tf_op jit(solution)/shard_map/pxa,pjba->pxjb/dot_general | solution.py:150
  78.0 0.8 fusion.4
  78.8 11.7 %shard_map.64 = f32[4096,512]{1,0:T(8,128)} custom-call(s32[2,64]{1,0:T(2,128)} %compare_select_fusion.5.table_ref, s32[2]{0:T(128)} %pad_add_fusion.place_ref, f32[32,64,128]{2,1,0:T(8,128)} %constant_dynamic-update-slice_fusion.5.group_ref, bf16[128,512]{1,0:T(8,128)(2,1)} %get-tuple-element.16.high_ref, bf16[128,512]{1,0:T(8,128)(2,1)} %get-tuple-element.15.low_ref, ...), custom_call_target="tpu_custom_call" | custom-call | flops 1610612736 | bytes 18087936 | tf_op jit(solution)/shard_map/pallas_call | solution.py:56
  (72 shorter events, 10.5 us)
Async XLA Ops:
  0.0 37.8 %collective-permute-start.5 = (f32[2,16,64]{2,1,0:T(8,128)}, f32[2,16,64]{2,1,0:T(8,128)S(1)}, u32[]{:S(2)}, u32[]{:S(2)}) collective-permute-start(f32[2,16,64]{2,1,0:T(8,128)} %param.6), channel_id=1, source_target_pairs={{0,32},{32,64},{64,96},{96,0},{1,33},{33,65},{65,97},{97,1},{2,34}... | collective-permute-start | bytes 24584 | tf_op jit(solution)/shard_map/ppermute | solution.py:113
  1.3 36.5 %collective-permute-start.7 = (f32[2,16,64]{2,1,0:T(8,128)}, f32[2,16,64]{2,1,0:T(8,128)S(1)}, u32[]{:S(2)}, u32[]{:S(2)}) collective-permute-start(f32[2,16,64]{2,1,0:T(8,128)} %param.6), channel_id=1, source_target_pairs={{0,96},{32,0},{64,32},{96,64},{1,97},{33,1},{65,33},{97,65},{2,98}... | collective-permute-start | bytes 24584 | tf_op jit(solution)/shard_map/ppermute | solution.py:113
  2.7 35.1 %collective-permute-start.6 = (f32[2,16,64]{2,1,0:T(8,128)}, f32[2,16,64]{2,1,0:T(8,128)S(1)}, u32[]{:S(2)}, u32[]{:S(2)}) collective-permute-start(f32[2,16,64]{2,1,0:T(8,128)} %param.6), channel_id=1, source_target_pairs={{0,64},{32,96},{64,0},{96,32},{1,65},{33,97},{65,1},{97,33},{2,66}... | collective-permute-start | bytes 24584 | tf_op jit(solution)/shard_map/ppermute | solution.py:113
  5.3 9.0 %collective-permute-start = (f32[1,64,128]{2,1,0:T(8,128)S(1)}, f32[1,64,128]{2,1,0:T(8,128)S(1)}, u32[]{:S(2)}, u32[]{:S(2)}) collective-permute-start(f32[1,64,128]{2,1,0:T(8,128)S(1)} %copy.44), channel_id=1, source_target_pairs={{0,16},{1,17},{2,18},{3,19},{4,20},{5,21},{6,22},{7,23},{8,24},{9,... | collective-permute-start | bytes 98312 | tf_op jit(solution)/shard_map/ppermute | solution.py:84
  9.0 26.3 %copy-start = (s32[32]{0:T(128)S(1)}, s32[32]{0:T(128)}, u32[]{:S(2)}) copy-start(s32[32]{0:T(128)} %constant.140.clone) | copy-start | bytes 388
  9.0 28.1 %copy-start.3 = (f32[2,64,64]{2,1,0:T(8,128)S(1)}, f32[2,64,64]{2,1,0:T(8,128)}, u32[]{:S(2)}) copy-start(f32[2,64,64]{2,1,0:T(8,128)} %param.7) | copy-start | bytes 98308
  12.3 25.5 %copy-start.5 = (f32[2,16,64]{2,1,0:T(8,128)S(1)}, f32[2,16,64]{2,1,0:T(8,128)}, u32[]{:S(2)}) copy-start(f32[2,16,64]{2,1,0:T(8,128)} %param.6) | copy-start | bytes 24580
  14.3 3.2 %collective-permute-start.1 = (f32[2,64,128]{2,1,0:T(8,128)S(1)}, f32[2,64,128]{2,1,0:T(8,128)S(1)}, u32[]{:S(2)}, u32[]{:S(2)}) collective-permute-start(f32[2,64,128]{2,1,0:T(8,128)S(1)} %pad_maximum_fusion.2), channel_id=1, source_target_pairs={{0,8},{1,9},{2,10},{3,11},{4,12},{5,13},{6,14},{7,15},{8,0},{9,1},... | collective-permute-start | bytes 196616 | tf_op jit(solution)/shard_map/ppermute | solution.py:84
  17.5 5.4 %collective-permute-start.2 = (f32[4,64,128]{2,1,0:T(8,128)S(1)}, f32[4,64,128]{2,1,0:T(8,128)S(1)}, u32[]{:S(2)}, u32[]{:S(2)}) collective-permute-start(f32[4,64,128]{2,1,0:T(8,128)S(1)} %pad_maximum_fusion.1), channel_id=1, source_target_pairs={{0,4},{1,5},{2,6},{3,7},{4,0},{5,1},{6,2},{7,3},{8,12},{9,13},{10,... | collective-permute-start | bytes 393224 | tf_op jit(solution)/shard_map/ppermute | solution.py:84
  23.0 5.3 %collective-permute-start.3 = (f32[8,64,128]{2,1,0:T(8,128)S(1)}, f32[8,64,128]{2,1,0:T(8,128)S(1)}, u32[]{:S(2)}, u32[]{:S(2)}) collective-permute-start(f32[8,64,128]{2,1,0:T(8,128)S(1)} %pad_maximum_fusion), channel_id=1, source_target_pairs={{0,2},{1,3},{2,0},{3,1},{4,6},{5,7},{6,4},{7,5},{8,10},{9,11},{10,... | collective-permute-start | bytes 786440 | tf_op jit(solution)/shard_map/ppermute | solution.py:84
  29.0 12.4 %collective-permute-start.4 = (f32[16,64,128]{2,1,0:T(8,128)S(1)}, f32[16,64,128]{2,1,0:T(8,128)S(1)}, u32[]{:S(2)}, u32[]{:S(2)}) collective-permute-start(f32[16,64,128]{2,1,0:T(8,128)S(1)} %get-tuple-element.17), channel_id=1, source_target_pairs={{0,1},{1,0},{2,3},{3,2},{4,5},{5,4},{6,7},{7,6},{8,9},{9,8},{10,11... | collective-permute-start | bytes 1572872 | tf_op jit(solution)/shard_map/ppermute | solution.py:84
  41.4 1.2 %copy-start.1 = (f32[16,64,128]{2,1,0:T(8,128)}, f32[16,64,128]{2,1,0:T(8,128)S(1)}, u32[]{:S(2)}) copy-start(f32[16,64,128]{2,1,0:T(8,128)S(1)} %collective-permute-done.4) | copy-start | bytes 1572868
  45.3 29.0 %copy-start.4 = (f32[64,64]{1,0:T(8,128)S(1)}, f32[64,64]{1,0:T(8,128)}, u32[]{:S(2)}) copy-start(f32[64,64]{1,0:T(8,128)} %fusion.13) | copy-start | bytes 49156
  45.3 29.6 %copy-start.2 = (f32[16,64,128]{2,1,0:T(8,128)S(1)}, f32[16,64,128]{2,1,0:T(8,128)}, u32[]{:S(2)}) copy-start(f32[16,64,128]{2,1,0:T(8,128)} %copy-done.1) | copy-start | bytes 1572868
  46.9 28.9 %collective-permute-start.10 = (f32[2,8,64,64]{3,1,2,0:T(8,128)S(1)}, f32[2,8,64,64]{3,1,2,0:T(8,128)S(1)}, u32[]{:S(2)}, u32[]{:S(2)}) collective-permute-start(f32[2,8,64,64]{3,1,2,0:T(8,128)S(1)} %fusion.14), channel_id=1, source_target_pairs={{0,96},{1,97},{2,98},{3,99},{4,100},{5,101},{6,102},{7,103}} | collective-permute-start | bytes 786440 | tf_op jit(solution)/shard_map/ppermute | solution.py:144
  49.6 26.2 %collective-permute-start.9 = (f32[2,8,64,64]{3,1,2,0:T(8,128)S(1)}, f32[2,8,64,64]{3,1,2,0:T(8,128)S(1)}, u32[]{:S(2)}, u32[]{:S(2)}) collective-permute-start(f32[2,8,64,64]{3,1,2,0:T(8,128)S(1)} %fusion.14), channel_id=1, source_target_pairs={{0,64},{1,65},{2,66},{3,67},{4,68},{5,69},{6,70},{7,71},{40,104},{... | collective-permute-start | bytes 786440 | tf_op jit(solution)/shard_map/ppermute | solution.py:144
  50.9 24.9 %collective-permute-start.8 = (f32[2,8,64,64]{3,1,2,0:T(8,128)S(1)}, f32[2,8,64,64]{3,1,2,0:T(8,128)S(1)}, u32[]{:S(2)}, u32[]{:S(2)}) collective-permute-start(f32[2,8,64,64]{3,1,2,0:T(8,128)S(1)} %fusion.14), channel_id=1, source_target_pairs={{0,32},{1,33},{2,34},{3,35},{4,36},{5,37},{6,38},{7,39},{40,72},{4... | collective-permute-start | bytes 786440 | tf_op jit(solution)/shard_map/ppermute | solution.py:144

commit v4 on v3

--- a/solution.py
+++ b/solution.py
@@ -19,38 +19,53 @@
 
 
 def front_kernel(width, row_blocks, col_blocks, table_ref, place_ref,
-                 group_ref, high_ref, low_ref, front_ref, out_ref, left_ref):
+                 group_ref, stack_ref, front_ref, out_ref, left_ref):
     step = pl.program_id(0)
     tile_rows, cols = front_ref.shape
     per_tile = tile_rows // width
-    lane = lax.broadcasted_iota(jnp.int32, (width, 2 * width), 1)
-    for local in range(per_tile):
-        block = step * per_tile + local
-        first = table_ref[0, block]
-        second = table_ref[1, block]
-        from_first = group_ref[jnp.maximum(first, 0)]
-        from_second = group_ref[jnp.maximum(second, 0)]
-        left_ref[local * width:(local + 1) * width, :] = jnp.where(
-            lane < width,
-            jnp.where(first >= 0, from_first, 0.0),
-            jnp.where(second >= 0, from_second, 0.0),
-        )
-    left_high, left_low = split_bf16(left_ref[...])
-    right_high = high_ref[...]
-    update = jnp.dot(left_high, right_high, preferred_element_type=jnp.float32)
-    update += jnp.dot(left_high, low_ref[...], preferred_element_type=jnp.float32)
-    update += jnp.dot(left_low, right_high, preferred_element_type=jnp.float32)
-    row0 = place_ref[0] * (row_blocks * width) + step * tile_rows
-    col0 = place_ref[1] * (col_blocks * width)
-    rows = row0 + lax.broadcasted_iota(jnp.int32, (tile_rows, cols), 0)
-    cols_at = col0 + lax.broadcasted_iota(jnp.int32, (tile_rows, cols), 1)
-    lower = rows >= jnp.bitwise_and(cols_at, -width)
-    out_ref[...] = front_ref[...] - jnp.where(lower, update, 0.0)
+    first_row = place_ref[0] * row_blocks + step * per_tile
+    first_col = place_ref[1] * col_blocks
+
+    def update():
+        lane = lax.broadcasted_iota(jnp.int32, (width, 2 * width), 1)
+        for local in range(per_tile):
+            block = step * per_tile + local
+            first = table_ref[0, block]
+            second = table_ref[1, block]
+            from_first = group_ref[jnp.maximum(first, 0)]
+            from_second = group_ref[jnp.maximum(second, 0)]
+            left_ref[local * width:(local + 1) * width, :] = jnp.where(
+                lane < width,
+                jnp.where(first >= 0, from_first, 0.0),
+                jnp.where(second >= 0, from_second, 0.0),
+            )
+        high, low = split_bf16(left_ref[...])
+        return jnp.dot(jnp.concatenate([high, high, low], axis=1), stack_ref[...],
+                       preferred_element_type=jnp.float32)
+
+    all_upper = first_row + per_tile <= first_col
+    all_lower = first_row >= first_col + col_blocks - 1
+
+    @pl.when(all_upper)
+    def _():
+        out_ref[...] = front_ref[...]
+
+    @pl.when(all_lower)
+    def _():
+        out_ref[...] = front_ref[...] - update()
+
+    @pl.when(jnp.logical_not(all_upper | all_lower))
+    def _():
+        rows = first_row * width + lax.broadcasted_iota(jnp.int32, (tile_rows, cols), 0)
+        cols_at = first_col * width + lax.broadcasted_iota(jnp.int32, (tile_rows, cols), 1)
+        lower = rows >= jnp.bitwise_and(cols_at, -width)
+        out_ref[...] = front_ref[...] - jnp.where(lower, update(), 0.0)
 
 
 def apply_update(table, place, group, right, front, width, row_blocks, col_blocks):
     rows, cols = front.shape
     high, low = split_bf16(right)
+    stack = jnp.concatenate([high, low, high], axis=0)
     tiles = rows // TILE_ROWS
     kernel = functools.partial(front_kernel, width, row_blocks, col_blocks)
     return pl.pallas_call(
@@ -61,8 +76,7 @@
             grid=(tiles,),
             in_specs=[
                 pl.BlockSpec(group.shape, lambda i, t, p: (0, 0, 0)),
-                pl.BlockSpec(right.shape, lambda i, t, p: (0, 0)),
-                pl.BlockSpec(right.shape, lambda i, t, p: (0, 0)),
+                pl.BlockSpec(stack.shape, lambda i, t, p: (0, 0)),
                 pl.BlockSpec((TILE_ROWS, cols), lambda i, t, p: (i, 0)),
             ],
             out_specs=pl.BlockSpec((TILE_ROWS, cols), lambda i, t, p: (i, 0)),
@@ -70,10 +84,10 @@
         ),
         cost_estimate=pl.CostEstimate(
             flops=3 * 2 * rows * cols * 2 * width,
-            bytes_accessed=2 * rows * cols * 4 + group.size * 4 + right.size * 4,
+            bytes_accessed=2 * rows * cols * 4 + group.size * 4 + stack.size * 2,
             transcendentals=0,
         ),
-    )(table, place, group, high, low, front)
+    )(table, place, group, stack, front)
 
 
 def doubling_gather(block, axis, count):

time: 91.1 us -> 89.9 us (0.987)
  the two profiles are of different devices: /device:TPU:7 before, /device:TPU:14 now
where the time goes in v4:
time: 89.9 us; the launch traced here: 89.1 us
  other arithmetic  28.6 us (32%)
  local copies, waits for them, and re-layouts  16.3 us (18%)
  starting transfers between devices  14.6 us (16%)
  waiting for transfers between devices  14 us (16%)
  Pallas kernels  11.5 us (13%)
  matrix products  3.75 us (4%)
    another operation x4, other arithmetic, per_device(): lower_factor = jnp.linalg.cholesky(whole_diag)  11.9 us
    pallas_call x1, Pallas kernels, apply_update(): pl.pallas_call(kernel, out_shape=jax.ShapeDtypeStruct(front.shape, front....  11.5 us
    ppermute x5, waiting for transfers between devices, doubling_gather(): other = lax.ppermute(block, axis, [(i, i ^ mask) for i in range(count)])  11 us
    another operation x3, other arithmetic, per_device(): lax.linalg.triangular_solve(lower_factor, eye, left_side=True, lower=True)  9.92 us
    concatenate x13, local copies, waits for them, and re-layouts, doubling_gather(): block = jnp.concatenate([block, other], axis=0)  8.88 us
    ppermute x5, starting transfers between devices, doubling_gather(): other = lax.ppermute(block, axis, [(i, i ^ mask) for i in range(count)])  7.39 us
    ppermute x3, starting transfers between devices, per_device(): lax.ppermute(diag_blocks, 'prow', [(i, (i + k) % row_count) for i in rang...  4.32 us
    ppermute x3, waiting for transfers between devices, per_device(): lax.ppermute(window, ('prow', 'pcol'), [(owner[c] * col_count + c, (owner...  2.92 us
  transfers between devices with their start and end apart: 11, of which 4 were waited for; matrix products, arithmetic and copies ran while one was open for 45% of the time, Pallas kernels for 0%

profile of v4, /device:TPU:14, one launch (start us, length us, event | category | flops | bytes accessed | tf_op | source)
XLA Modules:
  0.0 89.1 jit_solution(17736856714977800225)
XLA Ops:
  0.0 1.6 %collective-permute-start.5 = (f32[2,16,64]{2,1,0:T(8,128)}, f32[2,16,64]{2,1,0:T(8,128)S(1)}, u32[]{:S(2)}, u32[]{:S(2)}) collective-permute-start(f32[2,16,64]{2,1,0:T(8,128)} %param.6), channel_id=1, source_target_pairs={{0,32},{32,64},{64,96},{96,0},{1,33},{33,65},{65,97},{97,1},{2,34}... | collective-permute-start | bytes 24584 | tf_op jit(solution)/shard_map/ppermute | solution.py:127
  2.0 2.3 %collective-permute-start.6 = (f32[2,16,64]{2,1,0:T(8,128)}, f32[2,16,64]{2,1,0:T(8,128)S(1)}, u32[]{:S(2)}, u32[]{:S(2)}) collective-permute-start(f32[2,16,64]{2,1,0:T(8,128)} %param.6), channel_id=1, source_target_pairs={{0,64},{32,96},{64,0},{96,32},{1,65},{33,97},{65,1},{97,33},{2,66}... | collective-permute-start | bytes 24584 | tf_op jit(solution)/shard_map/ppermute | solution.py:127
  4.3 0.9 %copy.44 = f32[1,64,128]{2,1,0:T(8,128)S(1)} copy(f32[1,64,128]{1,2,0:T(8,128)} %bitcast.55) | data formatting | bytes 65536 | tf_op jit(solution)/shard_map/broadcast_in_dim;reshape | solution.py:121
  5.2 4.0 %collective-permute-start = (f32[1,64,128]{2,1,0:T(8,128)S(1)}, f32[1,64,128]{2,1,0:T(8,128)S(1)}, u32[]{:S(2)}, u32[]{:S(2)}) collective-permute-start(f32[1,64,128]{2,1,0:T(8,128)S(1)} %copy.44), channel_id=1, source_target_pairs={{0,16},{1,17},{2,18},{3,19},{4,20},{5,21},{6,22},{7,23},{8,24},{9,... | collective-permute-start | bytes 98312 | tf_op jit(solution)/shard_map/ppermute | solution.py:98
  9.2 0.8 constant_dynamic-slice_fusion
  10.2 0.8 compare_reduce_fusion
  11.1 0.7 iota_reduce_fusion
  12.5 1.4 %gather_fusion = s32[32]{0:T(128)S(1)} fusion(s32[32]{0:T(128)} %constant.140.clone, s32[1024]{0:T(1024)S(1)} %get-tuple-element.34), kind=kCustom, calls=%fused_computation | custom fusion | bytes 384 | tf_op jit(solution)/shard_map/jit(_take)/gather | solution.py:124
  14.5 1.1 %collective-permute-start.1 = (f32[2,64,128]{2,1,0:T(8,128)S(1)}, f32[2,64,128]{2,1,0:T(8,128)S(1)}, u32[]{:S(2)}, u32[]{:S(2)}) collective-permute-start(f32[2,64,128]{2,1,0:T(8,128)S(1)} %pad_maximum_fusion.3), channel_id=1, source_target_pairs={{0,8},{1,9},{2,10},{3,11},{4,12},{5,13},{6,14},{7,15},{8,0},{9,1},... | collective-permute-start | bytes 196616 | tf_op jit(solution)/shard_map/ppermute | solution.py:98
  15.7 3.2 %collective-permute-done.1 = f32[2,64,128]{2,1,0:T(8,128)S(1)} collective-permute-done((f32[2,64,128]{2,1,0:T(8,128)S(1)}, f32[2,64,128]{2,1,0:T(8,128)S(1)}, u32[]{:S(2)}, u32[]{:S(2)}) %collective-permute-start.1) | collective-permute-done | bytes 65568 | tf_op jit(solution)/shard_map/ppermute | solution.py:98
  18.9 1.5 %collective-permute-start.2 = (f32[4,64,128]{2,1,0:T(8,128)S(1)}, f32[4,64,128]{2,1,0:T(8,128)S(1)}, u32[]{:S(2)}, u32[]{:S(2)}) collective-permute-start(f32[4,64,128]{2,1,0:T(8,128)S(1)} %pad_maximum_fusion.2), channel_id=1, source_target_pairs={{0,4},{1,5},{2,6},{3,7},{4,0},{5,1},{6,2},{7,3},{8,12},{9,13},{10,... | collective-permute-start | bytes 393224 | tf_op jit(solution)/shard_map/ppermute | solution.py:98
  20.4 1.2 %gather_fusion.1 = s32[128]{0:T(128)S(1)} fusion(s32[32]{0:T(128)S(1)} %and_select_fusion.1, s32[1024]{0:T(1024)S(1)} %get-tuple-element.33), kind=kCustom, calls=%fused_computation.1 | custom fusion | bytes 1536 | tf_op jit(solution)/shard_map/jit(_take)/gather | solution.py:139
  22.3 4.1 %collective-permute-done.2 = f32[4,64,128]{2,1,0:T(8,128)S(1)} collective-permute-done((f32[4,64,128]{2,1,0:T(8,128)S(1)}, f32[4,64,128]{2,1,0:T(8,128)S(1)}, u32[]{:S(2)}, u32[]{:S(2)}) %collective-permute-start.2) | collective-permute-done | bytes 131104 | tf_op jit(solution)/shard_map/ppermute | solution.py:98
  26.4 0.9 collective-permute-start.3
  28.5 0.7 constant_dynamic-update-slice_fusion.1
  29.2 3.7 %collective-permute-done.3 = f32[8,64,128]{2,1,0:T(8,128)S(1)} collective-permute-done((f32[8,64,128]{2,1,0:T(8,128)S(1)}, f32[8,64,128]{2,1,0:T(8,128)S(1)}, u32[]{:S(2)}, u32[]{:S(2)}) %collective-permute-start.3) | collective-permute-done | bytes 262176 | tf_op jit(solution)/shard_map/ppermute | solution.py:98
  32.9 0.8 constant_dynamic-update-slice_fusion
  36.5 0.7 copy.29
  37.3 0.7 copy.30
  38.7 1.1 %copy.32 = f32[8,64,2,64]{3,0,1,2:T(8,128)} copy(f32[8,64,2,64]{3,2,1,0:T(2,128)S(1)} %concatenate.46) | data formatting | bytes 524288 | tf_op jit(solution)/shard_map/concatenate | solution.py:99
  41.1 2.6 %concatenate.48 = f32[32,64,2,64]{3,0,1,2:T(8,128)S(1)} concatenate(f32[1,64,2,64]{3,0,1,2:T(1,128)S(1)} %bitcast.54, f32[1,64,2,64]{3,0,1,2:T(1,128)} %copy.29, f32[2,64,2,64]{3,0,1,2:T(2,128)} %copy.30, f32[4,64,2,64]{3,0,1,2:T(4,128)S(1)} %copy.31, f32[8,64,2,64]{3,0,1,2:T(8,128)} %copy.32, f32[16,64,2,64]{3,0,1,2:T(8,128)S(1)} %copy.33), dimensions={0} | concatenate | bytes 2097152 | tf_op jit(solution)/shard_map/concatenate | solution.py:99
  43.8 1.5 %fusion.14 = f32[2,8,64,64]{3,1,2,0:T(8,128)S(1)} fusion(f32[32,64,2,64]{3,0,1,2:T(8,128)S(1)} %concatenate.48, s32[32]{0:T(128)} %broadcast_xor_fusion, s32[2,8]{1,0:T(2,128)} %get-tuple-element.14, pred[2,8]{1,0:T(4,128)(4,1)} %get-tuple-element.13), kind=kOutput, calls=%fused_computation.47 | convolution fusion | flops 25166848 | bytes 1310928 | tf_op jit(solution)/shard_map/pjk,kbpa->pjba/dot_general | solution.py:147
  45.3 0.7 collective-permute-start.10
  46.0 0.7 collective-permute-start.9
  46.7 1.5 %collective-permute-start.8 = (f32[2,8,64,64]{3,1,2,0:T(8,128)S(1)}, f32[2,8,64,64]{3,1,2,0:T(8,128)S(1)}, u32[]{:S(2)}, u32[]{:S(2)}) collective-permute-start(f32[2,8,64,64]{3,1,2,0:T(8,128)S(1)} %fusion.14), channel_id=1, source_target_pairs={{0,32},{1,33},{2,34},{3,35},{4,36},{5,37},{6,38},{7,39},{40,72},{4... | collective-permute-start | bytes 786440 | tf_op jit(solution)/shard_map/ppermute | solution.py:158
  48.3 11.7 %custom-call.7 = f32[2,64,64]{2,1,0:T(8,128)S(1)} custom-call(f32[2,64,64]{2,1,0:T(8,128)S(1)} %fusion.7), custom_call_target="Cholesky" | custom-call | tf_op jit(solution)/shard_map/jit(cholesky)/cholesky | solution.py:150
  60.3 9.8 %custom-call.8 = f32[2,1,64,64]{2,3,1,0:T(8,128)S(1)} custom-call(f32[2,1,64,64]{3,2,1,0:T(8,128)S(1)} %select_bitcast_fusion), custom_call_target="InvertDiagBlocksLowerTriangular" | custom-call | tf_op jit(solution)/shard_map/triangular_solve | solution.py:152
  70.7 0.8 constant_dynamic-update-slice_fusion.5.group_ref
  71.6 2.9 %collective-permute-done.8 = f32[2,8,64,64]{3,1,2,0:T(8,128)S(1)} collective-permute-done((f32[2,8,64,64]{3,1,2,0:T(8,128)S(1)}, f32[2,8,64,64]{3,1,2,0:T(8,128)S(1)}, u32[]{:S(2)}, u32[]{:S(2)}) %collective-permute-start.8) | collective-permute-done | bytes 262176 | tf_op jit(solution)/shard_map/ppermute | solution.py:158
  74.6 1.6 %fusion = f32[2,64,8,64]{3,1,2,0:T(8,128)S(1)} fusion(f32[2,64,64,1]{2,1,3,0:T(8,128)S(1)} %convolution_bitcast_fusion, f32[2,8,64,64]{3,1,2,0:T(8,128)S(1)} %add_add_fusion), kind=kOutput, calls=%fused_computation.3 | convolution fusion | flops 50331648 | bytes 557056 | tf_op jit(solution)/shard_map/pxa,pjba->pxjb/dot_general | solution.py:164
  76.7 0.8 pad_maximum_fusion.stack_ref
  77.5 11.5 %shard_map.64 = f32[4096,512]{1,0:T(8,128)} custom-call(s32[2,64]{1,0:T(2,128)} %compare_select_fusion.5.table_ref, s32[2]{0:T(128)} %pad_add_fusion.place_ref, f32[32,64,128]{2,1,0:T(8,128)} %constant_dynamic-update-slice_fusion.5.group_ref, bf16[384,512]{1,0:T(8,128)(2,1)} %pad_maximum_fusion.stack_ref, f32[4096,512]{1,0:T(8,128)} %front_ref.1), custom_call_target="tpu_custom_call" | custom-call | flops 1610612736 | bytes 18219008 | tf_op jit(solution)/shard_map/pallas_call | solution.py:71
  (73 shorter events, 10.4 us)
Async XLA Ops:
  0.0 36.2 %collective-permute-start.5 = (f32[2,16,64]{2,1,0:T(8,128)}, f32[2,16,64]{2,1,0:T(8,128)S(1)}, u32[]{:S(2)}, u32[]{:S(2)}) collective-permute-start(f32[2,16,64]{2,1,0:T(8,128)} %param.6), channel_id=1, source_target_pairs={{0,32},{32,64},{64,96},{96,0},{1,33},{33,65},{65,97},{97,1},{2,34}... | collective-permute-start | bytes 24584 | tf_op jit(solution)/shard_map/ppermute | solution.py:127
  1.6 34.7 %collective-permute-start.7 = (f32[2,16,64]{2,1,0:T(8,128)}, f32[2,16,64]{2,1,0:T(8,128)S(1)}, u32[]{:S(2)}, u32[]{:S(2)}) collective-permute-start(f32[2,16,64]{2,1,0:T(8,128)} %param.6), channel_id=1, source_target_pairs={{0,96},{32,0},{64,32},{96,64},{1,97},{33,1},{65,33},{97,65},{2,98}... | collective-permute-start | bytes 24584 | tf_op jit(solution)/shard_map/ppermute | solution.py:127
  2.0 34.2 %collective-permute-start.6 = (f32[2,16,64]{2,1,0:T(8,128)}, f32[2,16,64]{2,1,0:T(8,128)S(1)}, u32[]{:S(2)}, u32[]{:S(2)}) collective-permute-start(f32[2,16,64]{2,1,0:T(8,128)} %param.6), channel_id=1, source_target_pairs={{0,64},{32,96},{64,0},{96,32},{1,65},{33,97},{65,1},{97,33},{2,66}... | collective-permute-start | bytes 24584 | tf_op jit(solution)/shard_map/ppermute | solution.py:127
  5.2 9.3 %collective-permute-start = (f32[1,64,128]{2,1,0:T(8,128)S(1)}, f32[1,64,128]{2,1,0:T(8,128)S(1)}, u32[]{:S(2)}, u32[]{:S(2)}) collective-permute-start(f32[1,64,128]{2,1,0:T(8,128)S(1)} %copy.44), channel_id=1, source_target_pairs={{0,16},{1,17},{2,18},{3,19},{4,20},{5,21},{6,22},{7,23},{8,24},{9,... | collective-permute-start | bytes 98312 | tf_op jit(solution)/shard_map/ppermute | solution.py:98
  9.2 24.5 %copy-start = (s32[32]{0:T(128)S(1)}, s32[32]{0:T(128)}, u32[]{:S(2)}) copy-start(s32[32]{0:T(128)} %constant.140.clone) | copy-start | bytes 388
  9.2 26.3 %copy-start.3 = (f32[2,64,64]{2,1,0:T(8,128)S(1)}, f32[2,64,64]{2,1,0:T(8,128)}, u32[]{:S(2)}) copy-start(f32[2,64,64]{2,1,0:T(8,128)} %param.7) | copy-start | bytes 98308
  12.5 23.7 %copy-start.5 = (f32[2,16,64]{2,1,0:T(8,128)S(1)}, f32[2,16,64]{2,1,0:T(8,128)}, u32[]{:S(2)}) copy-start(f32[2,16,64]{2,1,0:T(8,128)} %param.6) | copy-start | bytes 24580
  14.5 4.3 %collective-permute-start.1 = (f32[2,64,128]{2,1,0:T(8,128)S(1)}, f32[2,64,128]{2,1,0:T(8,128)S(1)}, u32[]{:S(2)}, u32[]{:S(2)}) collective-permute-start(f32[2,64,128]{2,1,0:T(8,128)S(1)} %pad_maximum_fusion.3), channel_id=1, source_target_pairs={{0,8},{1,9},{2,10},{3,11},{4,12},{5,13},{6,14},{7,15},{8,0},{9,1},... | collective-permute-start | bytes 196616 | tf_op jit(solution)/shard_map/ppermute | solution.py:98
  18.9 7.5 %collective-permute-start.2 = (f32[4,64,128]{2,1,0:T(8,128)S(1)}, f32[4,64,128]{2,1,0:T(8,128)S(1)}, u32[]{:S(2)}, u32[]{:S(2)}) collective-permute-start(f32[4,64,128]{2,1,0:T(8,128)S(1)} %pad_maximum_fusion.2), channel_id=1, source_target_pairs={{0,4},{1,5},{2,6},{3,7},{4,0},{5,1},{6,2},{7,3},{8,12},{9,13},{10,... | collective-permute-start | bytes 393224 | tf_op jit(solution)/shard_map/ppermute | solution.py:98
  26.4 6.5 %collective-permute-start.3 = (f32[8,64,128]{2,1,0:T(8,128)S(1)}, f32[8,64,128]{2,1,0:T(8,128)S(1)}, u32[]{:S(2)}, u32[]{:S(2)}) collective-permute-start(f32[8,64,128]{2,1,0:T(8,128)S(1)} %pad_maximum_fusion.1), channel_id=1, source_target_pairs={{0,2},{1,3},{2,0},{3,1},{4,6},{5,7},{6,4},{7,5},{8,10},{9,11},{10,... | collective-permute-start | bytes 786440 | tf_op jit(solution)/shard_map/ppermute | solution.py:98
  33.6 6.2 %collective-permute-start.4 = (f32[16,64,128]{2,1,0:T(8,128)S(1)}, f32[16,64,128]{2,1,0:T(8,128)S(1)}, u32[]{:S(2)}, u32[]{:S(2)}) collective-permute-start(f32[16,64,128]{2,1,0:T(8,128)S(1)} %get-tuple-element.17), channel_id=1, source_target_pairs={{0,1},{1,0},{2,3},{3,2},{4,5},{5,4},{6,7},{7,6},{8,9},{9,8},{10,11... | collective-permute-start | bytes 1572872 | tf_op jit(solution)/shard_map/ppermute | solution.py:98
  39.9 1.2 %copy-start.1 = (f32[16,64,128]{2,1,0:T(8,128)}, f32[16,64,128]{2,1,0:T(8,128)S(1)}, u32[]{:S(2)}) copy-start(f32[16,64,128]{2,1,0:T(8,128)S(1)} %collective-permute-done.4) | copy-start | bytes 1572868
  43.7 26.4 %copy-start.4 = (f32[64,64]{1,0:T(8,128)S(1)}, f32[64,64]{1,0:T(8,128)}, u32[]{:S(2)}) copy-start(f32[64,64]{1,0:T(8,128)} %fusion.13) | copy-start | bytes 49156
  43.7 27.0 %copy-start.2 = (f32[16,64,128]{2,1,0:T(8,128)S(1)}, f32[16,64,128]{2,1,0:T(8,128)}, u32[]{:S(2)}) copy-start(f32[16,64,128]{2,1,0:T(8,128)} %copy-done.1) | copy-start | bytes 1572868
  45.3 26.3 %collective-permute-start.10 = (f32[2,8,64,64]{3,1,2,0:T(8,128)S(1)}, f32[2,8,64,64]{3,1,2,0:T(8,128)S(1)}, u32[]{:S(2)}, u32[]{:S(2)}) collective-permute-start(f32[2,8,64,64]{3,1,2,0:T(8,128)S(1)} %fusion.14), channel_id=1, source_target_pairs={{0,96},{1,97},{2,98},{3,99},{4,100},{5,101},{6,102},{7,103}} | collective-permute-start | bytes 786440 | tf_op jit(solution)/shard_map/ppermute | solution.py:158
  46.0 25.6 %collective-permute-start.9 = (f32[2,8,64,64]{3,1,2,0:T(8,128)S(1)}, f32[2,8,64,64]{3,1,2,0:T(8,128)S(1)}, u32[]{:S(2)}, u32[]{:S(2)}) collective-permute-start(f32[2,8,64,64]{3,1,2,0:T(8,128)S(1)} %fusion.14), channel_id=1, source_target_pairs={{0,64},{1,65},{2,66},{3,67},{4,68},{5,69},{6,70},{7,71},{40,104},{... | collective-permute-start | bytes 786440 | tf_op jit(solution)/shard_map/ppermute | solution.py:158
  46.7 27.8 %collective-permute-start.8 = (f32[2,8,64,64]{3,1,2,0:T(8,128)S(1)}, f32[2,8,64,64]{3,1,2,0:T(8,128)S(1)}, u32[]{:S(2)}, u32[]{:S(2)}) collective-permute-start(f32[2,8,64,64]{3,1,2,0:T(8,128)S(1)} %fusion.14), channel_id=1, source_target_pairs={{0,32},{1,33},{2,34},{3,35},{4,36},{5,37},{6,38},{7,39},{40,72},{4... | collective-permute-start | bytes 786440 | tf_op jit(solution)/shard_map/ppermute | solution.py:158

commit v5 on v4

--- a/solution.py
+++ b/solution.py
@@ -19,10 +19,17 @@
 
 
 def front_kernel(width, row_blocks, col_blocks, table_ref, place_ref,
-                 group_ref, stack_ref, front_ref, out_ref, left_ref):
+                 near_ref, far_ref, stack_ref, front_ref, out_ref, left_ref):
     step = pl.program_id(0)
     tile_rows, cols = front_ref.shape
     per_tile = tile_rows // width
+    half = near_ref.shape[0]
+
+    def held(slot):
+        near = near_ref[jnp.clip(slot, 0, half - 1)]
+        far = far_ref[jnp.clip(slot - half, 0, half - 1)]
+        return jnp.where(slot < half, near, far)
+
     first_row = place_ref[0] * row_blocks + step * per_tile
     first_col = place_ref[1] * col_blocks
 
@@ -32,8 +39,8 @@
             block = step * per_tile + local
             first = table_ref[0, block]
             second = table_ref[1, block]
-            from_first = group_ref[jnp.maximum(first, 0)]
-            from_second = group_ref[jnp.maximum(second, 0)]
+            from_first = held(first)
+            from_second = held(second)
             left_ref[local * width:(local + 1) * width, :] = jnp.where(
                 lane < width,
                 jnp.where(first >= 0, from_first, 0.0),
@@ -62,7 +69,7 @@
         out_ref[...] = front_ref[...] - jnp.where(lower, update(), 0.0)
 
 
-def apply_update(table, place, group, right, front, width, row_blocks, col_blocks):
+def apply_update(table, place, near, far, right, front, width, row_blocks, col_blocks):
     rows, cols = front.shape
     high, low = split_bf16(right)
     stack = jnp.concatenate([high, low, high], axis=0)
@@ -75,7 +82,8 @@
             num_scalar_prefetch=2,
             grid=(tiles,),
             in_specs=[
-                pl.BlockSpec(group.shape, lambda i, t, p: (0, 0, 0)),
+                pl.BlockSpec(near.shape, lambda i, t, p: (0, 0, 0)),
+                pl.BlockSpec(far.shape, lambda i, t, p: (0, 0, 0)),
                 pl.BlockSpec(stack.shape, lambda i, t, p: (0, 0)),
                 pl.BlockSpec((TILE_ROWS, cols), lambda i, t, p: (i, 0)),
             ],
@@ -84,10 +92,10 @@
         ),
         cost_estimate=pl.CostEstimate(
             flops=3 * 2 * rows * cols * 2 * width,
-            bytes_accessed=2 * rows * cols * 4 + group.size * 4 + stack.size * 2,
+            bytes_accessed=2 * rows * cols * 4 + 2 * near.size * 4 + stack.size * 2,
             transcendentals=0,
         ),
-    )(table, place, group, stack, front)
+    )(table, place, near, far, stack, front)
 
 
 def doubling_gather(block, axis, count):
@@ -96,9 +104,10 @@
     for bit in reversed(range(bits)):
         mask = 1 << bit
         other = lax.ppermute(block, axis, [(i, i ^ mask) for i in range(count)])
+        spread = spread + [s ^ mask for s in spread]
+        if bit == 0:
+            return block, other, spread
         block = jnp.concatenate([block, other], axis=0)
-        spread = spread + [s ^ mask for s in spread]
-    return block, spread
 
 
 def first_match(mapping, targets):
@@ -118,7 +127,8 @@
     row_count = lax.axis_size("prow")
 
     local = jnp.transpose(panel_rows, (2, 0, 1)).reshape(width, 2 * width)
-    group, spread = doubling_gather(local[None], "pcol", col_count)
+    near, far, spread = doubling_gather(local[None], "pcol", col_count)
+    half = near.shape[0]
     child_at = jnp.bitwise_xor(col_index, jnp.asarray(spread, jnp.int32))
     slot_of = jnp.bitwise_xor(col_index, jnp.arange(col_count, dtype=jnp.int32))
     slot_of = jnp.take(jnp.asarray(np.argsort(spread), jnp.int32), slot_of)
@@ -144,8 +154,12 @@
     picks = first_match(source_map, first_col + jnp.arange(col_blocks, dtype=jnp.int32))
     keep = (picks >= 0) & (row_index == source)
     select = (picks[:, :, None] == child_at) & keep[:, :, None]
-    window = jnp.einsum("pjk,kbpa->pjba", select.astype(jnp.float32),
-                        group.reshape(col_count, width, 2, width), precision=HIGHEST)
+    select = select.astype(jnp.float32)
+    window = sum(
+        jnp.einsum("pjk,kbpa->pjba", select[:, :, part * half:(part + 1) * half],
+                   held.reshape(half, width, 2, width), precision=HIGHEST)
+        for part, held in enumerate((near, far))
+    )
     window, whole_diag = lax.optimization_barrier((window, whole_diag))
     lower_factor = jnp.linalg.cholesky(whole_diag)
     eye = jnp.broadcast_to(jnp.eye(width, dtype=jnp.float32), whole_diag.shape)
@@ -165,7 +179,7 @@
     right = right.reshape(2 * width, col_blocks * width)
 
     place = jnp.stack([row_index, col_index]).astype(jnp.int32)
-    return apply_update(table, place, group, right, front, width, row_blocks, col_blocks)
+    return apply_update(table, place, near, far, right, front, width, row_blocks, col_blocks)
 
 
 def solution(mesh):

time: 89.9 us -> 87.3 us (0.971)
  local copies, waits for them, and re-layouts: 16.3 us -> 8.37 us
  waiting for transfers between devices: 14 us -> 18.7 us
    concatenate x13 -> x10, local copies, waits for them, and re-layouts: 8.88 us -> 2 us  [doubling_gather(): block = jnp.concatenate([block, other], axis=0)]
    ppermute x5, waiting for transfers between devices: 11 us -> 14.8 us  [doubling_gather(): other = lax.ppermute(block, axis, [(i, i ^ mask) for i in range(count)])]
    unnamed x17 -> x9, local copies, waits for them, and re-layouts: 2.62 us -> 0.95 us
    add x1, other arithmetic: 0.1 us -> 1.14 us  [per_device(): window + sum((lax.ppermute(window, ('prow', 'pcol'), [(owner[c] * col_cou...]
    ppermute x3, waiting for transfers between devices: 2.92 us -> 3.83 us  [per_device(): lax.ppermute(window, ('prow', 'pcol'), [(owner[c] * col_count + c, (owner...]
  transfers between devices with their start and end apart: 11 -> 11, of which waited for: 4 -> 4; matrix products, arithmetic and copies ran while one was open for 45% -> 41% of each run, Pallas kernels for 0% -> 0%
where the time goes in v5:
time: 87.3 us; the launch traced here: 86.7 us
  other arithmetic  29.3 us (34%)
  waiting for transfers between devices  18.7 us (21%)
  starting transfers between devices  14.7 us (17%)
  Pallas kernels  11.6 us (13%)
  local copies, waits for them, and re-layouts  8.37 us (10%)
  matrix products  3.77 us (4%)
    ppermute x5, waiting for transfers between devices, doubling_gather(): other = lax.ppermute(block, axis, [(i, i ^ mask) for i in range(count)])  14.8 us
    another operation x4, other arithmetic, per_device(): lower_factor = jnp.linalg.cholesky(whole_diag)  11.9 us
    pallas_call x1, Pallas kernels, apply_update(): pl.pallas_call(kernel, out_shape=jax.ShapeDtypeStruct(front.shape, front....  11.6 us
    another operation x3, other arithmetic, per_device(): lax.linalg.triangular_solve(lower_factor, eye, left_side=True, lower=True)  9.92 us
    ppermute x5, starting transfers between devices, doubling_gather(): other = lax.ppermute(block, axis, [(i, i ^ mask) for i in range(count)])  7.48 us
    ppermute x3, starting transfers between devices, per_device(): lax.ppermute(diag_blocks, 'prow', [(i, (i + k) % row_count) for i in rang...  4.32 us
    ppermute x3, waiting for transfers between devices, per_device(): lax.ppermute(window, ('prow', 'pcol'), [(owner[c] * col_count + c, (owner...  3.83 us
    ppermute x3, starting transfers between devices, per_device(): lax.ppermute(window, ('prow', 'pcol'), [(owner[c] * col_count + c, (owner...  2.86 us
  transfers between devices with their start and end apart: 11, of which 4 were waited for; matrix products, arithmetic and copies ran while one was open for 41% of the time, Pallas kernels for 0%

profile of v5, /device:TPU:14, one launch (start us, length us, event | category | flops | bytes accessed | tf_op | source)
XLA Modules:
  0.0 86.7 jit_solution(17096076920432042638)
XLA Ops:
  0.0 1.6 %collective-permute-start.5 = (f32[2,16,64]{2,1,0:T(8,128)}, f32[2,16,64]{2,1,0:T(8,128)S(1)}, u32[]{:S(2)}, u32[]{:S(2)}) collective-permute-start(f32[2,16,64]{2,1,0:T(8,128)} %param.6), channel_id=1, source_target_pairs={{0,32},{32,64},{64,96},{96,0},{1,33},{33,65},{65,97},{97,1},{2,34}... | collective-permute-start | bytes 24584 | tf_op jit(solution)/shard_map/ppermute | solution.py:137
  2.0 2.3 %collective-permute-start.6 = (f32[2,16,64]{2,1,0:T(8,128)}, f32[2,16,64]{2,1,0:T(8,128)S(1)}, u32[]{:S(2)}, u32[]{:S(2)}) collective-permute-start(f32[2,16,64]{2,1,0:T(8,128)} %param.6), channel_id=1, source_target_pairs={{0,64},{32,96},{64,0},{96,32},{1,65},{33,97},{65,1},{97,33},{2,66}... | collective-permute-start | bytes 24584 | tf_op jit(solution)/shard_map/ppermute | solution.py:137
  4.3 0.9 %copy.45 = f32[1,64,128]{2,1,0:T(8,128)S(1)} copy(f32[1,64,128]{1,2,0:T(8,128)} %bitcast.60) | data formatting | bytes 65536 | tf_op jit(solution)/shard_map/broadcast_in_dim;reshape | solution.py:130
  5.2 4.0 %collective-permute-start = (f32[1,64,128]{2,1,0:T(8,128)S(1)}, f32[1,64,128]{2,1,0:T(8,128)S(1)}, u32[]{:S(2)}, u32[]{:S(2)}) collective-permute-start(f32[1,64,128]{2,1,0:T(8,128)S(1)} %copy.45), channel_id=1, source_target_pairs={{0,16},{1,17},{2,18},{3,19},{4,20},{5,21},{6,22},{7,23},{8,24},{9,... | collective-permute-start | bytes 98312 | tf_op jit(solution)/shard_map/ppermute | solution.py:106
  9.2 0.8 constant_dynamic-slice_fusion
  10.2 0.8 compare_reduce_fusion
  11.1 0.7 iota_reduce_fusion
  11.9 1.4 %gather_fusion = s32[32]{0:T(128)S(1)} fusion(s32[32]{0:T(128)} %constant.140.clone, s32[1024]{0:T(1024)S(1)} %get-tuple-element.24), kind=kCustom, calls=%fused_computation | custom fusion | bytes 384 | tf_op jit(solution)/shard_map/jit(_take)/gather | solution.py:134
  13.3 1.2 %gather_fusion.1 = s32[128]{0:T(128)S(1)} fusion(s32[32]{0:T(128)S(1)} %and_select_fusion.1, s32[1024]{0:T(1024)S(1)} %get-tuple-element.23), kind=kCustom, calls=%fused_computation.1 | custom fusion | bytes 1536 | tf_op jit(solution)/shard_map/jit(_take)/gather | solution.py:149
  15.2 1.1 %collective-permute-start.1 = (f32[2,64,128]{2,1,0:T(8,128)S(1)}, f32[2,64,128]{2,1,0:T(8,128)S(1)}, u32[]{:S(2)}, u32[]{:S(2)}) collective-permute-start(f32[2,64,128]{2,1,0:T(8,128)S(1)} %pad_maximum_fusion.3), channel_id=1, source_target_pairs={{0,8},{1,9},{2,10},{3,11},{4,12},{5,13},{6,14},{7,15},{8,0},{9,1},... | collective-permute-start | bytes 196616 | tf_op jit(solution)/shard_map/ppermute | solution.py:106
  16.3 3.2 %collective-permute-done.1 = f32[2,64,128]{2,1,0:T(8,128)S(1)} collective-permute-done((f32[2,64,128]{2,1,0:T(8,128)S(1)}, f32[2,64,128]{2,1,0:T(8,128)S(1)}, u32[]{:S(2)}, u32[]{:S(2)}) %collective-permute-start.1) | collective-permute-done | bytes 65568 | tf_op jit(solution)/shard_map/ppermute | solution.py:106
  19.6 1.5 %collective-permute-start.2 = (f32[4,64,128]{2,1,0:T(8,128)S(1)}, f32[4,64,128]{2,1,0:T(8,128)S(1)}, u32[]{:S(2)}, u32[]{:S(2)}) collective-permute-start(f32[4,64,128]{2,1,0:T(8,128)S(1)} %pad_maximum_fusion.2), channel_id=1, source_target_pairs={{0,4},{1,5},{2,6},{3,7},{4,0},{5,1},{6,2},{7,3},{8,12},{9,13},{10,... | collective-permute-start | bytes 393224 | tf_op jit(solution)/shard_map/ppermute | solution.py:106
  21.1 6.0 %collective-permute-done.2 = f32[4,64,128]{2,1,0:T(8,128)S(1)} collective-permute-done((f32[4,64,128]{2,1,0:T(8,128)S(1)}, f32[4,64,128]{2,1,0:T(8,128)S(1)}, u32[]{:S(2)}, u32[]{:S(2)}) %collective-permute-start.2) | collective-permute-done | bytes 131104 | tf_op jit(solution)/shard_map/ppermute | solution.py:106
  27.1 0.9 collective-permute-start.3
  28.0 5.6 %collective-permute-done.3 = f32[8,64,128]{2,1,0:T(8,128)S(1)} collective-permute-done((f32[8,64,128]{2,1,0:T(8,128)S(1)}, f32[8,64,128]{2,1,0:T(8,128)S(1)}, u32[]{:S(2)}, u32[]{:S(2)}) %collective-permute-start.3) | collective-permute-done | bytes 262176 | tf_op jit(solution)/shard_map/ppermute | solution.py:106
  33.7 0.7 broadcast_xor_fusion
  34.5 0.7 pad_add_fusion.place_ref
  35.1 0.9 %copy.27 = f32[2,64,64]{1,2,0:T(8,128)S(1)} copy(f32[2,64,64]{2,1,0:T(8,128)} %param.7) | data formatting | bytes 65536 | tf_op args[1]
  36.7 0.8 fusion.10
  39.0 0.6 concatenate.40
  39.6 0.6 reshape.96
  40.2 1.1 %fusion = f32[2,8,64,64]{3,1,2,0:T(8,128)S(1)} fusion(f32[16,64,2,64]{3,2,1,0:T(2,128)S(1)} %reshape.96, pred[2,8,32]{2,1,0:T(8,128)(4,1)S(1)} %compare_and_fusion), kind=kOutput, calls=%fused_computation.4 | convolution fusion | flops 12582912 | bytes 786944 | tf_op jit(solution)/shard_map/pjk,kbpa->pjba/dot_general | solution.py:159
  41.8 0.7 collective-permute-start.10
  42.5 0.7 collective-permute-start.9
  43.2 1.5 %collective-permute-start.8 = (f32[2,8,64,64]{3,1,2,0:T(8,128)S(1)}, f32[2,8,64,64]{3,1,2,0:T(8,128)}, u32[]{:S(2)}, u32[]{:S(2)}) collective-permute-start(f32[2,8,64,64]{3,1,2,0:T(8,128)S(1)} %convolution_add_fusion), channel_id=1, source_target_pairs={{0,32},{1,33},{2,34},{3,35},{4,36},{5,37},{6,38},{7,39},{40,72},{4... | collective-permute-start | bytes 786440 | tf_op jit(solution)/shard_map/ppermute | solution.py:172
  44.8 11.7 %custom-call.7 = f32[2,64,64]{2,1,0:T(8,128)S(1)} custom-call(f32[2,64,64]{2,1,0:T(8,128)S(1)} %fusion.9), custom_call_target="Cholesky" | custom-call | tf_op jit(solution)/shard_map/jit(cholesky)/cholesky | solution.py:164
  56.7 9.8 %custom-call.8 = f32[2,1,64,64]{2,3,1,0:T(8,128)S(1)} custom-call(f32[2,1,64,64]{3,2,1,0:T(8,128)S(1)} %select_bitcast_fusion), custom_call_target="InvertDiagBlocksLowerTriangular" | custom-call | tf_op jit(solution)/shard_map/triangular_solve | solution.py:166
  67.2 3.8 %collective-permute-done.8 = f32[2,8,64,64]{3,1,2,0:T(8,128)} collective-permute-done((f32[2,8,64,64]{3,1,2,0:T(8,128)S(1)}, f32[2,8,64,64]{3,1,2,0:T(8,128)}, u32[]{:S(2)}, u32[]{:S(2)}) %collective-permute-start.8) | collective-permute-done | bytes 262176 | tf_op jit(solution)/shard_map/ppermute | solution.py:172
  71.0 1.1 %add_add_fusion = f32[2,8,64,64]{3,1,2,0:T(8,128)S(1)} fusion(f32[2,8,64,64]{3,1,2,0:T(8,128)S(1)} %convolution_add_fusion, f32[2,8,64,64]{3,1,2,0:T(8,128)S(1)} %collective-permute-done.10, f32[2,8,64,64]{3,1,2,0:T(8,128)} %collective-permute-done.8, f32[2,8,64,64]{3,1,2,0:T(8,128)S(1)} %collective-permute-done.9), kind=kLoop, calls=%fused_computation.8 | loop fusion | flops 196608 | bytes 1310720 | tf_op jit(solution)/shard_map/add | solution.py:171
  72.2 1.6 %fusion.2 = f32[2,64,8,64]{3,1,2,0:T(8,128)S(1)} fusion(f32[2,64,64,1]{2,1,3,0:T(8,128)S(1)} %convolution_bitcast_fusion, f32[2,8,64,64]{3,1,2,0:T(8,128)S(1)} %add_add_fusion), kind=kOutput, calls=%fused_computation.6 | convolution fusion | flops 50331648 | bytes 557056 | tf_op jit(solution)/shard_map/pxa,pjba->pxjb/dot_general | solution.py:178
  74.3 0.8 pad_maximum_fusion.stack_ref
  75.1 11.6 %shard_map.64 = f32[4096,512]{1,0:T(8,128)} custom-call(s32[2,64]{1,0:T(2,128)} %compare_select_fusion.5.table_ref, s32[2]{0:T(128)} %pad_add_fusion.place_ref, f32[16,64,128]{2,1,0:T(8,128)} %copy-done.1, f32[16,64,128]{2,1,0:T(8,128)} %copy-done, bf16[384,512]{1,0:T(8,128)(2,1)} %pad_maximum_fusion.stack_ref, f32[4096,512]{1,0:T(8,128)} %front_ref.1), custom_call_target="tpu_custom_call" | custom-call | flops 1610612736 | bytes 18219008 | tf_op jit(solution)/shard_map/pallas_call | solution.py:78
  (65 shorter events, 5.7 us)
Async XLA Ops:
  0.0 36.7 %collective-permute-start.5 = (f32[2,16,64]{2,1,0:T(8,128)}, f32[2,16,64]{2,1,0:T(8,128)S(1)}, u32[]{:S(2)}, u32[]{:S(2)}) collective-permute-start(f32[2,16,64]{2,1,0:T(8,128)} %param.6), channel_id=1, source_target_pairs={{0,32},{32,64},{64,96},{96,0},{1,33},{33,65},{65,97},{97,1},{2,34}... | collective-permute-start | bytes 24584 | tf_op jit(solution)/shard_map/ppermute | solution.py:137
  1.6 35.1 %collective-permute-start.7 = (f32[2,16,64]{2,1,0:T(8,128)}, f32[2,16,64]{2,1,0:T(8,128)S(1)}, u32[]{:S(2)}, u32[]{:S(2)}) collective-permute-start(f32[2,16,64]{2,1,0:T(8,128)} %param.6), channel_id=1, source_target_pairs={{0,96},{32,0},{64,32},{96,64},{1,97},{33,1},{65,33},{97,65},{2,98}... | collective-permute-start | bytes 24584 | tf_op jit(solution)/shard_map/ppermute | solution.py:137
  2.0 34.7 %collective-permute-start.6 = (f32[2,16,64]{2,1,0:T(8,128)}, f32[2,16,64]{2,1,0:T(8,128)S(1)}, u32[]{:S(2)}, u32[]{:S(2)}) collective-permute-start(f32[2,16,64]{2,1,0:T(8,128)} %param.6), channel_id=1, source_target_pairs={{0,64},{32,96},{64,0},{96,32},{1,65},{33,97},{65,1},{97,33},{2,66}... | collective-permute-start | bytes 24584 | tf_op jit(solution)/shard_map/ppermute | solution.py:137
  5.2 10.0 %collective-permute-start = (f32[1,64,128]{2,1,0:T(8,128)S(1)}, f32[1,64,128]{2,1,0:T(8,128)S(1)}, u32[]{:S(2)}, u32[]{:S(2)}) collective-permute-start(f32[1,64,128]{2,1,0:T(8,128)S(1)} %copy.45), channel_id=1, source_target_pairs={{0,16},{1,17},{2,18},{3,19},{4,20},{5,21},{6,22},{7,23},{8,24},{9,... | collective-permute-start | bytes 98312 | tf_op jit(solution)/shard_map/ppermute | solution.py:106
  15.2 4.3 %collective-permute-start.1 = (f32[2,64,128]{2,1,0:T(8,128)S(1)}, f32[2,64,128]{2,1,0:T(8,128)S(1)}, u32[]{:S(2)}, u32[]{:S(2)}) collective-permute-start(f32[2,64,128]{2,1,0:T(8,128)S(1)} %pad_maximum_fusion.3), channel_id=1, source_target_pairs={{0,8},{1,9},{2,10},{3,11},{4,12},{5,13},{6,14},{7,15},{8,0},{9,1},... | collective-permute-start | bytes 196616 | tf_op jit(solution)/shard_map/ppermute | solution.py:106
  19.6 7.5 %collective-permute-start.2 = (f32[4,64,128]{2,1,0:T(8,128)S(1)}, f32[4,64,128]{2,1,0:T(8,128)S(1)}, u32[]{:S(2)}, u32[]{:S(2)}) collective-permute-start(f32[4,64,128]{2,1,0:T(8,128)S(1)} %pad_maximum_fusion.2), channel_id=1, source_target_pairs={{0,4},{1,5},{2,6},{3,7},{4,0},{5,1},{6,2},{7,3},{8,12},{9,13},{10,... | collective-permute-start | bytes 393224 | tf_op jit(solution)/shard_map/ppermute | solution.py:106
  27.1 6.5 %collective-permute-start.3 = (f32[8,64,128]{2,1,0:T(8,128)S(1)}, f32[8,64,128]{2,1,0:T(8,128)S(1)}, u32[]{:S(2)}, u32[]{:S(2)}) collective-permute-start(f32[8,64,128]{2,1,0:T(8,128)S(1)} %pad_maximum_fusion.1), channel_id=1, source_target_pairs={{0,2},{1,3},{2,0},{3,1},{4,6},{5,7},{6,4},{7,5},{8,10},{9,11},{10,... | collective-permute-start | bytes 786440 | tf_op jit(solution)/shard_map/ppermute | solution.py:106
  33.6 40.5 %copy-start.1 = (f32[16,64,128]{2,1,0:T(8,128)}, f32[16,64,128]{2,1,0:T(8,128)S(1)}, u32[]{:S(2)}) copy-start(f32[16,64,128]{2,1,0:T(8,128)S(1)} %constant_dynamic-update-slice_fusion.near_ref) | copy-start | bytes 1572868
  33.6 6.0 %collective-permute-start.4 = (f32[16,64,128]{2,1,0:T(8,128)S(1)}, f32[16,64,128]{2,1,0:T(8,128)S(1)}, u32[]{:S(2)}, u32[]{:S(2)}) collective-permute-start(f32[16,64,128]{2,1,0:T(8,128)S(1)} %constant_dynamic-update-slice_fusion.near_ref), channel_id=1, source_target_pairs={{0,1},{1,0},{2,3},{3,2},{4,5},{5,4},{6,7},{7,6},{8,9},{9,8},{10,11... | collective-permute-start | bytes 1572872 | tf_op jit(solution)/shard_map/ppermute | solution.py:106
  39.6 35.5 %copy-start = (f32[16,64,128]{2,1,0:T(8,128)}, f32[16,64,128]{2,1,0:T(8,128)S(1)}, u32[]{:S(2)}) copy-start(f32[16,64,128]{2,1,0:T(8,128)S(1)} %collective-permute-done.4.far_ref) | copy-start | bytes 1572868
  41.8 25.4 %collective-permute-start.10 = (f32[2,8,64,64]{3,1,2,0:T(8,128)S(1)}, f32[2,8,64,64]{3,1,2,0:T(8,128)S(1)}, u32[]{:S(2)}, u32[]{:S(2)}) collective-permute-start(f32[2,8,64,64]{3,1,2,0:T(8,128)S(1)} %convolution_add_fusion), channel_id=1, source_target_pairs={{0,96},{1,97},{2,98},{3,99},{4,100},{5,101},{6,102},{7,103}} | collective-permute-start | bytes 786440 | tf_op jit(solution)/shard_map/ppermute | solution.py:172
  42.5 24.7 %collective-permute-start.9 = (f32[2,8,64,64]{3,1,2,0:T(8,128)S(1)}, f32[2,8,64,64]{3,1,2,0:T(8,128)S(1)}, u32[]{:S(2)}, u32[]{:S(2)}) collective-permute-start(f32[2,8,64,64]{3,1,2,0:T(8,128)S(1)} %convolution_add_fusion), channel_id=1, source_target_pairs={{0,64},{1,65},{2,66},{3,67},{4,68},{5,69},{6,70},{7,71},{40,104},{... | collective-permute-start | bytes 786440 | tf_op jit(solution)/shard_map/ppermute | solution.py:172
  43.2 27.8 %collective-permute-start.8 = (f32[2,8,64,64]{3,1,2,0:T(8,128)S(1)}, f32[2,8,64,64]{3,1,2,0:T(8,128)}, u32[]{:S(2)}, u32[]{:S(2)}) collective-permute-start(f32[2,8,64,64]{3,1,2,0:T(8,128)S(1)} %convolution_add_fusion), channel_id=1, source_target_pairs={{0,32},{1,33},{2,34},{3,35},{4,36},{5,37},{6,38},{7,39},{40,72},{4... | collective-permute-start | bytes 786440 | tf_op jit(solution)/shard_map/ppermute | solution.py:172

commit v6 on v5

--- a/solution.py
+++ b/solution.py
@@ -98,6 +98,44 @@
     )(table, place, near, far, stack, front)
 
 
+def inverse_kernel(system_ref, out_ref, work_ref):
+    order = out_ref.shape[1]
+    shape = system_ref.shape
+    lane = lax.broadcasted_iota(jnp.int32, shape, 2)
+    lane_row = lax.broadcasted_iota(jnp.int32, (shape[0], 1, shape[2]), 2)
+    row_at = lax.broadcasted_iota(jnp.int32, shape, 1)
+    work_ref[...] = system_ref[...]
+
+    def eliminate(k, carry):
+        work = work_ref[...]
+        row = work_ref[:, pl.ds(k, 1), :]
+        pivot = jnp.sum(jnp.where(lane_row == k, row, 0.0), axis=2, keepdims=True)
+        row = row / pivot
+        column = jnp.sum(jnp.where(lane == k, work, 0.0), axis=2, keepdims=True)
+        work_ref[...] = jnp.where(row_at == k, row, work - column * row)
+        return carry
+
+    lax.fori_loop(0, order, eliminate, 0)
+    out_ref[...] = work_ref[:, :, order:]
+
+
+def invert_spd(matrix):
+    order = matrix.shape[1]
+    symmetric = 0.5 * (matrix + jnp.swapaxes(matrix, 1, 2))
+    eye = jnp.broadcast_to(jnp.eye(order, dtype=jnp.float32), matrix.shape)
+    system = jnp.concatenate([symmetric, eye], axis=2)
+    return pl.pallas_call(
+        inverse_kernel,
+        out_shape=jax.ShapeDtypeStruct(matrix.shape, jnp.float32),
+        in_specs=[pl.BlockSpec(memory_space=pltpu.VMEM)],
+        out_specs=pl.BlockSpec(memory_space=pltpu.VMEM),
+        scratch_shapes=[pltpu.VMEM(system.shape, jnp.float32)],
+        cost_estimate=pl.CostEstimate(
+            flops=4 * system.size * order, bytes_accessed=system.size * 6,
+            transcendentals=0),
+    )(system)
+
+
 def doubling_gather(block, axis, count):
     bits = count.bit_length() - 1
     spread = [0]
@@ -161,12 +199,7 @@
         for part, held in enumerate((near, far))
     )
     window, whole_diag = lax.optimization_barrier((window, whole_diag))
-    lower_factor = jnp.linalg.cholesky(whole_diag)
-    eye = jnp.broadcast_to(jnp.eye(width, dtype=jnp.float32), whole_diag.shape)
-    inverse_factor = lax.linalg.triangular_solve(
-        lower_factor, eye, left_side=True, lower=True)
-    inverse = jnp.einsum("pca,pcb->pab", inverse_factor, inverse_factor,
-                         precision=HIGHEST)
+    inverse = invert_spd(whole_diag)
     owner = [(c * col_blocks) // row_blocks for c in range(col_count)]
     window = window + sum(
         lax.ppermute(window, ("prow", "pcol"), [

time: 87.3 us -> 87.2 us (level)
  other arithmetic: 29.3 us -> 7.46 us
  waiting for transfers between devices: 18.7 us -> 31.1 us
  Pallas kernels: 11.6 us -> 19.6 us
  local copies, waits for them, and re-layouts: 8.37 us -> 9.44 us
    another operation x7 -> x0, other arithmetic: 21.8 us -> none  [the longest x4 11.9 us: per_device(): lower_factor = jnp.linalg.cholesky(whole_diag)]
    ppermute x3, waiting for transfers between devices: 3.83 us -> 17.6 us  [per_device(): lax.ppermute(window, ('prow', 'pcol'), [(owner[c] * col_count + c, (owner...]
    pallas_call x0 -> x1, Pallas kernels: none -> 8.03 us  [invert_spd(): pl.pallas_call(inverse_kernel, out_shape=jax.ShapeDtypeStruct(matrix.shap...]
    ppermute x5, waiting for transfers between devices: 14.8 us -> 13.5 us  [doubling_gather(): other = lax.ppermute(block, axis, [(i, i ^ mask) for i in range(count)])]
    broadcast_in_dim x8 -> x16, local copies, waits for them, and re-layouts: 0.64 us -> 1.71 us  [per_device(): jnp.where((order == k)[None, :, None, None], piece[:, None], 0.0)]
  transfers between devices with their start and end apart: 11 -> 11, of which waited for: 4 -> 4; matrix products, arithmetic and copies ran while one was open for 41% -> 16% of each run, Pallas kernels for 0% -> 9%
where the time goes in v6:
time: 87.2 us; the launch traced here: 86.5 us
  waiting for transfers between devices  31.1 us (36%)
  Pallas kernels  19.6 us (22%)
  starting transfers between devices  14.5 us (17%)
  local copies, waits for them, and re-layouts  9.44 us (11%)
  other arithmetic  7.46 us (9%)
  matrix products  4.01 us (5%)
    ppermute x3, waiting for transfers between devices, per_device(): lax.ppermute(window, ('prow', 'pcol'), [(owner[c] * col_count + c, (owner...  17.6 us
    ppermute x5, waiting for transfers between devices, doubling_gather(): other = lax.ppermute(block, axis, [(i, i ^ mask) for i in range(count)])  13.5 us
    pallas_call x1, Pallas kernels, apply_update(): pl.pallas_call(kernel, out_shape=jax.ShapeDtypeStruct(front.shape, front....  11.6 us
    pallas_call x1, Pallas kernels, invert_spd(): pl.pallas_call(inverse_kernel, out_shape=jax.ShapeDtypeStruct(matrix.shap...  8.03 us
    ppermute x5, starting transfers between devices, doubling_gather(): other = lax.ppermute(block, axis, [(i, i ^ mask) for i in range(count)])  7.48 us
    ppermute x3, starting transfers between devices, per_device(): lax.ppermute(diag_blocks, 'prow', [(i, (i + k) % row_count) for i in rang...  4.32 us
    ppermute x3, starting transfers between devices, per_device(): lax.ppermute(window, ('prow', 'pcol'), [(owner[c] * col_count + c, (owner...  2.68 us
    dot_general x1, matrix products, per_device(): right = jnp.einsum('pxa,pjba->pxjb', inverse, window, precision=HIGHEST)  2.47 us
  transfers between devices with their start and end apart: 11, of which 4 were waited for; matrix products, arithmetic and copies ran while one was open for 16% of the time, Pallas kernels for 9%

profile of v6, /device:TPU:14, one launch (start us, length us, event | category | flops | bytes accessed | tf_op | source)
XLA Modules:
  0.0 86.5 jit_solution(9879466865447497619)
XLA Ops:
  0.0 1.6 %collective-permute-start.5 = (f32[2,16,64]{2,1,0:T(8,128)}, f32[2,16,64]{2,1,0:T(8,128)S(1)}, u32[]{:S(2)}, u32[]{:S(2)}) collective-permute-start(f32[2,16,64]{2,1,0:T(8,128)} %param.6), channel_id=1, source_target_pairs={{0,32},{32,64},{64,96},{96,0},{1,33},{33,65},{65,97},{97,1},{2,34}... | collective-permute-start | bytes 24584 | tf_op jit(solution)/shard_map/ppermute | solution.py:175
  2.0 2.3 %collective-permute-start.6 = (f32[2,16,64]{2,1,0:T(8,128)}, f32[2,16,64]{2,1,0:T(8,128)S(1)}, u32[]{:S(2)}, u32[]{:S(2)}) collective-permute-start(f32[2,16,64]{2,1,0:T(8,128)} %param.6), channel_id=1, source_target_pairs={{0,64},{32,96},{64,0},{96,32},{1,65},{33,97},{65,1},{97,33},{2,66}... | collective-permute-start | bytes 24584 | tf_op jit(solution)/shard_map/ppermute | solution.py:175
  4.3 0.9 %copy.53 = f32[1,64,128]{2,1,0:T(8,128)S(1)} copy(f32[1,64,128]{1,2,0:T(8,128)} %bitcast.41) | data formatting | bytes 65536 | tf_op jit(solution)/shard_map/broadcast_in_dim;reshape | solution.py:168
  5.2 4.0 %collective-permute-start = (f32[1,64,128]{2,1,0:T(8,128)S(1)}, f32[1,64,128]{2,1,0:T(8,128)S(1)}, u32[]{:S(2)}, u32[]{:S(2)}) collective-permute-start(f32[1,64,128]{2,1,0:T(8,128)S(1)} %copy.53), channel_id=1, source_target_pairs={{0,16},{1,17},{2,18},{3,19},{4,20},{5,21},{6,22},{7,23},{8,24},{9,... | collective-permute-start | bytes 98312 | tf_op jit(solution)/shard_map/ppermute | solution.py:144
  9.2 0.8 constant_dynamic-slice_fusion
  10.2 0.8 compare_reduce_fusion
  11.1 0.7 iota_reduce_fusion
  11.8 0.7 broadcast_xor_fusion
  12.5 1.4 %gather_fusion = s32[32]{0:T(128)S(1)} fusion(s32[32]{0:T(128)} %constant.101.clone, s32[1024]{0:T(1024)S(1)} %get-tuple-element.24), kind=kCustom, calls=%fused_computation | custom fusion | bytes 384 | tf_op jit(solution)/shard_map/jit(_take)/gather | solution.py:172
  14.0 1.1 %collective-permute-start.1 = (f32[2,64,128]{2,1,0:T(8,128)S(1)}, f32[2,64,128]{2,1,0:T(8,128)S(1)}, u32[]{:S(2)}, u32[]{:S(2)}) collective-permute-start(f32[2,64,128]{2,1,0:T(8,128)S(1)} %pad_maximum_fusion.3), channel_id=1, source_target_pairs={{0,8},{1,9},{2,10},{3,11},{4,12},{5,13},{6,14},{7,15},{8,0},{9,1},... | collective-permute-start | bytes 196616 | tf_op jit(solution)/shard_map/ppermute | solution.py:144
  15.1 3.2 %collective-permute-done.1 = f32[2,64,128]{2,1,0:T(8,128)S(1)} collective-permute-done((f32[2,64,128]{2,1,0:T(8,128)S(1)}, f32[2,64,128]{2,1,0:T(8,128)S(1)}, u32[]{:S(2)}, u32[]{:S(2)}) %collective-permute-start.1) | collective-permute-done | bytes 65568 | tf_op jit(solution)/shard_map/ppermute | solution.py:144
  18.4 1.5 %collective-permute-start.2 = (f32[4,64,128]{2,1,0:T(8,128)S(1)}, f32[4,64,128]{2,1,0:T(8,128)S(1)}, u32[]{:S(2)}, u32[]{:S(2)}) collective-permute-start(f32[4,64,128]{2,1,0:T(8,128)S(1)} %pad_maximum_fusion.2), channel_id=1, source_target_pairs={{0,4},{1,5},{2,6},{3,7},{4,0},{5,1},{6,2},{7,3},{8,12},{9,13},{10,... | collective-permute-start | bytes 393224 | tf_op jit(solution)/shard_map/ppermute | solution.py:144
  19.9 1.2 %gather_fusion.1 = s32[128]{0:T(128)S(1)} fusion(s32[32]{0:T(128)S(1)} %and_select_fusion.1, s32[1024]{0:T(1024)S(1)} %get-tuple-element.23), kind=kCustom, calls=%fused_computation.1 | custom fusion | bytes 1536 | tf_op jit(solution)/shard_map/jit(_take)/gather | solution.py:187
  21.2 4.7 %collective-permute-done.2 = f32[4,64,128]{2,1,0:T(8,128)S(1)} collective-permute-done((f32[4,64,128]{2,1,0:T(8,128)S(1)}, f32[4,64,128]{2,1,0:T(8,128)S(1)}, u32[]{:S(2)}, u32[]{:S(2)}) %collective-permute-start.2) | collective-permute-done | bytes 131104 | tf_op jit(solution)/shard_map/ppermute | solution.py:144
  25.9 0.9 collective-permute-start.3
  26.8 5.6 %collective-permute-done.3 = f32[8,64,128]{2,1,0:T(8,128)S(1)} collective-permute-done((f32[8,64,128]{2,1,0:T(8,128)S(1)}, f32[8,64,128]{2,1,0:T(8,128)S(1)}, u32[]{:S(2)}, u32[]{:S(2)}) %collective-permute-start.3) | collective-permute-done | bytes 262176 | tf_op jit(solution)/shard_map/ppermute | solution.py:144
  32.5 0.7 compare_select_fusion.5.table_ref
  33.2 0.7 pad_add_fusion.place_ref
  33.8 0.9 %copy.35 = f32[2,64,64]{1,2,0:T(8,128)S(1)} copy(f32[2,64,64]{2,1,0:T(8,128)} %param.7) | data formatting | bytes 65536 | tf_op args[1]
  35.4 0.7 broadcast_in_dim.126
  38.6 0.6 reshape.86
  39.3 1.1 %fusion = f32[2,8,64,64]{3,1,2,0:T(8,128)S(1)} fusion(f32[16,64,2,64]{3,2,1,0:T(2,128)S(1)} %reshape.86, pred[2,8,32]{2,1,0:T(8,128)(4,1)S(1)} %compare_and_fusion), kind=kOutput, calls=%fused_computation.3 | convolution fusion | flops 12582912 | bytes 786944 | tf_op jit(solution)/shard_map/pjk,kbpa->pjba/dot_general | solution.py:197
  40.8 0.7 collective-permute-start.10
  41.5 0.7 collective-permute-start.9
  42.2 1.3 %collective-permute-start.8 = (f32[2,8,64,64]{3,1,2,0:T(8,128)S(1)}, f32[2,8,64,64]{3,1,2,0:T(8,128)}, u32[]{:S(2)}, u32[]{:S(2)}) collective-permute-start(f32[2,8,64,64]{3,1,2,0:T(8,128)S(1)} %convolution_add_fusion), channel_id=1, source_target_pairs={{0,32},{1,33},{2,34},{3,35},{4,36},{5,37},{6,38},{7,39},{40,72},{4... | collective-permute-start | bytes 786440 | tf_op jit(solution)/shard_map/ppermute | solution.py:205
  43.6 0.7 pad_maximum_fusion.4.system_ref
  44.4 8.0 %shard_map.64 = f32[2,64,64]{2,1,0:T(8,128)} custom-call(f32[2,64,128]{2,1,0:T(8,128)} %pad_maximum_fusion.4.system_ref), custom_call_target="tpu_custom_call" | custom-call | flops 4194304 | bytes 98304 | tf_op jit(solution)/shard_map/pallas_call | solution.py:127
  52.4 17.6 %collective-permute-done.8 = f32[2,8,64,64]{3,1,2,0:T(8,128)} collective-permute-done((f32[2,8,64,64]{3,1,2,0:T(8,128)S(1)}, f32[2,8,64,64]{3,1,2,0:T(8,128)}, u32[]{:S(2)}, u32[]{:S(2)}) %collective-permute-start.8) | collective-permute-done | bytes 262176 | tf_op jit(solution)/shard_map/ppermute | solution.py:205
  70.0 1.1 %add_add_fusion = f32[2,8,64,64]{3,1,2,0:T(8,128)S(1)} fusion(f32[2,8,64,64]{3,1,2,0:T(8,128)S(1)} %convolution_add_fusion, f32[2,8,64,64]{3,1,2,0:T(8,128)S(1)} %collective-permute-done.10, f32[2,8,64,64]{3,1,2,0:T(8,128)} %collective-permute-done.8, f32[2,8,64,64]{3,1,2,0:T(8,128)S(1)} %collective-permute-done.9), kind=kLoop, calls=%fused_computation.7 | loop fusion | flops 196608 | bytes 1310720 | tf_op jit(solution)/shard_map/add | solution.py:204
  71.2 2.5 %fusion.2 = f32[2,64,8,64]{3,1,2,0:T(8,128)S(1)} fusion(f32[2,8,64,64]{3,1,2,0:T(8,128)S(1)} %add_add_fusion, f32[2,64,64]{2,1,0:T(8,128)} %shard_map.64), kind=kOutput, calls=%fused_computation.5 | convolution fusion | flops 50331648 | bytes 557056 | tf_op jit(solution)/shard_map/pxa,pjba->pxjb/dot_general | solution.py:211
  74.2 0.8 pad_maximum_fusion.stack_ref
  74.9 11.6 %shard_map.65 = f32[4096,512]{1,0:T(8,128)} custom-call(s32[2,64]{1,0:T(2,128)} %compare_select_fusion.5.table_ref, s32[2]{0:T(128)} %pad_add_fusion.place_ref, f32[16,64,128]{2,1,0:T(8,128)} %copy-done.1, f32[16,64,128]{2,1,0:T(8,128)} %copy-done, bf16[384,512]{1,0:T(8,128)(2,1)} %pad_maximum_fusion.stack_ref, f32[4096,512]{1,0:T(8,128)} %front_ref.1), custom_call_target="tpu_custom_call" | custom-call | flops 1610612736 | bytes 18219008 | tf_op jit(solution)/shard_map/pallas_call | solution.py:78
  (67 shorter events, 5.3 us)
Async XLA Ops:
  0.0 36.4 %collective-permute-start.5 = (f32[2,16,64]{2,1,0:T(8,128)}, f32[2,16,64]{2,1,0:T(8,128)S(1)}, u32[]{:S(2)}, u32[]{:S(2)}) collective-permute-start(f32[2,16,64]{2,1,0:T(8,128)} %param.6), channel_id=1, source_target_pairs={{0,32},{32,64},{64,96},{96,0},{1,33},{33,65},{65,97},{97,1},{2,34}... | collective-permute-start | bytes 24584 | tf_op jit(solution)/shard_map/ppermute | solution.py:175
  1.6 34.7 %collective-permute-start.7 = (f32[2,16,64]{2,1,0:T(8,128)}, f32[2,16,64]{2,1,0:T(8,128)S(1)}, u32[]{:S(2)}, u32[]{:S(2)}) collective-permute-start(f32[2,16,64]{2,1,0:T(8,128)} %param.6), channel_id=1, source_target_pairs={{0,96},{32,0},{64,32},{96,64},{1,97},{33,1},{65,33},{97,65},{2,98}... | collective-permute-start | bytes 24584 | tf_op jit(solution)/shard_map/ppermute | solution.py:175
  2.0 34.2 %collective-permute-start.6 = (f32[2,16,64]{2,1,0:T(8,128)}, f32[2,16,64]{2,1,0:T(8,128)S(1)}, u32[]{:S(2)}, u32[]{:S(2)}) collective-permute-start(f32[2,16,64]{2,1,0:T(8,128)} %param.6), channel_id=1, source_target_pairs={{0,64},{32,96},{64,0},{96,32},{1,65},{33,97},{65,1},{97,33},{2,66}... | collective-permute-start | bytes 24584 | tf_op jit(solution)/shard_map/ppermute | solution.py:175
  5.2 8.8 %collective-permute-start = (f32[1,64,128]{2,1,0:T(8,128)S(1)}, f32[1,64,128]{2,1,0:T(8,128)S(1)}, u32[]{:S(2)}, u32[]{:S(2)}) collective-permute-start(f32[1,64,128]{2,1,0:T(8,128)S(1)} %copy.53), channel_id=1, source_target_pairs={{0,16},{1,17},{2,18},{3,19},{4,20},{5,21},{6,22},{7,23},{8,24},{9,... | collective-permute-start | bytes 98312 | tf_op jit(solution)/shard_map/ppermute | solution.py:144
  14.0 4.3 %collective-permute-start.1 = (f32[2,64,128]{2,1,0:T(8,128)S(1)}, f32[2,64,128]{2,1,0:T(8,128)S(1)}, u32[]{:S(2)}, u32[]{:S(2)}) collective-permute-start(f32[2,64,128]{2,1,0:T(8,128)S(1)} %pad_maximum_fusion.3), channel_id=1, source_target_pairs={{0,8},{1,9},{2,10},{3,11},{4,12},{5,13},{6,14},{7,15},{8,0},{9,1},... | collective-permute-start | bytes 196616 | tf_op jit(solution)/shard_map/ppermute | solution.py:144
  18.4 7.5 %collective-permute-start.2 = (f32[4,64,128]{2,1,0:T(8,128)S(1)}, f32[4,64,128]{2,1,0:T(8,128)S(1)}, u32[]{:S(2)}, u32[]{:S(2)}) collective-permute-start(f32[4,64,128]{2,1,0:T(8,128)S(1)} %pad_maximum_fusion.2), channel_id=1, source_target_pairs={{0,4},{1,5},{2,6},{3,7},{4,0},{5,1},{6,2},{7,3},{8,12},{9,13},{10,... | collective-permute-start | bytes 393224 | tf_op jit(solution)/shard_map/ppermute | solution.py:144
  25.9 6.5 %collective-permute-start.3 = (f32[8,64,128]{2,1,0:T(8,128)S(1)}, f32[8,64,128]{2,1,0:T(8,128)S(1)}, u32[]{:S(2)}, u32[]{:S(2)}) collective-permute-start(f32[8,64,128]{2,1,0:T(8,128)S(1)} %pad_maximum_fusion.1), channel_id=1, source_target_pairs={{0,2},{1,3},{2,0},{3,1},{4,6},{5,7},{6,4},{7,5},{8,10},{9,11},{10,... | collective-permute-start | bytes 786440 | tf_op jit(solution)/shard_map/ppermute | solution.py:144
  32.4 41.6 %copy-start.1 = (f32[16,64,128]{2,1,0:T(8,128)}, f32[16,64,128]{2,1,0:T(8,128)S(1)}, u32[]{:S(2)}) copy-start(f32[16,64,128]{2,1,0:T(8,128)S(1)} %constant_dynamic-update-slice_fusion.near_ref) | copy-start | bytes 1572868
  32.4 6.2 %collective-permute-start.4 = (f32[16,64,128]{2,1,0:T(8,128)S(1)}, f32[16,64,128]{2,1,0:T(8,128)S(1)}, u32[]{:S(2)}, u32[]{:S(2)}) collective-permute-start(f32[16,64,128]{2,1,0:T(8,128)S(1)} %constant_dynamic-update-slice_fusion.near_ref), channel_id=1, source_target_pairs={{0,1},{1,0},{2,3},{3,2},{4,5},{5,4},{6,7},{7,6},{8,9},{9,8},{10,11... | collective-permute-start | bytes 1572872 | tf_op jit(solution)/shard_map/ppermute | solution.py:144
  38.6 36.3 %copy-start = (f32[16,64,128]{2,1,0:T(8,128)}, f32[16,64,128]{2,1,0:T(8,128)S(1)}, u32[]{:S(2)}) copy-start(f32[16,64,128]{2,1,0:T(8,128)S(1)} %collective-permute-done.4.far_ref) | copy-start | bytes 1572868
  40.8 11.6 %collective-permute-start.10 = (f32[2,8,64,64]{3,1,2,0:T(8,128)S(1)}, f32[2,8,64,64]{3,1,2,0:T(8,128)S(1)}, u32[]{:S(2)}, u32[]{:S(2)}) collective-permute-start(f32[2,8,64,64]{3,1,2,0:T(8,128)S(1)} %convolution_add_fusion), channel_id=1, source_target_pairs={{0,96},{1,97},{2,98},{3,99},{4,100},{5,101},{6,102},{7,103}} | collective-permute-start | bytes 786440 | tf_op jit(solution)/shard_map/ppermute | solution.py:205
  41.5 10.9 %collective-permute-start.9 = (f32[2,8,64,64]{3,1,2,0:T(8,128)S(1)}, f32[2,8,64,64]{3,1,2,0:T(8,128)S(1)}, u32[]{:S(2)}, u32[]{:S(2)}) collective-permute-start(f32[2,8,64,64]{3,1,2,0:T(8,128)S(1)} %convolution_add_fusion), channel_id=1, source_target_pairs={{0,64},{1,65},{2,66},{3,67},{4,68},{5,69},{6,70},{7,71},{40,104},{... | collective-permute-start | bytes 786440 | tf_op jit(solution)/shard_map/ppermute | solution.py:205
  42.2 27.8 %collective-permute-start.8 = (f32[2,8,64,64]{3,1,2,0:T(8,128)S(1)}, f32[2,8,64,64]{3,1,2,0:T(8,128)}, u32[]{:S(2)}, u32[]{:S(2)}) collective-permute-start(f32[2,8,64,64]{3,1,2,0:T(8,128)S(1)} %convolution_add_fusion), channel_id=1, source_target_pairs={{0,32},{1,33},{2,34},{3,35},{4,36},{5,37},{6,38},{7,39},{40,72},{4... | collective-permute-start | bytes 786440 | tf_op jit(solution)/shard_map/ppermute | solution.py:205

commit v7 on v6

--- a/solution.py
+++ b/solution.py
@@ -181,11 +181,6 @@
         for k, piece in enumerate(pieces)
     ).reshape(diag_blocks.shape[0], -1, diag_blocks.shape[2])
 
-    own_map = lax.dynamic_slice_in_dim(child_map, row_index * col_count, col_count, 1)
-    table = first_match(own_map - row_index * row_blocks,
-                        jnp.arange(row_blocks, dtype=jnp.int32))
-    table = jnp.where(table >= 0, jnp.take(slot_of, jnp.maximum(table, 0)), -1)
-
     first_col = col_index * col_blocks
     source = first_col // row_blocks
     source_map = lax.dynamic_slice_in_dim(child_map, source * col_count, col_count, 1)
@@ -198,8 +193,13 @@
                    held.reshape(half, width, 2, width), precision=HIGHEST)
         for part, held in enumerate((near, far))
     )
-    window, whole_diag = lax.optimization_barrier((window, whole_diag))
+    window, whole_diag, child_map = lax.optimization_barrier((window, whole_diag, child_map))
     inverse = invert_spd(whole_diag)
+    own_map = lax.dynamic_slice_in_dim(child_map, row_index * col_count, col_count, 1)
+    table = first_match(own_map - row_index * row_blocks,
+                        jnp.arange(row_blocks, dtype=jnp.int32))
+    table = jnp.where(table >= 0, jnp.take(slot_of, jnp.maximum(table, 0)), -1)
+
     owner = [(c * col_blocks) // row_blocks for c in range(col_count)]
     window = window + sum(
         lax.ppermute(window, ("prow", "pcol"), [

time: 87.2 us -> 85.1 us (0.976)
  waiting for transfers between devices: 31.1 us -> 29.1 us
    ppermute x3, waiting for transfers between devices: 17.6 us -> 15.7 us  [per_device(): lax.ppermute(window, ('prow', 'pcol'), [(owner[c] * col_count + c, (owner...]
  transfers between devices with their start and end apart: 11 -> 11, of which waited for: 4 -> 4; matrix products, arithmetic and copies ran while one was open for 16% -> 15% of each run, Pallas kernels for 9% -> 10%
where the time goes in v7:
time: 85.1 us; the launch traced here: 84.5 us
  waiting for transfers between devices  29.1 us (34%)
  Pallas kernels  19.6 us (23%)
  starting transfers between devices  14.5 us (17%)
  local copies, waits for them, and re-layouts  10.2 us (12%)
  other arithmetic  6.62 us (8%)
  matrix products  4.01 us (5%)
    ppermute x3, waiting for transfers between devices, per_device(): lax.ppermute(window, ('prow', 'pcol'), [(owner[c] * col_count + c, (owner...  15.7 us
    ppermute x5, waiting for transfers between devices, doubling_gather(): other = lax.ppermute(block, axis, [(i, i ^ mask) for i in range(count)])  13.5 us
    pallas_call x1, Pallas kernels, apply_update(): pl.pallas_call(kernel, out_shape=jax.ShapeDtypeStruct(front.shape, front....  11.6 us
    pallas_call x1, Pallas kernels, invert_spd(): pl.pallas_call(inverse_kernel, out_shape=jax.ShapeDtypeStruct(matrix.shap...  8.03 us
    ppermute x5, starting transfers between devices, doubling_gather(): other = lax.ppermute(block, axis, [(i, i ^ mask) for i in range(count)])  7.48 us
    ppermute x3, starting transfers between devices, per_device(): lax.ppermute(diag_blocks, 'prow', [(i, (i + k) % row_count) for i in rang...  4.32 us
    ppermute x3, starting transfers between devices, per_device(): lax.ppermute(window, ('prow', 'pcol'), [(owner[c] * col_count + c, (owner...  2.67 us
    dot_general x1, matrix products, per_device(): right = jnp.einsum('pxa,pjba->pxjb', inverse, window, precision=HIGHEST)  2.47 us
  transfers between devices with their start and end apart: 11, of which 4 were waited for; matrix products, arithmetic and copies ran while one was open for 15% of the time, Pallas kernels for 10%

profile of v7, /device:TPU:14, one launch (start us, length us, event | category | flops | bytes accessed | tf_op | source)
XLA Modules:
  0.0 84.5 jit_solution(1582382457752697281)
XLA Ops:
  0.0 1.6 %collective-permute-start.5 = (f32[2,16,64]{2,1,0:T(8,128)}, f32[2,16,64]{2,1,0:T(8,128)S(1)}, u32[]{:S(2)}, u32[]{:S(2)}) collective-permute-start(f32[2,16,64]{2,1,0:T(8,128)} %param.6), channel_id=1, source_target_pairs={{0,32},{32,64},{64,96},{96,0},{1,33},{33,65},{65,97},{97,1},{2,34}... | collective-permute-start | bytes 24584 | tf_op jit(solution)/shard_map/ppermute | solution.py:175
  2.0 2.3 %collective-permute-start.6 = (f32[2,16,64]{2,1,0:T(8,128)}, f32[2,16,64]{2,1,0:T(8,128)S(1)}, u32[]{:S(2)}, u32[]{:S(2)}) collective-permute-start(f32[2,16,64]{2,1,0:T(8,128)} %param.6), channel_id=1, source_target_pairs={{0,64},{32,96},{64,0},{96,32},{1,65},{33,97},{65,1},{97,33},{2,66}... | collective-permute-start | bytes 24584 | tf_op jit(solution)/shard_map/ppermute | solution.py:175
  4.3 0.9 %copy.53 = f32[1,64,128]{2,1,0:T(8,128)S(1)} copy(f32[1,64,128]{1,2,0:T(8,128)} %bitcast.41) | data formatting | bytes 65536 | tf_op jit(solution)/shard_map/broadcast_in_dim;reshape | solution.py:168
  5.2 4.0 %collective-permute-start = (f32[1,64,128]{2,1,0:T(8,128)S(1)}, f32[1,64,128]{2,1,0:T(8,128)S(1)}, u32[]{:S(2)}, u32[]{:S(2)}) collective-permute-start(f32[1,64,128]{2,1,0:T(8,128)S(1)} %copy.53), channel_id=1, source_target_pairs={{0,16},{1,17},{2,18},{3,19},{4,20},{5,21},{6,22},{7,23},{8,24},{9,... | collective-permute-start | bytes 98312 | tf_op jit(solution)/shard_map/ppermute | solution.py:144
  9.2 0.7 constant_dynamic-slice_fusion
  10.1 0.8 compare_reduce_fusion
  10.9 0.7 broadcast_xor_fusion
  11.7 1.1 %collective-permute-start.1 = (f32[2,64,128]{2,1,0:T(8,128)S(1)}, f32[2,64,128]{2,1,0:T(8,128)S(1)}, u32[]{:S(2)}, u32[]{:S(2)}) collective-permute-start(f32[2,64,128]{2,1,0:T(8,128)S(1)} %pad_maximum_fusion.3), channel_id=1, source_target_pairs={{0,8},{1,9},{2,10},{3,11},{4,12},{5,13},{6,14},{7,15},{8,0},{9,1},... | collective-permute-start | bytes 196616 | tf_op jit(solution)/shard_map/ppermute | solution.py:144
  12.8 3.2 %collective-permute-done.1 = f32[2,64,128]{2,1,0:T(8,128)S(1)} collective-permute-done((f32[2,64,128]{2,1,0:T(8,128)S(1)}, f32[2,64,128]{2,1,0:T(8,128)S(1)}, u32[]{:S(2)}, u32[]{:S(2)}) %collective-permute-start.1) | collective-permute-done | bytes 65568 | tf_op jit(solution)/shard_map/ppermute | solution.py:144
  16.1 1.5 %collective-permute-start.2 = (f32[4,64,128]{2,1,0:T(8,128)S(1)}, f32[4,64,128]{2,1,0:T(8,128)S(1)}, u32[]{:S(2)}, u32[]{:S(2)}) collective-permute-start(f32[4,64,128]{2,1,0:T(8,128)S(1)} %pad_maximum_fusion.2), channel_id=1, source_target_pairs={{0,4},{1,5},{2,6},{3,7},{4,0},{5,1},{6,2},{7,3},{8,12},{9,13},{10,... | collective-permute-start | bytes 393224 | tf_op jit(solution)/shard_map/ppermute | solution.py:144
  17.6 1.4 %gather_fusion = s32[32]{0:T(128)S(1)} fusion(s32[32]{0:T(128)} %constant.101.clone, s32[1024]{0:T(1024)S(1)} %pad_clamp_fusion.1), kind=kCustom, calls=%fused_computation | custom fusion | bytes 384 | tf_op jit(solution)/shard_map/jit(_take)/gather | solution.py:172
  18.9 4.7 %collective-permute-done.2 = f32[4,64,128]{2,1,0:T(8,128)S(1)} collective-permute-done((f32[4,64,128]{2,1,0:T(8,128)S(1)}, f32[4,64,128]{2,1,0:T(8,128)S(1)}, u32[]{:S(2)}, u32[]{:S(2)}) %collective-permute-start.2) | collective-permute-done | bytes 131104 | tf_op jit(solution)/shard_map/ppermute | solution.py:144
  23.6 0.9 %collective-permute-start.3 = (f32[8,64,128]{2,1,0:T(8,128)S(1)}, f32[8,64,128]{2,1,0:T(8,128)S(1)}, u32[]{:S(2)}, u32[]{:S(2)}) collective-permute-start(f32[8,64,128]{2,1,0:T(8,128)S(1)} %pad_maximum_fusion.1), channel_id=1, source_target_pairs={{0,2},{1,3},{2,0},{3,1},{4,6},{5,7},{6,4},{7,5},{8,10},{9,11},{10,... | collective-permute-start | bytes 786440 | tf_op jit(solution)/shard_map/ppermute | solution.py:144
  24.5 5.6 %collective-permute-done.3 = f32[8,64,128]{2,1,0:T(8,128)S(1)} collective-permute-done((f32[8,64,128]{2,1,0:T(8,128)S(1)}, f32[8,64,128]{2,1,0:T(8,128)S(1)}, u32[]{:S(2)}, u32[]{:S(2)}) %collective-permute-start.3) | collective-permute-done | bytes 262176 | tf_op jit(solution)/shard_map/ppermute | solution.py:144
  30.2 0.7 pad_add_fusion.place_ref
  30.9 0.9 %copy.35 = f32[2,64,64]{1,2,0:T(8,128)S(1)} copy(f32[2,64,64]{2,1,0:T(8,128)} %param.7) | data formatting | bytes 65536 | tf_op args[1]
  32.5 0.7 broadcast_in_dim.122
  35.1 0.6 concatenate.42
  35.7 0.6 reshape.86
  36.3 1.1 %fusion = f32[2,8,64,64]{3,1,2,0:T(8,128)S(1)} fusion(f32[16,64,2,64]{3,2,1,0:T(2,128)S(1)} %reshape.86, pred[2,8,32]{2,1,0:T(8,128)(4,1)S(1)} %compare_and_fusion), kind=kOutput, calls=%fused_computation.3 | convolution fusion | flops 12582912 | bytes 786944 | tf_op jit(solution)/shard_map/pjk,kbpa->pjba/dot_general | solution.py:192
  38.1 0.6 iota_reduce_fusion
  38.7 0.7 collective-permute-start.10
  39.4 0.7 collective-permute-start.9
  40.1 1.3 %collective-permute-start.8 = (f32[2,8,64,64]{3,1,2,0:T(8,128)S(1)}, f32[2,8,64,64]{3,1,2,0:T(8,128)}, u32[]{:S(2)}, u32[]{:S(2)}) collective-permute-start(f32[2,8,64,64]{3,1,2,0:T(8,128)S(1)} %convolution_add_fusion), channel_id=1, source_target_pairs={{0,32},{1,33},{2,34},{3,35},{4,36},{5,37},{6,38},{7,39},{40,72},{4... | collective-permute-start | bytes 786440 | tf_op jit(solution)/shard_map/ppermute | solution.py:205
  41.6 0.7 pad_maximum_fusion.4.system_ref
  42.3 1.2 %gather_fusion.1 = s32[128]{0:T(128)S(1)} fusion(s32[32]{0:T(128)S(1)} %and_select_fusion, s32[1024]{0:T(1024)S(1)} %pad_clamp_fusion), kind=kCustom, calls=%fused_computation.1 | custom fusion | bytes 1536 | tf_op jit(solution)/shard_map/jit(_take)/gather | solution.py:201
  43.6 8.0 %shard_map.64 = f32[2,64,64]{2,1,0:T(8,128)} custom-call(f32[2,64,128]{2,1,0:T(8,128)} %pad_maximum_fusion.4.system_ref), custom_call_target="tpu_custom_call" | custom-call | flops 4194304 | bytes 98304 | tf_op jit(solution)/shard_map/pallas_call | solution.py:127
  52.2 15.7 %collective-permute-done.8 = f32[2,8,64,64]{3,1,2,0:T(8,128)} collective-permute-done((f32[2,8,64,64]{3,1,2,0:T(8,128)S(1)}, f32[2,8,64,64]{3,1,2,0:T(8,128)}, u32[]{:S(2)}, u32[]{:S(2)}) %collective-permute-start.8) | collective-permute-done | bytes 262176 | tf_op jit(solution)/shard_map/ppermute | solution.py:205
  67.9 1.2 %add_add_fusion = f32[2,8,64,64]{3,1,2,0:T(8,128)S(1)} fusion(f32[2,8,64,64]{3,1,2,0:T(8,128)S(1)} %convolution_add_fusion, f32[2,8,64,64]{3,1,2,0:T(8,128)S(1)} %collective-permute-done.10, f32[2,8,64,64]{3,1,2,0:T(8,128)} %collective-permute-done.8, f32[2,8,64,64]{3,1,2,0:T(8,128)S(1)} %collective-permute-done.9), kind=kLoop, calls=%fused_computation.7 | loop fusion | flops 196608 | bytes 1310720 | tf_op jit(solution)/shard_map/add | solution.py:204
  69.1 2.5 %fusion.2 = f32[2,64,8,64]{3,1,2,0:T(8,128)S(1)} fusion(f32[2,8,64,64]{3,1,2,0:T(8,128)S(1)} %add_add_fusion, f32[2,64,64]{2,1,0:T(8,128)} %shard_map.64), kind=kOutput, calls=%fused_computation.5 | convolution fusion | flops 50331648 | bytes 557056 | tf_op jit(solution)/shard_map/pxa,pjba->pxjb/dot_general | solution.py:211
  72.1 0.8 pad_maximum_fusion.stack_ref
  72.9 11.6 %shard_map.65 = f32[4096,512]{1,0:T(8,128)} custom-call(s32[2,64]{1,0:T(2,128)} %compare_select_fusion.5.table_ref, s32[2]{0:T(128)} %pad_add_fusion.place_ref, f32[16,64,128]{2,1,0:T(8,128)} %copy-done.1, f32[16,64,128]{2,1,0:T(8,128)} %copy-done, bf16[384,512]{1,0:T(8,128)(2,1)} %pad_maximum_fusion.stack_ref, f32[4096,512]{1,0:T(8,128)} %front_ref.1), custom_call_target="tpu_custom_call" | custom-call | flops 1610612736 | bytes 18219008 | tf_op jit(solution)/shard_map/pallas_call | solution.py:78
  (71 shorter events, 5.4 us)
Async XLA Ops:
  0.0 37.9 %copy-start.2 = (s32[2,128]{1,0:T(2,128)S(1)}, s32[2,128]{1,0:T(2,128)}, u32[]{:S(2)}) copy-start(s32[2,128]{1,0:T(2,128)} %param.8) | copy-start | bytes 3076
  0.0 33.5 %collective-permute-start.5 = (f32[2,16,64]{2,1,0:T(8,128)}, f32[2,16,64]{2,1,0:T(8,128)S(1)}, u32[]{:S(2)}, u32[]{:S(2)}) collective-permute-start(f32[2,16,64]{2,1,0:T(8,128)} %param.6), channel_id=1, source_target_pairs={{0,32},{32,64},{64,96},{96,0},{1,33},{33,65},{65,97},{97,1},{2,34}... | collective-permute-start | bytes 24584 | tf_op jit(solution)/shard_map/ppermute | solution.py:175
  1.6 31.8 %collective-permute-start.7 = (f32[2,16,64]{2,1,0:T(8,128)}, f32[2,16,64]{2,1,0:T(8,128)S(1)}, u32[]{:S(2)}, u32[]{:S(2)}) collective-permute-start(f32[2,16,64]{2,1,0:T(8,128)} %param.6), channel_id=1, source_target_pairs={{0,96},{32,0},{64,32},{96,64},{1,97},{33,1},{65,33},{97,65},{2,98}... | collective-permute-start | bytes 24584 | tf_op jit(solution)/shard_map/ppermute | solution.py:175
  2.0 31.2 %collective-permute-start.6 = (f32[2,16,64]{2,1,0:T(8,128)}, f32[2,16,64]{2,1,0:T(8,128)S(1)}, u32[]{:S(2)}, u32[]{:S(2)}) collective-permute-start(f32[2,16,64]{2,1,0:T(8,128)} %param.6), channel_id=1, source_target_pairs={{0,64},{32,96},{64,0},{96,32},{1,65},{33,97},{65,1},{97,33},{2,66}... | collective-permute-start | bytes 24584 | tf_op jit(solution)/shard_map/ppermute | solution.py:175
  5.2 6.5 %collective-permute-start = (f32[1,64,128]{2,1,0:T(8,128)S(1)}, f32[1,64,128]{2,1,0:T(8,128)S(1)}, u32[]{:S(2)}, u32[]{:S(2)}) collective-permute-start(f32[1,64,128]{2,1,0:T(8,128)S(1)} %copy.53), channel_id=1, source_target_pairs={{0,16},{1,17},{2,18},{3,19},{4,20},{5,21},{6,22},{7,23},{8,24},{9,... | collective-permute-start | bytes 98312 | tf_op jit(solution)/shard_map/ppermute | solution.py:144
  11.7 4.3 %collective-permute-start.1 = (f32[2,64,128]{2,1,0:T(8,128)S(1)}, f32[2,64,128]{2,1,0:T(8,128)S(1)}, u32[]{:S(2)}, u32[]{:S(2)}) collective-permute-start(f32[2,64,128]{2,1,0:T(8,128)S(1)} %pad_maximum_fusion.3), channel_id=1, source_target_pairs={{0,8},{1,9},{2,10},{3,11},{4,12},{5,13},{6,14},{7,15},{8,0},{9,1},... | collective-permute-start | bytes 196616 | tf_op jit(solution)/shard_map/ppermute | solution.py:144
  16.1 7.5 %collective-permute-start.2 = (f32[4,64,128]{2,1,0:T(8,128)S(1)}, f32[4,64,128]{2,1,0:T(8,128)S(1)}, u32[]{:S(2)}, u32[]{:S(2)}) collective-permute-start(f32[4,64,128]{2,1,0:T(8,128)S(1)} %pad_maximum_fusion.2), channel_id=1, source_target_pairs={{0,4},{1,5},{2,6},{3,7},{4,0},{5,1},{6,2},{7,3},{8,12},{9,13},{10,... | collective-permute-start | bytes 393224 | tf_op jit(solution)/shard_map/ppermute | solution.py:144
  23.6 6.5 %collective-permute-start.3 = (f32[8,64,128]{2,1,0:T(8,128)S(1)}, f32[8,64,128]{2,1,0:T(8,128)S(1)}, u32[]{:S(2)}, u32[]{:S(2)}) collective-permute-start(f32[8,64,128]{2,1,0:T(8,128)S(1)} %pad_maximum_fusion.1), channel_id=1, source_target_pairs={{0,2},{1,3},{2,0},{3,1},{4,6},{5,7},{6,4},{7,5},{8,10},{9,11},{10,... | collective-permute-start | bytes 786440 | tf_op jit(solution)/shard_map/ppermute | solution.py:144
  30.1 41.5 %copy-start.1 = (f32[16,64,128]{2,1,0:T(8,128)}, f32[16,64,128]{2,1,0:T(8,128)S(1)}, u32[]{:S(2)}) copy-start(f32[16,64,128]{2,1,0:T(8,128)S(1)} %constant_dynamic-update-slice_fusion.near_ref) | copy-start | bytes 1572868
  30.1 5.6 %collective-permute-start.4 = (f32[16,64,128]{2,1,0:T(8,128)S(1)}, f32[16,64,128]{2,1,0:T(8,128)S(1)}, u32[]{:S(2)}, u32[]{:S(2)}) collective-permute-start(f32[16,64,128]{2,1,0:T(8,128)S(1)} %constant_dynamic-update-slice_fusion.near_ref), channel_id=1, source_target_pairs={{0,1},{1,0},{2,3},{3,2},{4,5},{5,4},{6,7},{7,6},{8,9},{9,8},{10,11... | collective-permute-start | bytes 1572872 | tf_op jit(solution)/shard_map/ppermute | solution.py:144
  35.7 37.2 %copy-start = (f32[16,64,128]{2,1,0:T(8,128)}, f32[16,64,128]{2,1,0:T(8,128)S(1)}, u32[]{:S(2)}) copy-start(f32[16,64,128]{2,1,0:T(8,128)S(1)} %collective-permute-done.4.far_ref) | copy-start | bytes 1572868
  38.7 13.6 %collective-permute-start.10 = (f32[2,8,64,64]{3,1,2,0:T(8,128)S(1)}, f32[2,8,64,64]{3,1,2,0:T(8,128)S(1)}, u32[]{:S(2)}, u32[]{:S(2)}) collective-permute-start(f32[2,8,64,64]{3,1,2,0:T(8,128)S(1)} %convolution_add_fusion), channel_id=1, source_target_pairs={{0,96},{1,97},{2,98},{3,99},{4,100},{5,101},{6,102},{7,103}} | collective-permute-start | bytes 786440 | tf_op jit(solution)/shard_map/ppermute | solution.py:205
  39.4 12.9 %collective-permute-start.9 = (f32[2,8,64,64]{3,1,2,0:T(8,128)S(1)}, f32[2,8,64,64]{3,1,2,0:T(8,128)S(1)}, u32[]{:S(2)}, u32[]{:S(2)}) collective-permute-start(f32[2,8,64,64]{3,1,2,0:T(8,128)S(1)} %convolution_add_fusion), channel_id=1, source_target_pairs={{0,64},{1,65},{2,66},{3,67},{4,68},{5,69},{6,70},{7,71},{40,104},{... | collective-permute-start | bytes 786440 | tf_op jit(solution)/shard_map/ppermute | solution.py:205
  40.1 27.8 %collective-permute-start.8 = (f32[2,8,64,64]{3,1,2,0:T(8,128)S(1)}, f32[2,8,64,64]{3,1,2,0:T(8,128)}, u32[]{:S(2)}, u32[]{:S(2)}) collective-permute-start(f32[2,8,64,64]{3,1,2,0:T(8,128)S(1)} %convolution_add_fusion), channel_id=1, source_target_pairs={{0,32},{1,33},{2,34},{3,35},{4,36},{5,37},{6,38},{7,39},{40,72},{4... | collective-permute-start | bytes 786440 | tf_op jit(solution)/shard_map/ppermute | solution.py:205

commit v8 on v7

--- a/solution.py
+++ b/solution.py
@@ -201,13 +201,23 @@
     table = jnp.where(table >= 0, jnp.take(slot_of, jnp.maximum(table, 0)), -1)
 
     owner = [(c * col_blocks) // row_blocks for c in range(col_count)]
-    window = window + sum(
-        lax.ppermute(window, ("prow", "pcol"), [
-            (owner[c] * col_count + c, (owner[c] + k) * col_count + c)
-            for c in range(col_count) if owner[c] + k < row_count
-        ])
-        for k in range(1, row_count)
-    )
+    def send(value, moves):
+        return lax.ppermute(value, ("prow", "pcol"), [
+            (a * col_count + c, b * col_count + c) for c, a, b in moves])
+
+    if row_count == 4:
+        down = send(window, [(c, owner[c], owner[c] + 1)
+                             for c in range(col_count) if owner[c] < 3])
+        wrapped = [c for c in range(col_count) if owner[c] < 2]
+        back = send(window, [(c, owner[c], (owner[c] - 1) % 4) for c in wrapped])
+        relay = send(back, [(c, (owner[c] - 1) % 4, (owner[c] - 2) % 4) for c in wrapped])
+        window = window + down + back + relay
+    else:
+        window = window + sum(
+            send(window, [(c, owner[c], owner[c] + k)
+                          for c in range(col_count) if owner[c] + k < row_count])
+            for k in range(1, row_count)
+        )
     right = jnp.einsum("pxa,pjba->pxjb", inverse, window, precision=HIGHEST)
     right = right.reshape(2 * width, col_blocks * width)
 

time: 85.1 us -> 86.5 us (1.016)
  the two profiles are of different devices: /device:TPU:14 before, /device:TPU:22 now
where the time goes in v8:
time: 86.5 us; the launch traced here: 85.9 us
  waiting for transfers between devices  31.4 us (36%)
  Pallas kernels  19.6 us (23%)
  starting transfers between devices  13.7 us (16%)
  local copies, waits for them, and re-layouts  10.2 us (12%)
  other arithmetic  6.59 us (8%)
  matrix products  4.01 us (5%)
    ppermute x3, waiting for transfers between devices, send(): lax.ppermute(value, ('prow', 'pcol'), [(a * col_count + c, b * col_count...  18 us
    ppermute x5, waiting for transfers between devices, doubling_gather(): other = lax.ppermute(block, axis, [(i, i ^ mask) for i in range(count)])  13.3 us
    pallas_call x1, Pallas kernels, apply_update(): pl.pallas_call(kernel, out_shape=jax.ShapeDtypeStruct(front.shape, front....  11.6 us
    pallas_call x1, Pallas kernels, invert_spd(): pl.pallas_call(inverse_kernel, out_shape=jax.ShapeDtypeStruct(matrix.shap...  8.03 us
    ppermute x5, starting transfers between devices, doubling_gather(): other = lax.ppermute(block, axis, [(i, i ^ mask) for i in range(count)])  7.48 us
    ppermute x3, starting transfers between devices, per_device(): lax.ppermute(diag_blocks, 'prow', [(i, (i + k) % row_count) for i in rang...  3.57 us
    ppermute x3, starting transfers between devices, send(): lax.ppermute(value, ('prow', 'pcol'), [(a * col_count + c, b * col_count...  2.66 us
    dot_general x1, matrix products, per_device(): right = jnp.einsum('pxa,pjba->pxjb', inverse, window, precision=HIGHEST)  2.47 us
  transfers between devices with their start and end apart: 11, of which 4 were waited for; matrix products, arithmetic and copies ran while one was open for 15% of the time, Pallas kernels for 9%

profile of v8, /device:TPU:22, one launch (start us, length us, event | category | flops | bytes accessed | tf_op | source)
XLA Modules:
  0.0 85.9 jit_solution(13685914342734660963)
XLA Ops:
  0.0 1.3 %collective-permute-start.5 = (f32[2,16,64]{2,1,0:T(8,128)}, f32[2,16,64]{2,1,0:T(8,128)S(1)}, u32[]{:S(2)}, u32[]{:S(2)}) collective-permute-start(f32[2,16,64]{2,1,0:T(8,128)} %param.6), channel_id=1, source_target_pairs={{0,32},{32,64},{64,96},{96,0},{1,33},{33,65},{65,97},{97,1},{2,34}... | collective-permute-start | bytes 24584 | tf_op jit(solution)/shard_map/ppermute | solution.py:175
  1.3 0.7 collective-permute-start.7
  2.0 1.5 %collective-permute-start.6 = (f32[2,16,64]{2,1,0:T(8,128)}, f32[2,16,64]{2,1,0:T(8,128)S(1)}, u32[]{:S(2)}, u32[]{:S(2)}) collective-permute-start(f32[2,16,64]{2,1,0:T(8,128)} %param.6), channel_id=1, source_target_pairs={{0,64},{32,96},{64,0},{96,32},{1,65},{33,97},{65,1},{97,33},{2,66}... | collective-permute-start | bytes 24584 | tf_op jit(solution)/shard_map/ppermute | solution.py:175
  3.6 0.9 %copy.53 = f32[1,64,128]{2,1,0:T(8,128)S(1)} copy(f32[1,64,128]{1,2,0:T(8,128)} %bitcast.41) | data formatting | bytes 65536 | tf_op jit(solution)/shard_map/broadcast_in_dim;reshape | solution.py:168
  4.5 4.0 %collective-permute-start = (f32[1,64,128]{2,1,0:T(8,128)S(1)}, f32[1,64,128]{2,1,0:T(8,128)S(1)}, u32[]{:S(2)}, u32[]{:S(2)}) collective-permute-start(f32[1,64,128]{2,1,0:T(8,128)S(1)} %copy.53), channel_id=1, source_target_pairs={{0,16},{1,17},{2,18},{3,19},{4,20},{5,21},{6,22},{7,23},{8,24},{9,... | collective-permute-start | bytes 98312 | tf_op jit(solution)/shard_map/ppermute | solution.py:144
  8.4 0.7 constant_dynamic-slice_fusion
  9.4 0.8 compare_reduce_fusion
  10.2 0.7 broadcast_xor_fusion
  11.0 1.1 %collective-permute-start.1 = (f32[2,64,128]{2,1,0:T(8,128)S(1)}, f32[2,64,128]{2,1,0:T(8,128)S(1)}, u32[]{:S(2)}, u32[]{:S(2)}) collective-permute-start(f32[2,64,128]{2,1,0:T(8,128)S(1)} %pad_maximum_fusion.3), channel_id=1, source_target_pairs={{0,8},{1,9},{2,10},{3,11},{4,12},{5,13},{6,14},{7,15},{8,0},{9,1},... | collective-permute-start | bytes 196616 | tf_op jit(solution)/shard_map/ppermute | solution.py:144
  12.1 3.2 %collective-permute-done.1 = f32[2,64,128]{2,1,0:T(8,128)S(1)} collective-permute-done((f32[2,64,128]{2,1,0:T(8,128)S(1)}, f32[2,64,128]{2,1,0:T(8,128)S(1)}, u32[]{:S(2)}, u32[]{:S(2)}) %collective-permute-start.1) | collective-permute-done | bytes 65568 | tf_op jit(solution)/shard_map/ppermute | solution.py:144
  15.3 1.5 %collective-permute-start.2 = (f32[4,64,128]{2,1,0:T(8,128)S(1)}, f32[4,64,128]{2,1,0:T(8,128)S(1)}, u32[]{:S(2)}, u32[]{:S(2)}) collective-permute-start(f32[4,64,128]{2,1,0:T(8,128)S(1)} %pad_maximum_fusion.2), channel_id=1, source_target_pairs={{0,4},{1,5},{2,6},{3,7},{4,0},{5,1},{6,2},{7,3},{8,12},{9,13},{10,... | collective-permute-start | bytes 393224 | tf_op jit(solution)/shard_map/ppermute | solution.py:144
  16.8 1.4 %gather_fusion = s32[32]{0:T(128)S(1)} fusion(s32[32]{0:T(128)} %constant.101.clone, s32[1024]{0:T(1024)S(1)} %pad_clamp_fusion.1), kind=kCustom, calls=%fused_computation | custom fusion | bytes 384 | tf_op jit(solution)/shard_map/jit(_take)/gather | solution.py:172
  18.2 4.5 %collective-permute-done.2 = f32[4,64,128]{2,1,0:T(8,128)S(1)} collective-permute-done((f32[4,64,128]{2,1,0:T(8,128)S(1)}, f32[4,64,128]{2,1,0:T(8,128)S(1)}, u32[]{:S(2)}, u32[]{:S(2)}) %collective-permute-start.2) | collective-permute-done | bytes 131104 | tf_op jit(solution)/shard_map/ppermute | solution.py:144
  22.7 0.9 collective-permute-start.3
  23.6 5.6 %collective-permute-done.3 = f32[8,64,128]{2,1,0:T(8,128)S(1)} collective-permute-done((f32[8,64,128]{2,1,0:T(8,128)S(1)}, f32[8,64,128]{2,1,0:T(8,128)S(1)}, u32[]{:S(2)}, u32[]{:S(2)}) %collective-permute-start.3) | collective-permute-done | bytes 262176 | tf_op jit(solution)/shard_map/ppermute | solution.py:144
  29.3 0.7 pad_add_fusion.place_ref
  30.0 0.9 %copy.35 = f32[2,64,64]{1,2,0:T(8,128)S(1)} copy(f32[2,64,64]{2,1,0:T(8,128)} %param.7) | data formatting | bytes 65536 | tf_op args[1]
  31.6 0.7 broadcast_in_dim.122
  34.8 0.6 reshape.86
  35.4 1.1 %fusion = f32[2,8,64,64]{3,1,2,0:T(8,128)S(1)} fusion(f32[16,64,2,64]{3,2,1,0:T(2,128)S(1)} %reshape.86, pred[2,8,32]{2,1,0:T(8,128)(4,1)S(1)} %compare_and_fusion), kind=kOutput, calls=%fused_computation.3 | convolution fusion | flops 12582912 | bytes 786944 | tf_op jit(solution)/shard_map/pjk,kbpa->pjba/dot_general | solution.py:192
  37.2 0.6 iota_reduce_fusion
  37.8 0.7 collective-permute-start.9
  38.5 0.7 collective-permute-start.8
  39.4 0.7 pad_maximum_fusion.4.system_ref
  40.1 1.3 %collective-permute-start.10 = (f32[2,8,64,64]{3,1,2,0:T(8,128)S(1)}, f32[2,8,64,64]{3,1,2,0:T(8,128)}, u32[]{:S(2)}, u32[]{:S(2)}) collective-permute-start(f32[2,8,64,64]{3,1,2,0:T(8,128)S(1)} %collective-permute-done.9), channel_id=1, source_target_pairs={{96,64},{97,65},{98,66},{99,67},{100,68},{101,69},{102,70},{103,71... | collective-permute-start | bytes 786440 | tf_op jit(solution)/shard_map/ppermute | solution.py:205
  41.4 1.2 %gather_fusion.1 = s32[128]{0:T(128)S(1)} fusion(s32[32]{0:T(128)S(1)} %and_select_fusion, s32[1024]{0:T(1024)S(1)} %pad_clamp_fusion), kind=kCustom, calls=%fused_computation.1 | custom fusion | bytes 1536 | tf_op jit(solution)/shard_map/jit(_take)/gather | solution.py:201
  42.7 8.0 %shard_map.64 = f32[2,64,64]{2,1,0:T(8,128)} custom-call(f32[2,64,128]{2,1,0:T(8,128)} %pad_maximum_fusion.4.system_ref), custom_call_target="tpu_custom_call" | custom-call | flops 4194304 | bytes 98304 | tf_op jit(solution)/shard_map/pallas_call | solution.py:127
  51.4 18.0 %collective-permute-done.10 = f32[2,8,64,64]{3,1,2,0:T(8,128)} collective-permute-done((f32[2,8,64,64]{3,1,2,0:T(8,128)S(1)}, f32[2,8,64,64]{3,1,2,0:T(8,128)}, u32[]{:S(2)}, u32[]{:S(2)}) %collective-permute-start.10) | collective-permute-done | bytes 262176 | tf_op jit(solution)/shard_map/ppermute | solution.py:205
  69.4 1.1 %add_add_fusion = f32[2,8,64,64]{3,1,2,0:T(8,128)S(1)} fusion(f32[2,8,64,64]{3,1,2,0:T(8,128)} %collective-permute-done.10, f32[2,8,64,64]{3,1,2,0:T(8,128)S(1)} %collective-permute-done.9, f32[2,8,64,64]{3,1,2,0:T(8,128)S(1)} %convolution_add_fusion, f32[2,8,64,64]{3,1,2,0:T(8,128)S(1)} %collective-permute-done.8), kind=kLoop, calls=%fused_computation.7 | loop fusion | flops 196608 | bytes 1310720 | tf_op jit(solution)/shard_map/add | solution.py:214
  70.5 2.5 %fusion.2 = f32[2,64,8,64]{3,1,2,0:T(8,128)S(1)} fusion(f32[2,8,64,64]{3,1,2,0:T(8,128)S(1)} %add_add_fusion, f32[2,64,64]{2,1,0:T(8,128)} %shard_map.64), kind=kOutput, calls=%fused_computation.5 | convolution fusion | flops 50331648 | bytes 557056 | tf_op jit(solution)/shard_map/pxa,pjba->pxjb/dot_general | solution.py:221
  73.5 0.8 pad_maximum_fusion.stack_ref
  74.3 11.6 %shard_map.65 = f32[4096,512]{1,0:T(8,128)} custom-call(s32[2,64]{1,0:T(2,128)} %compare_select_fusion.5.table_ref, s32[2]{0:T(128)} %pad_add_fusion.place_ref, f32[16,64,128]{2,1,0:T(8,128)} %copy-done.1, f32[16,64,128]{2,1,0:T(8,128)} %copy-done, bf16[384,512]{1,0:T(8,128)(2,1)} %pad_maximum_fusion.stack_ref, f32[4096,512]{1,0:T(8,128)} %front_ref.1), custom_call_target="tpu_custom_call" | custom-call | flops 1610612736 | bytes 18219008 | tf_op jit(solution)/shard_map/pallas_call | solution.py:78
  (71 shorter events, 5.5 us)
Async XLA Ops:
  0.0 37.0 %copy-start.2 = (s32[2,128]{1,0:T(2,128)S(1)}, s32[2,128]{1,0:T(2,128)}, u32[]{:S(2)}) copy-start(s32[2,128]{1,0:T(2,128)} %param.8) | copy-start | bytes 3076
  0.0 32.6 %collective-permute-start.5 = (f32[2,16,64]{2,1,0:T(8,128)}, f32[2,16,64]{2,1,0:T(8,128)S(1)}, u32[]{:S(2)}, u32[]{:S(2)}) collective-permute-start(f32[2,16,64]{2,1,0:T(8,128)} %param.6), channel_id=1, source_target_pairs={{0,32},{32,64},{64,96},{96,0},{1,33},{33,65},{65,97},{97,1},{2,34}... | collective-permute-start | bytes 24584 | tf_op jit(solution)/shard_map/ppermute | solution.py:175
  1.3 31.2 %collective-permute-start.7 = (f32[2,16,64]{2,1,0:T(8,128)}, f32[2,16,64]{2,1,0:T(8,128)S(1)}, u32[]{:S(2)}, u32[]{:S(2)}) collective-permute-start(f32[2,16,64]{2,1,0:T(8,128)} %param.6), channel_id=1, source_target_pairs={{0,96},{32,0},{64,32},{96,64},{1,97},{33,1},{65,33},{97,65},{2,98}... | collective-permute-start | bytes 24584 | tf_op jit(solution)/shard_map/ppermute | solution.py:175
  2.0 30.4 %collective-permute-start.6 = (f32[2,16,64]{2,1,0:T(8,128)}, f32[2,16,64]{2,1,0:T(8,128)S(1)}, u32[]{:S(2)}, u32[]{:S(2)}) collective-permute-start(f32[2,16,64]{2,1,0:T(8,128)} %param.6), channel_id=1, source_target_pairs={{0,64},{32,96},{64,0},{96,32},{1,65},{33,97},{65,1},{97,33},{2,66}... | collective-permute-start | bytes 24584 | tf_op jit(solution)/shard_map/ppermute | solution.py:175
  4.5 6.5 %collective-permute-start = (f32[1,64,128]{2,1,0:T(8,128)S(1)}, f32[1,64,128]{2,1,0:T(8,128)S(1)}, u32[]{:S(2)}, u32[]{:S(2)}) collective-permute-start(f32[1,64,128]{2,1,0:T(8,128)S(1)} %copy.53), channel_id=1, source_target_pairs={{0,16},{1,17},{2,18},{3,19},{4,20},{5,21},{6,22},{7,23},{8,24},{9,... | collective-permute-start | bytes 98312 | tf_op jit(solution)/shard_map/ppermute | solution.py:144
  11.0 4.3 %collective-permute-start.1 = (f32[2,64,128]{2,1,0:T(8,128)S(1)}, f32[2,64,128]{2,1,0:T(8,128)S(1)}, u32[]{:S(2)}, u32[]{:S(2)}) collective-permute-start(f32[2,64,128]{2,1,0:T(8,128)S(1)} %pad_maximum_fusion.3), channel_id=1, source_target_pairs={{0,8},{1,9},{2,10},{3,11},{4,12},{5,13},{6,14},{7,15},{8,0},{9,1},... | collective-permute-start | bytes 196616 | tf_op jit(solution)/shard_map/ppermute | solution.py:144
  15.3 7.4 %collective-permute-start.2 = (f32[4,64,128]{2,1,0:T(8,128)S(1)}, f32[4,64,128]{2,1,0:T(8,128)S(1)}, u32[]{:S(2)}, u32[]{:S(2)}) collective-permute-start(f32[4,64,128]{2,1,0:T(8,128)S(1)} %pad_maximum_fusion.2), channel_id=1, source_target_pairs={{0,4},{1,5},{2,6},{3,7},{4,0},{5,1},{6,2},{7,3},{8,12},{9,13},{10,... | collective-permute-start | bytes 393224 | tf_op jit(solution)/shard_map/ppermute | solution.py:144
  22.7 6.5 %collective-permute-start.3 = (f32[8,64,128]{2,1,0:T(8,128)S(1)}, f32[8,64,128]{2,1,0:T(8,128)S(1)}, u32[]{:S(2)}, u32[]{:S(2)}) collective-permute-start(f32[8,64,128]{2,1,0:T(8,128)S(1)} %pad_maximum_fusion.1), channel_id=1, source_target_pairs={{0,2},{1,3},{2,0},{3,1},{4,6},{5,7},{6,4},{7,5},{8,10},{9,11},{10,... | collective-permute-start | bytes 786440 | tf_op jit(solution)/shard_map/ppermute | solution.py:144
  29.2 43.8 %copy-start.1 = (f32[16,64,128]{2,1,0:T(8,128)}, f32[16,64,128]{2,1,0:T(8,128)S(1)}, u32[]{:S(2)}) copy-start(f32[16,64,128]{2,1,0:T(8,128)S(1)} %constant_dynamic-update-slice_fusion.near_ref) | copy-start | bytes 1572868
  29.2 5.6 %collective-permute-start.4 = (f32[16,64,128]{2,1,0:T(8,128)S(1)}, f32[16,64,128]{2,1,0:T(8,128)S(1)}, u32[]{:S(2)}, u32[]{:S(2)}) collective-permute-start(f32[16,64,128]{2,1,0:T(8,128)S(1)} %constant_dynamic-update-slice_fusion.near_ref), channel_id=1, source_target_pairs={{0,1},{1,0},{2,3},{3,2},{4,5},{5,4},{6,7},{7,6},{8,9},{9,8},{10,11... | collective-permute-start | bytes 1572872 | tf_op jit(solution)/shard_map/ppermute | solution.py:144
  34.8 39.5 %copy-start = (f32[16,64,128]{2,1,0:T(8,128)}, f32[16,64,128]{2,1,0:T(8,128)S(1)}, u32[]{:S(2)}) copy-start(f32[16,64,128]{2,1,0:T(8,128)S(1)} %collective-permute-done.4.far_ref) | copy-start | bytes 1572868
  37.8 2.3 %collective-permute-start.9 = (f32[2,8,64,64]{3,1,2,0:T(8,128)S(1)}, f32[2,8,64,64]{3,1,2,0:T(8,128)S(1)}, u32[]{:S(2)}, u32[]{:S(2)}) collective-permute-start(f32[2,8,64,64]{3,1,2,0:T(8,128)S(1)} %convolution_add_fusion), channel_id=1, source_target_pairs={{0,96},{1,97},{2,98},{3,99},{4,100},{5,101},{6,102},{7,103},{40,8}... | collective-permute-start | bytes 786440 | tf_op jit(solution)/shard_map/ppermute | solution.py:205
  38.5 12.9 %collective-permute-start.8 = (f32[2,8,64,64]{3,1,2,0:T(8,128)S(1)}, f32[2,8,64,64]{3,1,2,0:T(8,128)S(1)}, u32[]{:S(2)}, u32[]{:S(2)}) collective-permute-start(f32[2,8,64,64]{3,1,2,0:T(8,128)S(1)} %convolution_add_fusion), channel_id=1, source_target_pairs={{0,32},{1,33},{2,34},{3,35},{4,36},{5,37},{6,38},{7,39},{40,72},{4... | collective-permute-start | bytes 786440 | tf_op jit(solution)/shard_map/ppermute | solution.py:205
  40.1 29.2 %collective-permute-start.10 = (f32[2,8,64,64]{3,1,2,0:T(8,128)S(1)}, f32[2,8,64,64]{3,1,2,0:T(8,128)}, u32[]{:S(2)}, u32[]{:S(2)}) collective-permute-start(f32[2,8,64,64]{3,1,2,0:T(8,128)S(1)} %collective-permute-done.9), channel_id=1, source_target_pairs={{96,64},{97,65},{98,66},{99,67},{100,68},{101,69},{102,70},{103,71... | collective-permute-start | bytes 786440 | tf_op jit(solution)/shard_map/ppermute | solution.py:205

commit v9 on v7

--- a/solution.py
+++ b/solution.py
@@ -201,13 +201,14 @@
     table = jnp.where(table >= 0, jnp.take(slot_of, jnp.maximum(table, 0)), -1)
 
     owner = [(c * col_blocks) // row_blocks for c in range(col_count)]
-    window = window + sum(
-        lax.ppermute(window, ("prow", "pcol"), [
+    def send(value, k):
+        return lax.ppermute(value, ("prow", "pcol"), [
             (owner[c] * col_count + c, (owner[c] + k) * col_count + c)
             for c in range(col_count) if owner[c] + k < row_count
         ])
-        for k in range(1, row_count)
-    )
+
+    nearest = jnp.stack([send(window[panel], 1) for panel in range(window.shape[0])])
+    window = window + nearest + sum(send(window, k) for k in range(2, row_count))
     right = jnp.einsum("pxa,pjba->pxjb", inverse, window, precision=HIGHEST)
     right = right.reshape(2 * width, col_blocks * width)
 

time: 85.1 us -> 83.6 us (0.982)
  waiting for transfers between devices: 29.1 us -> 24.4 us
  local copies, waits for them, and re-layouts: 10.2 us -> 13.4 us
  starting transfers between devices: 14.5 us -> 15.7 us
  other arithmetic: 6.62 us -> 5.51 us
    unnamed x11 -> x9, local copies, waits for them, and re-layouts: 0.95 us -> 3.41 us
    ppermute x5, waiting for transfers between devices: 13.5 us -> 11 us  [doubling_gather(): other = lax.ppermute(block, axis, [(i, i ^ mask) for i in range(count)])]
    ppermute x3 -> x4, waiting for transfers between devices: 15.7 us -> 13.3 us  [send(): lax.ppermute(value, ('prow', 'pcol'), [(owner[c] * col_count + c, (owner[...]
    ppermute x3 -> x4, starting transfers between devices: 2.67 us -> 3.97 us  [send(): lax.ppermute(value, ('prow', 'pcol'), [(owner[c] * col_count + c, (owner[...]
    add x1, other arithmetic: 1.18 us -> 0.1 us  [per_device(): window + nearest + sum((send(window, k) for k in range(2, row_count)))]
  transfers between devices with their start and end apart: 11 -> 12, of which waited for: 4 -> 5; matrix products, arithmetic and copies ran while one was open for 15% -> 19% of each run, Pallas kernels for 10% -> 10%
where the time goes in v9:
time: 83.6 us; the launch traced here: 83 us
  waiting for transfers between devices  24.4 us (29%)
  Pallas kernels  19.6 us (23%)
  starting transfers between devices  15.7 us (19%)
  local copies, waits for them, and re-layouts  13.4 us (16%)
  other arithmetic  5.51 us (7%)
  matrix products  4.01 us (5%)
    ppermute x4, waiting for transfers between devices, send(): lax.ppermute(value, ('prow', 'pcol'), [(owner[c] * col_count + c, (owner[...  13.3 us
    pallas_call x1, Pallas kernels, apply_update(): pl.pallas_call(kernel, out_shape=jax.ShapeDtypeStruct(front.shape, front....  11.6 us
    ppermute x5, waiting for transfers between devices, doubling_gather(): other = lax.ppermute(block, axis, [(i, i ^ mask) for i in range(count)])  11 us
    pallas_call x1, Pallas kernels, invert_spd(): pl.pallas_call(inverse_kernel, out_shape=jax.ShapeDtypeStruct(matrix.shap...  8.03 us
    ppermute x5, starting transfers between devices, doubling_gather(): other = lax.ppermute(block, axis, [(i, i ^ mask) for i in range(count)])  7.39 us
    ppermute x3, starting transfers between devices, per_device(): lax.ppermute(diag_blocks, 'prow', [(i, (i + k) % row_count) for i in rang...  4.32 us
    ppermute x4, starting transfers between devices, send(): lax.ppermute(value, ('prow', 'pcol'), [(owner[c] * col_count + c, (owner[...  3.97 us
    unnamed x9, local copies, waits for them, and re-layouts  3.41 us
  transfers between devices with their start and end apart: 12, of which 5 were waited for; matrix products, arithmetic and copies ran while one was open for 19% of the time, Pallas kernels for 10%

profile of v9, /device:TPU:14, one launch (start us, length us, event | category | flops | bytes accessed | tf_op | source)
XLA Modules:
  0.0 83.0 jit_solution(1717472396080689414)
XLA Ops:
  0.0 1.6 %collective-permute-start.5 = (f32[2,16,64]{2,1,0:T(8,128)}, f32[2,16,64]{2,1,0:T(8,128)S(1)}, u32[]{:S(2)}, u32[]{:S(2)}) collective-permute-start(f32[2,16,64]{2,1,0:T(8,128)} %param.6), channel_id=1, source_target_pairs={{0,32},{32,64},{64,96},{96,0},{1,33},{33,65},{65,97},{97,1},{2,34}... | collective-permute-start | bytes 24584 | tf_op jit(solution)/shard_map/ppermute | solution.py:175
  2.0 2.3 %collective-permute-start.6 = (f32[2,16,64]{2,1,0:T(8,128)}, f32[2,16,64]{2,1,0:T(8,128)S(1)}, u32[]{:S(2)}, u32[]{:S(2)}) collective-permute-start(f32[2,16,64]{2,1,0:T(8,128)} %param.6), channel_id=1, source_target_pairs={{0,64},{32,96},{64,0},{96,32},{1,65},{33,97},{65,1},{97,33},{2,66}... | collective-permute-start | bytes 24584 | tf_op jit(solution)/shard_map/ppermute | solution.py:175
  4.3 0.9 %copy.53 = f32[1,64,128]{2,1,0:T(8,128)S(1)} copy(f32[1,64,128]{1,2,0:T(8,128)} %bitcast.49) | data formatting | bytes 65536 | tf_op jit(solution)/shard_map/broadcast_in_dim;reshape | solution.py:168
  5.2 4.0 %collective-permute-start = (f32[1,64,128]{2,1,0:T(8,128)S(1)}, f32[1,64,128]{2,1,0:T(8,128)S(1)}, u32[]{:S(2)}, u32[]{:S(2)}) collective-permute-start(f32[1,64,128]{2,1,0:T(8,128)S(1)} %copy.53), channel_id=1, source_target_pairs={{0,16},{1,17},{2,18},{3,19},{4,20},{5,21},{6,22},{7,23},{8,24},{9,... | collective-permute-start | bytes 98312 | tf_op jit(solution)/shard_map/ppermute | solution.py:144
  9.2 0.7 constant_dynamic-slice_fusion
  10.1 0.8 compare_reduce_fusion
  10.9 0.7 broadcast_xor_fusion
  11.7 1.1 %collective-permute-start.1 = (f32[2,64,128]{2,1,0:T(8,128)S(1)}, f32[2,64,128]{2,1,0:T(8,128)S(1)}, u32[]{:S(2)}, u32[]{:S(2)}) collective-permute-start(f32[2,64,128]{2,1,0:T(8,128)S(1)} %pad_maximum_fusion.3), channel_id=1, source_target_pairs={{0,8},{1,9},{2,10},{3,11},{4,12},{5,13},{6,14},{7,15},{8,0},{9,1},... | collective-permute-start | bytes 196616 | tf_op jit(solution)/shard_map/ppermute | solution.py:144
  12.8 3.2 %collective-permute-done.1 = f32[2,64,128]{2,1,0:T(8,128)S(1)} collective-permute-done((f32[2,64,128]{2,1,0:T(8,128)S(1)}, f32[2,64,128]{2,1,0:T(8,128)S(1)}, u32[]{:S(2)}, u32[]{:S(2)}) %collective-permute-start.1) | collective-permute-done | bytes 65568 | tf_op jit(solution)/shard_map/ppermute | solution.py:144
  16.1 1.5 %collective-permute-start.2 = (f32[4,64,128]{2,1,0:T(8,128)S(1)}, f32[4,64,128]{2,1,0:T(8,128)S(1)}, u32[]{:S(2)}, u32[]{:S(2)}) collective-permute-start(f32[4,64,128]{2,1,0:T(8,128)S(1)} %pad_maximum_fusion.2), channel_id=1, source_target_pairs={{0,4},{1,5},{2,6},{3,7},{4,0},{5,1},{6,2},{7,3},{8,12},{9,13},{10,... | collective-permute-start | bytes 393224 | tf_op jit(solution)/shard_map/ppermute | solution.py:144
  17.6 1.4 %gather_fusion = s32[32]{0:T(128)S(1)} fusion(s32[32]{0:T(128)} %constant.101.clone, s32[1024]{0:T(1024)S(1)} %pad_clamp_fusion.1), kind=kCustom, calls=%fused_computation | custom fusion | bytes 384 | tf_op jit(solution)/shard_map/jit(_take)/gather | solution.py:172
  19.5 4.1 %collective-permute-done.2 = f32[4,64,128]{2,1,0:T(8,128)S(1)} collective-permute-done((f32[4,64,128]{2,1,0:T(8,128)S(1)}, f32[4,64,128]{2,1,0:T(8,128)S(1)}, u32[]{:S(2)}, u32[]{:S(2)}) %collective-permute-start.2) | collective-permute-done | bytes 131104 | tf_op jit(solution)/shard_map/ppermute | solution.py:144
  23.6 0.9 %collective-permute-start.3 = (f32[8,64,128]{2,1,0:T(8,128)S(1)}, f32[8,64,128]{2,1,0:T(8,128)S(1)}, u32[]{:S(2)}, u32[]{:S(2)}) collective-permute-start(f32[8,64,128]{2,1,0:T(8,128)S(1)} %pad_maximum_fusion.1), channel_id=1, source_target_pairs={{0,2},{1,3},{2,0},{3,1},{4,6},{5,7},{6,4},{7,5},{8,10},{9,11},{10,... | collective-permute-start | bytes 786440 | tf_op jit(solution)/shard_map/ppermute | solution.py:144
  25.7 0.6 constant_dynamic-update-slice_fusion.1
  26.3 3.7 %collective-permute-done.3 = f32[8,64,128]{2,1,0:T(8,128)S(1)} collective-permute-done((f32[8,64,128]{2,1,0:T(8,128)S(1)}, f32[8,64,128]{2,1,0:T(8,128)S(1)}, u32[]{:S(2)}, u32[]{:S(2)}) %collective-permute-start.3) | collective-permute-done | bytes 262176 | tf_op jit(solution)/shard_map/ppermute | solution.py:144
  30.1 0.7 constant_dynamic-update-slice_fusion.near_ref
  30.8 0.7 pad_add_fusion.place_ref
  31.5 0.9 %copy.35 = f32[2,64,64]{1,2,0:T(8,128)S(1)} copy(f32[2,64,64]{2,1,0:T(8,128)} %param.7) | data formatting | bytes 65536 | tf_op args[1]
  33.0 0.7 broadcast_in_dim.122
  36.9 1.1 %fusion = f32[2,8,64,64]{3,1,2,0:T(8,128)S(1)} fusion(f32[16,64,2,64]{3,2,1,0:T(2,128)S(1)} %reshape.86, pred[2,8,32]{2,1,0:T(8,128)(4,1)S(1)} %compare_and_fusion), kind=kOutput, calls=%fused_computation.3 | convolution fusion | flops 12582912 | bytes 786944 | tf_op jit(solution)/shard_map/pjk,kbpa->pjba/dot_general | solution.py:192
  39.3 0.7 collective-permute-start.10
  40.0 0.7 collective-permute-start.11
  40.8 1.2 %gather_fusion.1 = s32[128]{0:T(128)S(1)} fusion(s32[32]{0:T(128)S(1)} %and_select_fusion, s32[1024]{0:T(1024)S(1)} %pad_clamp_fusion), kind=kCustom, calls=%fused_computation.1 | custom fusion | bytes 1536 | tf_op jit(solution)/shard_map/jit(_take)/gather | solution.py:201
  42.2 1.3 %collective-permute-start.8 = (f32[8,64,64]{2,0,1:T(8,128)S(1)}, f32[8,64,64]{2,0,1:T(8,128)S(1)}, u32[]{:S(2)}, u32[]{:S(2)}) collective-permute-start(f32[8,64,64]{2,0,1:T(8,128)S(1)} %get-tuple-element.17), channel_id=1, source_target_pairs={{0,32},{1,33},{2,34},{3,35},{4,36},{5,37},{6,38},{7,39},{40,72},{4... | collective-permute-start | bytes 393224 | tf_op jit(solution)/shard_map/ppermute | solution.py:205
  43.5 1.3 %collective-permute-start.9 = (f32[8,64,64]{2,0,1:T(8,128)S(1)}, f32[8,64,64]{2,0,1:T(8,128)S(1)}, u32[]{:S(2)}, u32[]{:S(2)}) collective-permute-start(f32[8,64,64]{2,0,1:T(8,128)S(1)} %get-tuple-element.18), channel_id=1, source_target_pairs={{0,32},{1,33},{2,34},{3,35},{4,36},{5,37},{6,38},{7,39},{40,72},{4... | collective-permute-start | bytes 393224 | tf_op jit(solution)/shard_map/ppermute | solution.py:205
  44.8 0.7 pad_maximum_fusion.4.system_ref
  45.6 8.0 %shard_map.64 = f32[2,64,64]{2,1,0:T(8,128)} custom-call(f32[2,64,128]{2,1,0:T(8,128)} %pad_maximum_fusion.4.system_ref), custom_call_target="tpu_custom_call" | custom-call | flops 4194304 | bytes 98304 | tf_op jit(solution)/shard_map/pallas_call | solution.py:127
  54.2 8.2 %collective-permute-done.8 = f32[8,64,64]{2,0,1:T(8,128)S(1)} collective-permute-done((f32[8,64,64]{2,0,1:T(8,128)S(1)}, f32[8,64,64]{2,0,1:T(8,128)S(1)}, u32[]{:S(2)}, u32[]{:S(2)}) %collective-permute-start.8) | collective-permute-done | bytes 131104 | tf_op jit(solution)/shard_map/ppermute | solution.py:205
  62.3 5.2 %collective-permute-done.9 = f32[8,64,64]{2,0,1:T(8,128)S(1)} collective-permute-done((f32[8,64,64]{2,0,1:T(8,128)S(1)}, f32[8,64,64]{2,0,1:T(8,128)S(1)}, u32[]{:S(2)}, u32[]{:S(2)}) %collective-permute-start.9) | collective-permute-done | bytes 131104 | tf_op jit(solution)/shard_map/ppermute | solution.py:205
  67.6 2.5 %fusion.3 = f32[2,64,8,64]{3,1,2,0:T(8,128)S(1)} fusion(f32[2,8,64,64]{3,1,2,0:T(8,128)S(1)} %fusion.2, f32[2,64,64]{2,1,0:T(8,128)} %shard_map.64), kind=kOutput, calls=%fused_computation.7 | convolution fusion | flops 50331648 | bytes 557056 | tf_op jit(solution)/shard_map/pxa,pjba->pxjb/dot_general | solution.py:212
  70.6 0.8 pad_maximum_fusion.stack_ref
  71.4 11.6 %shard_map.65 = f32[4096,512]{1,0:T(8,128)} custom-call(s32[2,64]{1,0:T(2,128)} %compare_select_fusion.5.table_ref, s32[2]{0:T(128)} %pad_add_fusion.place_ref, f32[16,64,128]{2,1,0:T(8,128)} %constant_dynamic-update-slice_fusion.near_ref, f32[16,64,128]{2,1,0:T(8,128)} %copy-done, bf16[384,512]{1,0:T(8,128)(2,1)} %pad_maximum_fusion.stack_ref, ...), custom_call_target="tpu_custom_call" | custom-call | flops 1610612736 | bytes 18219008 | tf_op jit(solution)/shard_map/pallas_call | solution.py:78
  (72 shorter events, 9.0 us)
Async XLA Ops:
  0.0 38.5 %copy-start.1 = (s32[2,128]{1,0:T(2,128)S(1)}, s32[2,128]{1,0:T(2,128)}, u32[]{:S(2)}) copy-start(s32[2,128]{1,0:T(2,128)} %param.8) | copy-start | bytes 3076
  0.0 34.1 %collective-permute-start.5 = (f32[2,16,64]{2,1,0:T(8,128)}, f32[2,16,64]{2,1,0:T(8,128)S(1)}, u32[]{:S(2)}, u32[]{:S(2)}) collective-permute-start(f32[2,16,64]{2,1,0:T(8,128)} %param.6), channel_id=1, source_target_pairs={{0,32},{32,64},{64,96},{96,0},{1,33},{33,65},{65,97},{97,1},{2,34}... | collective-permute-start | bytes 24584 | tf_op jit(solution)/shard_map/ppermute | solution.py:175
  1.6 32.4 %collective-permute-start.7 = (f32[2,16,64]{2,1,0:T(8,128)}, f32[2,16,64]{2,1,0:T(8,128)S(1)}, u32[]{:S(2)}, u32[]{:S(2)}) collective-permute-start(f32[2,16,64]{2,1,0:T(8,128)} %param.6), channel_id=1, source_target_pairs={{0,96},{32,0},{64,32},{96,64},{1,97},{33,1},{65,33},{97,65},{2,98}... | collective-permute-start | bytes 24584 | tf_op jit(solution)/shard_map/ppermute | solution.py:175
  2.0 31.8 %collective-permute-start.6 = (f32[2,16,64]{2,1,0:T(8,128)}, f32[2,16,64]{2,1,0:T(8,128)S(1)}, u32[]{:S(2)}, u32[]{:S(2)}) collective-permute-start(f32[2,16,64]{2,1,0:T(8,128)} %param.6), channel_id=1, source_target_pairs={{0,64},{32,96},{64,0},{96,32},{1,65},{33,97},{65,1},{97,33},{2,66}... | collective-permute-start | bytes 24584 | tf_op jit(solution)/shard_map/ppermute | solution.py:175
  5.2 6.5 %collective-permute-start = (f32[1,64,128]{2,1,0:T(8,128)S(1)}, f32[1,64,128]{2,1,0:T(8,128)S(1)}, u32[]{:S(2)}, u32[]{:S(2)}) collective-permute-start(f32[1,64,128]{2,1,0:T(8,128)S(1)} %copy.53), channel_id=1, source_target_pairs={{0,16},{1,17},{2,18},{3,19},{4,20},{5,21},{6,22},{7,23},{8,24},{9,... | collective-permute-start | bytes 98312 | tf_op jit(solution)/shard_map/ppermute | solution.py:144
  11.7 4.3 %collective-permute-start.1 = (f32[2,64,128]{2,1,0:T(8,128)S(1)}, f32[2,64,128]{2,1,0:T(8,128)S(1)}, u32[]{:S(2)}, u32[]{:S(2)}) collective-permute-start(f32[2,64,128]{2,1,0:T(8,128)S(1)} %pad_maximum_fusion.3), channel_id=1, source_target_pairs={{0,8},{1,9},{2,10},{3,11},{4,12},{5,13},{6,14},{7,15},{8,0},{9,1},... | collective-permute-start | bytes 196616 | tf_op jit(solution)/shard_map/ppermute | solution.py:144
  16.1 7.5 %collective-permute-start.2 = (f32[4,64,128]{2,1,0:T(8,128)S(1)}, f32[4,64,128]{2,1,0:T(8,128)S(1)}, u32[]{:S(2)}, u32[]{:S(2)}) collective-permute-start(f32[4,64,128]{2,1,0:T(8,128)S(1)} %pad_maximum_fusion.2), channel_id=1, source_target_pairs={{0,4},{1,5},{2,6},{3,7},{4,0},{5,1},{6,2},{7,3},{8,12},{9,13},{10,... | collective-permute-start | bytes 393224 | tf_op jit(solution)/shard_map/ppermute | solution.py:144
  23.6 6.5 %collective-permute-start.3 = (f32[8,64,128]{2,1,0:T(8,128)S(1)}, f32[8,64,128]{2,1,0:T(8,128)S(1)}, u32[]{:S(2)}, u32[]{:S(2)}) collective-permute-start(f32[8,64,128]{2,1,0:T(8,128)S(1)} %pad_maximum_fusion.1), channel_id=1, source_target_pairs={{0,2},{1,3},{2,0},{3,1},{4,6},{5,7},{6,4},{7,5},{8,10},{9,11},{10,... | collective-permute-start | bytes 786440 | tf_op jit(solution)/shard_map/ppermute | solution.py:144
  30.8 5.5 %collective-permute-start.4 = (f32[16,64,128]{2,1,0:T(8,128)}, f32[16,64,128]{2,1,0:T(8,128)S(1)}, u32[]{:S(2)}, u32[]{:S(2)}) collective-permute-start(f32[16,64,128]{2,1,0:T(8,128)} %constant_dynamic-update-slice_fusion.near_ref), channel_id=1, source_target_pairs={{0,1},{1,0},{2,3},{3,2},{4,5},{5,4},{6,7},{7,6},{8,9},{9,8},{10,11... | collective-permute-start | bytes 1572872 | tf_op jit(solution)/shard_map/ppermute | solution.py:144
  36.3 35.1 %copy-start = (f32[16,64,128]{2,1,0:T(8,128)}, f32[16,64,128]{2,1,0:T(8,128)S(1)}, u32[]{:S(2)}) copy-start(f32[16,64,128]{2,1,0:T(8,128)S(1)} %collective-permute-done.4.far_ref) | copy-start | bytes 1572868
  39.3 28.2 %collective-permute-start.10 = (f32[2,8,64,64]{3,1,2,0:T(8,128)S(1)}, f32[2,8,64,64]{3,1,2,0:T(8,128)S(1)}, u32[]{:S(2)}, u32[]{:S(2)}) collective-permute-start(f32[2,8,64,64]{3,1,2,0:T(8,128)S(1)} %convolution_add_fusion), channel_id=1, source_target_pairs={{0,64},{1,65},{2,66},{3,67},{4,68},{5,69},{6,70},{7,71},{40,104},{... | collective-permute-start | bytes 786440 | tf_op jit(solution)/shard_map/ppermute | solution.py:205
  40.0 27.5 %collective-permute-start.11 = (f32[2,8,64,64]{3,1,2,0:T(8,128)S(1)}, f32[2,8,64,64]{3,1,2,0:T(8,128)S(1)}, u32[]{:S(2)}, u32[]{:S(2)}) collective-permute-start(f32[2,8,64,64]{3,1,2,0:T(8,128)S(1)} %convolution_add_fusion), channel_id=1, source_target_pairs={{0,96},{1,97},{2,98},{3,99},{4,100},{5,101},{6,102},{7,103}} | collective-permute-start | bytes 786440 | tf_op jit(solution)/shard_map/ppermute | solution.py:205
  42.2 20.1 %collective-permute-start.8 = (f32[8,64,64]{2,0,1:T(8,128)S(1)}, f32[8,64,64]{2,0,1:T(8,128)S(1)}, u32[]{:S(2)}, u32[]{:S(2)}) collective-permute-start(f32[8,64,64]{2,0,1:T(8,128)S(1)} %get-tuple-element.17), channel_id=1, source_target_pairs={{0,32},{1,33},{2,34},{3,35},{4,36},{5,37},{6,38},{7,39},{40,72},{4... | collective-permute-start | bytes 393224 | tf_op jit(solution)/shard_map/ppermute | solution.py:205
  43.5 24.0 %collective-permute-start.9 = (f32[8,64,64]{2,0,1:T(8,128)S(1)}, f32[8,64,64]{2,0,1:T(8,128)S(1)}, u32[]{:S(2)}, u32[]{:S(2)}) collective-permute-start(f32[8,64,64]{2,0,1:T(8,128)S(1)} %get-tuple-element.18), channel_id=1, source_target_pairs={{0,32},{1,33},{2,34},{3,35},{4,36},{5,37},{6,38},{7,39},{40,72},{4... | collective-permute-start | bytes 393224 | tf_op jit(solution)/shard_map/ppermute | solution.py:205

commit v10 on v9

--- a/solution.py
+++ b/solution.py
@@ -139,12 +139,14 @@
 def doubling_gather(block, axis, count):
     bits = count.bit_length() - 1
     spread = [0]
+    first = None
     for bit in reversed(range(bits)):
         mask = 1 << bit
         other = lax.ppermute(block, axis, [(i, i ^ mask) for i in range(count)])
+        first = other if first is None else first
         spread = spread + [s ^ mask for s in spread]
         if bit == 0:
-            return block, other, spread
+            return block, other, spread, first
         block = jnp.concatenate([block, other], axis=0)
 
 
@@ -165,7 +167,8 @@
     row_count = lax.axis_size("prow")
 
     local = jnp.transpose(panel_rows, (2, 0, 1)).reshape(width, 2 * width)
-    near, far, spread = doubling_gather(local[None], "pcol", col_count)
+    near, far, spread, first = doubling_gather(local[None], "pcol", col_count)
+    first, diag_blocks = lax.optimization_barrier((first, diag_blocks))
     half = near.shape[0]
     child_at = jnp.bitwise_xor(col_index, jnp.asarray(spread, jnp.int32))
     slot_of = jnp.bitwise_xor(col_index, jnp.arange(col_count, dtype=jnp.int32))

time: 83.6 us -> 82.1 us (0.982)
  waiting for transfers between devices: 24.4 us -> 22.2 us
    ppermute x4, waiting for transfers between devices: 13.3 us -> 12 us  [send(): lax.ppermute(value, ('prow', 'pcol'), [(owner[c] * col_count + c, (owner[...]
    ppermute x5, waiting for transfers between devices: 11 us -> 10.2 us  [doubling_gather(): other = lax.ppermute(block, axis, [(i, i ^ mask) for i in range(count)])]
  transfers between devices with their start and end apart: 12 -> 12, of which waited for: 5 -> 5; matrix products, arithmetic and copies ran while one was open for 19% -> 18% of each run, Pallas kernels for 10% -> 10%
where the time goes in v10:
time: 82.1 us; the launch traced here: 81.5 us
  waiting for transfers between devices  22.2 us (27%)
  Pallas kernels  19.6 us (24%)
  starting transfers between devices  16.4 us (20%)
  local copies, waits for them, and re-layouts  13.4 us (16%)
  other arithmetic  5.51 us (7%)
  matrix products  4.01 us (5%)
    ppermute x4, waiting for transfers between devices, send(): lax.ppermute(value, ('prow', 'pcol'), [(owner[c] * col_count + c, (owner[...  12 us
    pallas_call x1, Pallas kernels, apply_update(): pl.pallas_call(kernel, out_shape=jax.ShapeDtypeStruct(front.shape, front....  11.6 us
    ppermute x5, waiting for transfers between devices, doubling_gather(): other = lax.ppermute(block, axis, [(i, i ^ mask) for i in range(count)])  10.2 us
    pallas_call x1, Pallas kernels, invert_spd(): pl.pallas_call(inverse_kernel, out_shape=jax.ShapeDtypeStruct(matrix.shap...  8.03 us
    ppermute x5, starting transfers between devices, doubling_gather(): other = lax.ppermute(block, axis, [(i, i ^ mask) for i in range(count)])  7.39 us
    ppermute x3, starting transfers between devices, per_device(): lax.ppermute(diag_blocks, 'prow', [(i, (i + k) % row_count) for i in rang...  5 us
    ppermute x4, starting transfers between devices, send(): lax.ppermute(value, ('prow', 'pcol'), [(owner[c] * col_count + c, (owner[...  3.97 us
    unnamed x9, local copies, waits for them, and re-layouts  3.41 us
  transfers between devices with their start and end apart: 12, of which 5 were waited for; matrix products, arithmetic and copies ran while one was open for 18% of the time, Pallas kernels for 10%

profile of v10, /device:TPU:14, one launch (start us, length us, event | category | flops | bytes accessed | tf_op | source)
XLA Modules:
  0.0 81.5 jit_solution(1095271569726286225)
XLA Ops:
  0.0 0.9 %copy.53 = f32[1,64,128]{2,1,0:T(8,128)S(1)} copy(f32[1,64,128]{1,2,0:T(8,128)} %bitcast.49) | data formatting | bytes 65536 | tf_op jit(solution)/shard_map/broadcast_in_dim;reshape | solution.py:170
  0.9 4.0 %collective-permute-start = (f32[1,64,128]{2,1,0:T(8,128)S(1)}, f32[1,64,128]{2,1,0:T(8,128)S(1)}, u32[]{:S(2)}, u32[]{:S(2)}) collective-permute-start(f32[1,64,128]{2,1,0:T(8,128)S(1)} %copy.53), channel_id=1, source_target_pairs={{0,16},{1,17},{2,18},{3,19},{4,20},{5,21},{6,22},{7,23},{8,24},{9,... | collective-permute-start | bytes 98312 | tf_op jit(solution)/shard_map/ppermute | solution.py:145
  4.9 0.7 constant_dynamic-slice_fusion
  5.8 0.8 compare_reduce_fusion
  6.6 0.7 broadcast_xor_fusion
  7.4 1.1 %collective-permute-start.1 = (f32[2,64,128]{2,1,0:T(8,128)S(1)}, f32[2,64,128]{2,1,0:T(8,128)S(1)}, u32[]{:S(2)}, u32[]{:S(2)}) collective-permute-start(f32[2,64,128]{2,1,0:T(8,128)S(1)} %pad_maximum_fusion.3), channel_id=1, source_target_pairs={{0,8},{1,9},{2,10},{3,11},{4,12},{5,13},{6,14},{7,15},{8,0},{9,1},... | collective-permute-start | bytes 196616 | tf_op jit(solution)/shard_map/ppermute | solution.py:145
  8.5 3.2 %collective-permute-done.1 = f32[2,64,128]{2,1,0:T(8,128)S(1)} collective-permute-done((f32[2,64,128]{2,1,0:T(8,128)S(1)}, f32[2,64,128]{2,1,0:T(8,128)S(1)}, u32[]{:S(2)}, u32[]{:S(2)}) %collective-permute-start.1) | collective-permute-done | bytes 65568 | tf_op jit(solution)/shard_map/ppermute | solution.py:145
  11.8 1.5 %collective-permute-start.2 = (f32[4,64,128]{2,1,0:T(8,128)S(1)}, f32[4,64,128]{2,1,0:T(8,128)S(1)}, u32[]{:S(2)}, u32[]{:S(2)}) collective-permute-start(f32[4,64,128]{2,1,0:T(8,128)S(1)} %pad_maximum_fusion.2), channel_id=1, source_target_pairs={{0,4},{1,5},{2,6},{3,7},{4,0},{5,1},{6,2},{7,3},{8,12},{9,13},{10,... | collective-permute-start | bytes 393224 | tf_op jit(solution)/shard_map/ppermute | solution.py:145
  13.3 1.4 %gather_fusion = s32[32]{0:T(128)S(1)} fusion(s32[32]{0:T(128)} %constant.101.clone, s32[1024]{0:T(1024)S(1)} %pad_clamp_fusion.1), kind=kCustom, calls=%fused_computation | custom fusion | bytes 384 | tf_op jit(solution)/shard_map/jit(_take)/gather | solution.py:175
  15.2 3.2 %collective-permute-done.2 = f32[4,64,128]{2,1,0:T(8,128)S(1)} collective-permute-done((f32[4,64,128]{2,1,0:T(8,128)S(1)}, f32[4,64,128]{2,1,0:T(8,128)S(1)}, u32[]{:S(2)}, u32[]{:S(2)}) %collective-permute-start.2) | collective-permute-done | bytes 131104 | tf_op jit(solution)/shard_map/ppermute | solution.py:145
  18.5 0.9 %collective-permute-start.3 = (f32[8,64,128]{2,1,0:T(8,128)S(1)}, f32[8,64,128]{2,1,0:T(8,128)S(1)}, u32[]{:S(2)}, u32[]{:S(2)}) collective-permute-start(f32[8,64,128]{2,1,0:T(8,128)S(1)} %pad_maximum_fusion.1), channel_id=1, source_target_pairs={{0,2},{1,3},{2,0},{3,1},{4,6},{5,7},{6,4},{7,5},{8,10},{9,11},{10,... | collective-permute-start | bytes 786440 | tf_op jit(solution)/shard_map/ppermute | solution.py:145
  20.6 0.6 constant_dynamic-update-slice_fusion.1
  21.2 3.7 %collective-permute-done.3 = f32[8,64,128]{2,1,0:T(8,128)S(1)} collective-permute-done((f32[8,64,128]{2,1,0:T(8,128)S(1)}, f32[8,64,128]{2,1,0:T(8,128)S(1)}, u32[]{:S(2)}, u32[]{:S(2)}) %collective-permute-start.3) | collective-permute-done | bytes 262176 | tf_op jit(solution)/shard_map/ppermute | solution.py:145
  24.9 0.7 constant_dynamic-update-slice_fusion.near_ref
  26.2 2.6 %collective-permute-start.6 = (f32[2,16,64]{2,1,0:T(8,128)}, f32[2,16,64]{2,1,0:T(8,128)S(1)}, u32[]{:S(2)}, u32[]{:S(2)}) collective-permute-start(f32[2,16,64]{2,1,0:T(8,128)} %param.6), channel_id=1, source_target_pairs={{0,64},{32,96},{64,0},{96,32},{1,65},{33,97},{65,1},{97,33},{2,66}... | collective-permute-start | bytes 24584 | tf_op jit(solution)/shard_map/ppermute | solution.py:178
  28.8 1.9 %collective-permute-start.5 = (f32[2,16,64]{2,1,0:T(8,128)}, f32[2,16,64]{2,1,0:T(8,128)S(1)}, u32[]{:S(2)}, u32[]{:S(2)}) collective-permute-start(f32[2,16,64]{2,1,0:T(8,128)} %param.6), channel_id=1, source_target_pairs={{0,32},{32,64},{64,96},{96,0},{1,33},{33,65},{65,97},{97,1},{2,34}... | collective-permute-start | bytes 24584 | tf_op jit(solution)/shard_map/ppermute | solution.py:178
  30.7 0.7 pad_add_fusion.place_ref
  31.3 0.9 %copy.35 = f32[2,64,64]{1,2,0:T(8,128)S(1)} copy(f32[2,64,64]{2,1,0:T(8,128)} %param.7) | data formatting | bytes 65536 | tf_op args[1]
  32.9 0.7 broadcast_in_dim.122
  36.7 1.1 %fusion = f32[2,8,64,64]{3,1,2,0:T(8,128)S(1)} fusion(f32[16,64,2,64]{3,2,1,0:T(2,128)S(1)} %reshape.86, pred[2,8,32]{2,1,0:T(8,128)(4,1)S(1)} %compare_and_fusion), kind=kOutput, calls=%fused_computation.3 | convolution fusion | flops 12582912 | bytes 786944 | tf_op jit(solution)/shard_map/pjk,kbpa->pjba/dot_general | solution.py:195
  39.1 0.7 collective-permute-start.10
  39.8 0.7 collective-permute-start.11
  40.6 1.2 %gather_fusion.1 = s32[128]{0:T(128)S(1)} fusion(s32[32]{0:T(128)S(1)} %and_select_fusion, s32[1024]{0:T(1024)S(1)} %pad_clamp_fusion), kind=kCustom, calls=%fused_computation.1 | custom fusion | bytes 1536 | tf_op jit(solution)/shard_map/jit(_take)/gather | solution.py:204
  42.1 1.3 %collective-permute-start.8 = (f32[8,64,64]{2,0,1:T(8,128)S(1)}, f32[8,64,64]{2,0,1:T(8,128)S(1)}, u32[]{:S(2)}, u32[]{:S(2)}) collective-permute-start(f32[8,64,64]{2,0,1:T(8,128)S(1)} %get-tuple-element.19), channel_id=1, source_target_pairs={{0,32},{1,33},{2,34},{3,35},{4,36},{5,37},{6,38},{7,39},{40,72},{4... | collective-permute-start | bytes 393224 | tf_op jit(solution)/shard_map/ppermute | solution.py:208
  43.4 1.3 %collective-permute-start.9 = (f32[8,64,64]{2,0,1:T(8,128)S(1)}, f32[8,64,64]{2,0,1:T(8,128)S(1)}, u32[]{:S(2)}, u32[]{:S(2)}) collective-permute-start(f32[8,64,64]{2,0,1:T(8,128)S(1)} %get-tuple-element.20), channel_id=1, source_target_pairs={{0,32},{1,33},{2,34},{3,35},{4,36},{5,37},{6,38},{7,39},{40,72},{4... | collective-permute-start | bytes 393224 | tf_op jit(solution)/shard_map/ppermute | solution.py:208
  44.7 0.7 pad_maximum_fusion.4.system_ref
  45.4 8.0 %shard_map.64 = f32[2,64,64]{2,1,0:T(8,128)} custom-call(f32[2,64,128]{2,1,0:T(8,128)} %pad_maximum_fusion.4.system_ref), custom_call_target="tpu_custom_call" | custom-call | flops 4194304 | bytes 98304 | tf_op jit(solution)/shard_map/pallas_call | solution.py:127
  54.0 8.2 %collective-permute-done.8 = f32[8,64,64]{2,0,1:T(8,128)S(1)} collective-permute-done((f32[8,64,64]{2,0,1:T(8,128)S(1)}, f32[8,64,64]{2,0,1:T(8,128)S(1)}, u32[]{:S(2)}, u32[]{:S(2)}) %collective-permute-start.8) | collective-permute-done | bytes 131104 | tf_op jit(solution)/shard_map/ppermute | solution.py:208
  62.2 3.8 %collective-permute-done.9 = f32[8,64,64]{2,0,1:T(8,128)S(1)} collective-permute-done((f32[8,64,64]{2,0,1:T(8,128)S(1)}, f32[8,64,64]{2,0,1:T(8,128)S(1)}, u32[]{:S(2)}, u32[]{:S(2)}) %collective-permute-start.9) | collective-permute-done | bytes 131104 | tf_op jit(solution)/shard_map/ppermute | solution.py:208
  66.1 2.5 %fusion.3 = f32[2,64,8,64]{3,1,2,0:T(8,128)S(1)} fusion(f32[2,8,64,64]{3,1,2,0:T(8,128)S(1)} %fusion.2, f32[2,64,64]{2,1,0:T(8,128)} %shard_map.64), kind=kOutput, calls=%fused_computation.7 | convolution fusion | flops 50331648 | bytes 557056 | tf_op jit(solution)/shard_map/pxa,pjba->pxjb/dot_general | solution.py:215
  69.1 0.8 pad_maximum_fusion.stack_ref
  69.9 11.6 %shard_map.65 = f32[4096,512]{1,0:T(8,128)} custom-call(s32[2,64]{1,0:T(2,128)} %compare_select_fusion.5.table_ref, s32[2]{0:T(128)} %pad_add_fusion.place_ref, f32[16,64,128]{2,1,0:T(8,128)} %constant_dynamic-update-slice_fusion.near_ref, f32[16,64,128]{2,1,0:T(8,128)} %copy-done, bf16[384,512]{1,0:T(8,128)(2,1)} %pad_maximum_fusion.stack_ref, ...), custom_call_target="tpu_custom_call" | custom-call | flops 1610612736 | bytes 18219008 | tf_op jit(solution)/shard_map/pallas_call | solution.py:78
  (72 shorter events, 9.1 us)
Async XLA Ops:
  0.0 38.3 %copy-start.1 = (s32[2,128]{1,0:T(2,128)S(1)}, s32[2,128]{1,0:T(2,128)}, u32[]{:S(2)}) copy-start(s32[2,128]{1,0:T(2,128)} %param.8) | copy-start | bytes 3076
  0.9 6.5 %collective-permute-start = (f32[1,64,128]{2,1,0:T(8,128)S(1)}, f32[1,64,128]{2,1,0:T(8,128)S(1)}, u32[]{:S(2)}, u32[]{:S(2)}) collective-permute-start(f32[1,64,128]{2,1,0:T(8,128)S(1)} %copy.53), channel_id=1, source_target_pairs={{0,16},{1,17},{2,18},{3,19},{4,20},{5,21},{6,22},{7,23},{8,24},{9,... | collective-permute-start | bytes 98312 | tf_op jit(solution)/shard_map/ppermute | solution.py:145
  7.4 4.3 %collective-permute-start.1 = (f32[2,64,128]{2,1,0:T(8,128)S(1)}, f32[2,64,128]{2,1,0:T(8,128)S(1)}, u32[]{:S(2)}, u32[]{:S(2)}) collective-permute-start(f32[2,64,128]{2,1,0:T(8,128)S(1)} %pad_maximum_fusion.3), channel_id=1, source_target_pairs={{0,8},{1,9},{2,10},{3,11},{4,12},{5,13},{6,14},{7,15},{8,0},{9,1},... | collective-permute-start | bytes 196616 | tf_op jit(solution)/shard_map/ppermute | solution.py:145
  11.8 6.7 %collective-permute-start.2 = (f32[4,64,128]{2,1,0:T(8,128)S(1)}, f32[4,64,128]{2,1,0:T(8,128)S(1)}, u32[]{:S(2)}, u32[]{:S(2)}) collective-permute-start(f32[4,64,128]{2,1,0:T(8,128)S(1)} %pad_maximum_fusion.2), channel_id=1, source_target_pairs={{0,4},{1,5},{2,6},{3,7},{4,0},{5,1},{6,2},{7,3},{8,12},{9,13},{10,... | collective-permute-start | bytes 393224 | tf_op jit(solution)/shard_map/ppermute | solution.py:145
  18.5 6.5 %collective-permute-start.3 = (f32[8,64,128]{2,1,0:T(8,128)S(1)}, f32[8,64,128]{2,1,0:T(8,128)S(1)}, u32[]{:S(2)}, u32[]{:S(2)}) collective-permute-start(f32[8,64,128]{2,1,0:T(8,128)S(1)} %pad_maximum_fusion.1), channel_id=1, source_target_pairs={{0,2},{1,3},{2,0},{3,1},{4,6},{5,7},{6,4},{7,5},{8,10},{9,11},{10,... | collective-permute-start | bytes 786440 | tf_op jit(solution)/shard_map/ppermute | solution.py:145
  25.6 10.5 %collective-permute-start.4 = (f32[16,64,128]{2,1,0:T(8,128)}, f32[16,64,128]{2,1,0:T(8,128)S(1)}, u32[]{:S(2)}, u32[]{:S(2)}) collective-permute-start(f32[16,64,128]{2,1,0:T(8,128)} %constant_dynamic-update-slice_fusion.near_ref), channel_id=1, source_target_pairs={{0,1},{1,0},{2,3},{3,2},{4,5},{5,4},{6,7},{7,6},{8,9},{9,8},{10,11... | collective-permute-start | bytes 1572872 | tf_op jit(solution)/shard_map/ppermute | solution.py:145
  25.7 8.4 %collective-permute-start.7 = (f32[2,16,64]{2,1,0:T(8,128)}, f32[2,16,64]{2,1,0:T(8,128)S(1)}, u32[]{:S(2)}, u32[]{:S(2)}) collective-permute-start(f32[2,16,64]{2,1,0:T(8,128)} %param.6), channel_id=1, source_target_pairs={{0,96},{32,0},{64,32},{96,64},{1,97},{33,1},{65,33},{97,65},{2,98}... | collective-permute-start | bytes 24584 | tf_op jit(solution)/shard_map/ppermute | solution.py:178
  26.2 7.8 %collective-permute-start.6 = (f32[2,16,64]{2,1,0:T(8,128)}, f32[2,16,64]{2,1,0:T(8,128)S(1)}, u32[]{:S(2)}, u32[]{:S(2)}) collective-permute-start(f32[2,16,64]{2,1,0:T(8,128)} %param.6), channel_id=1, source_target_pairs={{0,64},{32,96},{64,0},{96,32},{1,65},{33,97},{65,1},{97,33},{2,66}... | collective-permute-start | bytes 24584 | tf_op jit(solution)/shard_map/ppermute | solution.py:178
  28.8 5.1 %collective-permute-start.5 = (f32[2,16,64]{2,1,0:T(8,128)}, f32[2,16,64]{2,1,0:T(8,128)S(1)}, u32[]{:S(2)}, u32[]{:S(2)}) collective-permute-start(f32[2,16,64]{2,1,0:T(8,128)} %param.6), channel_id=1, source_target_pairs={{0,32},{32,64},{64,96},{96,0},{1,33},{33,65},{65,97},{97,1},{2,34}... | collective-permute-start | bytes 24584 | tf_op jit(solution)/shard_map/ppermute | solution.py:178
  36.1 33.8 %copy-start = (f32[16,64,128]{2,1,0:T(8,128)}, f32[16,64,128]{2,1,0:T(8,128)S(1)}, u32[]{:S(2)}) copy-start(f32[16,64,128]{2,1,0:T(8,128)S(1)} %collective-permute-done.4.far_ref) | copy-start | bytes 1572868
  39.1 26.9 %collective-permute-start.10 = (f32[2,8,64,64]{3,1,2,0:T(8,128)S(1)}, f32[2,8,64,64]{3,1,2,0:T(8,128)S(1)}, u32[]{:S(2)}, u32[]{:S(2)}) collective-permute-start(f32[2,8,64,64]{3,1,2,0:T(8,128)S(1)} %convolution_add_fusion), channel_id=1, source_target_pairs={{0,64},{1,65},{2,66},{3,67},{4,68},{5,69},{6,70},{7,71},{40,104},{... | collective-permute-start | bytes 786440 | tf_op jit(solution)/shard_map/ppermute | solution.py:208
  39.8 26.2 %collective-permute-start.11 = (f32[2,8,64,64]{3,1,2,0:T(8,128)S(1)}, f32[2,8,64,64]{3,1,2,0:T(8,128)S(1)}, u32[]{:S(2)}, u32[]{:S(2)}) collective-permute-start(f32[2,8,64,64]{3,1,2,0:T(8,128)S(1)} %convolution_add_fusion), channel_id=1, source_target_pairs={{0,96},{1,97},{2,98},{3,99},{4,100},{5,101},{6,102},{7,103}} | collective-permute-start | bytes 786440 | tf_op jit(solution)/shard_map/ppermute | solution.py:208
  42.1 20.1 %collective-permute-start.8 = (f32[8,64,64]{2,0,1:T(8,128)S(1)}, f32[8,64,64]{2,0,1:T(8,128)S(1)}, u32[]{:S(2)}, u32[]{:S(2)}) collective-permute-start(f32[8,64,64]{2,0,1:T(8,128)S(1)} %get-tuple-element.19), channel_id=1, source_target_pairs={{0,32},{1,33},{2,34},{3,35},{4,36},{5,37},{6,38},{7,39},{40,72},{4... | collective-permute-start | bytes 393224 | tf_op jit(solution)/shard_map/ppermute | solution.py:208
  43.4 22.7 %collective-permute-start.9 = (f32[8,64,64]{2,0,1:T(8,128)S(1)}, f32[8,64,64]{2,0,1:T(8,128)S(1)}, u32[]{:S(2)}, u32[]{:S(2)}) collective-permute-start(f32[8,64,64]{2,0,1:T(8,128)S(1)} %get-tuple-element.20), channel_id=1, source_target_pairs={{0,32},{1,33},{2,34},{3,35},{4,36},{5,37},{6,38},{7,39},{40,72},{4... | collective-permute-start | bytes 393224 | tf_op jit(solution)/shard_map/ppermute | solution.py:208

commit v11 on v10

--- a/solution.py
+++ b/solution.py
@@ -9,7 +9,7 @@
 from jax.sharding import PartitionSpec as P
 
 HIGHEST = lax.Precision.HIGHEST
-TILE_ROWS = 512
+TILE_ROWS = 256
 
 
 def split_bf16(value):

time: 82.1 us -> 85.7 us (1.044)
  Pallas kernels: 19.6 us -> 23 us
    pallas_call x1, Pallas kernels: 11.6 us -> 15 us  [apply_update(): pl.pallas_call(kernel, out_shape=jax.ShapeDtypeStruct(front.shape, front....]
  transfers between devices with their start and end apart: 12 -> 12, of which waited for: 5 -> 5; matrix products, arithmetic and copies ran while one was open for 18% -> 17% of each run, Pallas kernels for 10% -> 9%
where the time goes in v11:
time: 85.7 us; the launch traced here: 84.9 us
  Pallas kernels  23 us (27%)
  waiting for transfers between devices  22.2 us (26%)
  starting transfers between devices  16.4 us (19%)
  local copies, waits for them, and re-layouts  13.4 us (16%)
  other arithmetic  5.51 us (6%)
  matrix products  4.01 us (5%)
    pallas_call x1, Pallas kernels, apply_update(): pl.pallas_call(kernel, out_shape=jax.ShapeDtypeStruct(front.shape, front....  15 us
    ppermute x4, waiting for transfers between devices, send(): lax.ppermute(value, ('prow', 'pcol'), [(owner[c] * col_count + c, (owner[...  12 us
    ppermute x5, waiting for transfers between devices, doubling_gather(): other = lax.ppermute(block, axis, [(i, i ^ mask) for i in range(count)])  10.2 us
    pallas_call x1, Pallas kernels, invert_spd(): pl.pallas_call(inverse_kernel, out_shape=jax.ShapeDtypeStruct(matrix.shap...  8.03 us
    ppermute x5, starting transfers between devices, doubling_gather(): other = lax.ppermute(block, axis, [(i, i ^ mask) for i in range(count)])  7.39 us
    ppermute x3, starting transfers between devices, per_device(): lax.ppermute(diag_blocks, 'prow', [(i, (i + k) % row_count) for i in rang...  5 us
    ppermute x4, starting transfers between devices, send(): lax.ppermute(value, ('prow', 'pcol'), [(owner[c] * col_count + c, (owner[...  3.97 us
    unnamed x9, local copies, waits for them, and re-layouts  3.41 us
  transfers between devices with their start and end apart: 12, of which 5 were waited for; matrix products, arithmetic and copies ran while one was open for 17% of the time, Pallas kernels for 9%

profile of v11, /device:TPU:14, one launch (start us, length us, event | category | flops | bytes accessed | tf_op | source)
XLA Modules:
  0.0 84.9 jit_solution(6882388958368407484)
XLA Ops:
  0.0 0.9 %copy.53 = f32[1,64,128]{2,1,0:T(8,128)S(1)} copy(f32[1,64,128]{1,2,0:T(8,128)} %bitcast.49) | data formatting | bytes 65536 | tf_op jit(solution)/shard_map/broadcast_in_dim;reshape | solution.py:170
  0.9 4.0 %collective-permute-start = (f32[1,64,128]{2,1,0:T(8,128)S(1)}, f32[1,64,128]{2,1,0:T(8,128)S(1)}, u32[]{:S(2)}, u32[]{:S(2)}) collective-permute-start(f32[1,64,128]{2,1,0:T(8,128)S(1)} %copy.53), channel_id=1, source_target_pairs={{0,16},{1,17},{2,18},{3,19},{4,20},{5,21},{6,22},{7,23},{8,24},{9,... | collective-permute-start | bytes 98312 | tf_op jit(solution)/shard_map/ppermute | solution.py:145
  4.9 0.7 constant_dynamic-slice_fusion
  5.8 0.8 compare_reduce_fusion
  6.6 0.7 broadcast_xor_fusion
  7.4 1.1 %collective-permute-start.1 = (f32[2,64,128]{2,1,0:T(8,128)S(1)}, f32[2,64,128]{2,1,0:T(8,128)S(1)}, u32[]{:S(2)}, u32[]{:S(2)}) collective-permute-start(f32[2,64,128]{2,1,0:T(8,128)S(1)} %pad_maximum_fusion.3), channel_id=1, source_target_pairs={{0,8},{1,9},{2,10},{3,11},{4,12},{5,13},{6,14},{7,15},{8,0},{9,1},... | collective-permute-start | bytes 196616 | tf_op jit(solution)/shard_map/ppermute | solution.py:145
  8.5 3.2 %collective-permute-done.1 = f32[2,64,128]{2,1,0:T(8,128)S(1)} collective-permute-done((f32[2,64,128]{2,1,0:T(8,128)S(1)}, f32[2,64,128]{2,1,0:T(8,128)S(1)}, u32[]{:S(2)}, u32[]{:S(2)}) %collective-permute-start.1) | collective-permute-done | bytes 65568 | tf_op jit(solution)/shard_map/ppermute | solution.py:145
  11.8 1.5 %collective-permute-start.2 = (f32[4,64,128]{2,1,0:T(8,128)S(1)}, f32[4,64,128]{2,1,0:T(8,128)S(1)}, u32[]{:S(2)}, u32[]{:S(2)}) collective-permute-start(f32[4,64,128]{2,1,0:T(8,128)S(1)} %pad_maximum_fusion.2), channel_id=1, source_target_pairs={{0,4},{1,5},{2,6},{3,7},{4,0},{5,1},{6,2},{7,3},{8,12},{9,13},{10,... | collective-permute-start | bytes 393224 | tf_op jit(solution)/shard_map/ppermute | solution.py:145
  13.3 1.4 %gather_fusion = s32[32]{0:T(128)S(1)} fusion(s32[32]{0:T(128)} %constant.101.clone, s32[1024]{0:T(1024)S(1)} %pad_clamp_fusion.1), kind=kCustom, calls=%fused_computation | custom fusion | bytes 384 | tf_op jit(solution)/shard_map/jit(_take)/gather | solution.py:175
  15.2 3.2 %collective-permute-done.2 = f32[4,64,128]{2,1,0:T(8,128)S(1)} collective-permute-done((f32[4,64,128]{2,1,0:T(8,128)S(1)}, f32[4,64,128]{2,1,0:T(8,128)S(1)}, u32[]{:S(2)}, u32[]{:S(2)}) %collective-permute-start.2) | collective-permute-done | bytes 131104 | tf_op jit(solution)/shard_map/ppermute | solution.py:145
  18.5 0.9 %collective-permute-start.3 = (f32[8,64,128]{2,1,0:T(8,128)S(1)}, f32[8,64,128]{2,1,0:T(8,128)S(1)}, u32[]{:S(2)}, u32[]{:S(2)}) collective-permute-start(f32[8,64,128]{2,1,0:T(8,128)S(1)} %pad_maximum_fusion.1), channel_id=1, source_target_pairs={{0,2},{1,3},{2,0},{3,1},{4,6},{5,7},{6,4},{7,5},{8,10},{9,11},{10,... | collective-permute-start | bytes 786440 | tf_op jit(solution)/shard_map/ppermute | solution.py:145
  20.6 0.6 constant_dynamic-update-slice_fusion.1
  21.2 3.7 %collective-permute-done.3 = f32[8,64,128]{2,1,0:T(8,128)S(1)} collective-permute-done((f32[8,64,128]{2,1,0:T(8,128)S(1)}, f32[8,64,128]{2,1,0:T(8,128)S(1)}, u32[]{:S(2)}, u32[]{:S(2)}) %collective-permute-start.3) | collective-permute-done | bytes 262176 | tf_op jit(solution)/shard_map/ppermute | solution.py:145
  24.9 0.7 constant_dynamic-update-slice_fusion.near_ref
  26.2 2.6 %collective-permute-start.6 = (f32[2,16,64]{2,1,0:T(8,128)}, f32[2,16,64]{2,1,0:T(8,128)S(1)}, u32[]{:S(2)}, u32[]{:S(2)}) collective-permute-start(f32[2,16,64]{2,1,0:T(8,128)} %param.6), channel_id=1, source_target_pairs={{0,64},{32,96},{64,0},{96,32},{1,65},{33,97},{65,1},{97,33},{2,66}... | collective-permute-start | bytes 24584 | tf_op jit(solution)/shard_map/ppermute | solution.py:178
  28.8 1.9 %collective-permute-start.5 = (f32[2,16,64]{2,1,0:T(8,128)}, f32[2,16,64]{2,1,0:T(8,128)S(1)}, u32[]{:S(2)}, u32[]{:S(2)}) collective-permute-start(f32[2,16,64]{2,1,0:T(8,128)} %param.6), channel_id=1, source_target_pairs={{0,32},{32,64},{64,96},{96,0},{1,33},{33,65},{65,97},{97,1},{2,34}... | collective-permute-start | bytes 24584 | tf_op jit(solution)/shard_map/ppermute | solution.py:178
  30.7 0.7 pad_add_fusion.place_ref
  31.3 0.9 %copy.35 = f32[2,64,64]{1,2,0:T(8,128)S(1)} copy(f32[2,64,64]{2,1,0:T(8,128)} %param.7) | data formatting | bytes 65536 | tf_op args[1]
  32.9 0.7 broadcast_in_dim.122
  36.7 1.1 %fusion = f32[2,8,64,64]{3,1,2,0:T(8,128)S(1)} fusion(f32[16,64,2,64]{3,2,1,0:T(2,128)S(1)} %reshape.86, pred[2,8,32]{2,1,0:T(8,128)(4,1)S(1)} %compare_and_fusion), kind=kOutput, calls=%fused_computation.3 | convolution fusion | flops 12582912 | bytes 786944 | tf_op jit(solution)/shard_map/pjk,kbpa->pjba/dot_general | solution.py:195
  39.1 0.7 collective-permute-start.10
  39.8 0.7 collective-permute-start.11
  40.6 1.2 %gather_fusion.1 = s32[128]{0:T(128)S(1)} fusion(s32[32]{0:T(128)S(1)} %and_select_fusion, s32[1024]{0:T(1024)S(1)} %pad_clamp_fusion), kind=kCustom, calls=%fused_computation.1 | custom fusion | bytes 1536 | tf_op jit(solution)/shard_map/jit(_take)/gather | solution.py:204
  42.1 1.3 %collective-permute-start.8 = (f32[8,64,64]{2,0,1:T(8,128)S(1)}, f32[8,64,64]{2,0,1:T(8,128)S(1)}, u32[]{:S(2)}, u32[]{:S(2)}) collective-permute-start(f32[8,64,64]{2,0,1:T(8,128)S(1)} %get-tuple-element.19), channel_id=1, source_target_pairs={{0,32},{1,33},{2,34},{3,35},{4,36},{5,37},{6,38},{7,39},{40,72},{4... | collective-permute-start | bytes 393224 | tf_op jit(solution)/shard_map/ppermute | solution.py:208
  43.4 1.3 %collective-permute-start.9 = (f32[8,64,64]{2,0,1:T(8,128)S(1)}, f32[8,64,64]{2,0,1:T(8,128)S(1)}, u32[]{:S(2)}, u32[]{:S(2)}) collective-permute-start(f32[8,64,64]{2,0,1:T(8,128)S(1)} %get-tuple-element.20), channel_id=1, source_target_pairs={{0,32},{1,33},{2,34},{3,35},{4,36},{5,37},{6,38},{7,39},{40,72},{4... | collective-permute-start | bytes 393224 | tf_op jit(solution)/shard_map/ppermute | solution.py:208
  44.7 0.7 pad_maximum_fusion.4.system_ref
  45.4 8.0 %shard_map.64 = f32[2,64,64]{2,1,0:T(8,128)} custom-call(f32[2,64,128]{2,1,0:T(8,128)} %pad_maximum_fusion.4.system_ref), custom_call_target="tpu_custom_call" | custom-call | flops 4194304 | bytes 98304 | tf_op jit(solution)/shard_map/pallas_call | solution.py:127
  54.0 8.2 %collective-permute-done.8 = f32[8,64,64]{2,0,1:T(8,128)S(1)} collective-permute-done((f32[8,64,64]{2,0,1:T(8,128)S(1)}, f32[8,64,64]{2,0,1:T(8,128)S(1)}, u32[]{:S(2)}, u32[]{:S(2)}) %collective-permute-start.8) | collective-permute-done | bytes 131104 | tf_op jit(solution)/shard_map/ppermute | solution.py:208
  62.2 3.8 %collective-permute-done.9 = f32[8,64,64]{2,0,1:T(8,128)S(1)} collective-permute-done((f32[8,64,64]{2,0,1:T(8,128)S(1)}, f32[8,64,64]{2,0,1:T(8,128)S(1)}, u32[]{:S(2)}, u32[]{:S(2)}) %collective-permute-start.9) | collective-permute-done | bytes 131104 | tf_op jit(solution)/shard_map/ppermute | solution.py:208
  66.1 2.5 %fusion.3 = f32[2,64,8,64]{3,1,2,0:T(8,128)S(1)} fusion(f32[2,8,64,64]{3,1,2,0:T(8,128)S(1)} %fusion.2, f32[2,64,64]{2,1,0:T(8,128)} %shard_map.64), kind=kOutput, calls=%fused_computation.7 | convolution fusion | flops 50331648 | bytes 557056 | tf_op jit(solution)/shard_map/pxa,pjba->pxjb/dot_general | solution.py:215
  69.1 0.8 pad_maximum_fusion.stack_ref
  69.9 15.0 %shard_map.65 = f32[4096,512]{1,0:T(8,128)} custom-call(s32[2,64]{1,0:T(2,128)} %compare_select_fusion.5.table_ref, s32[2]{0:T(128)} %pad_add_fusion.place_ref, f32[16,64,128]{2,1,0:T(8,128)} %constant_dynamic-update-slice_fusion.near_ref, f32[16,64,128]{2,1,0:T(8,128)} %copy-done, bf16[384,512]{1,0:T(8,128)(2,1)} %pad_maximum_fusion.stack_ref, ...), custom_call_target="tpu_custom_call" | custom-call | flops 1610612736 | bytes 18219008 | tf_op jit(solution)/shard_map/pallas_call | solution.py:78
  (72 shorter events, 9.1 us)
Async XLA Ops:
  0.0 38.3 %copy-start.1 = (s32[2,128]{1,0:T(2,128)S(1)}, s32[2,128]{1,0:T(2,128)}, u32[]{:S(2)}) copy-start(s32[2,128]{1,0:T(2,128)} %param.8) | copy-start | bytes 3076
  0.9 6.5 %collective-permute-start = (f32[1,64,128]{2,1,0:T(8,128)S(1)}, f32[1,64,128]{2,1,0:T(8,128)S(1)}, u32[]{:S(2)}, u32[]{:S(2)}) collective-permute-start(f32[1,64,128]{2,1,0:T(8,128)S(1)} %copy.53), channel_id=1, source_target_pairs={{0,16},{1,17},{2,18},{3,19},{4,20},{5,21},{6,22},{7,23},{8,24},{9,... | collective-permute-start | bytes 98312 | tf_op jit(solution)/shard_map/ppermute | solution.py:145
  7.4 4.3 %collective-permute-start.1 = (f32[2,64,128]{2,1,0:T(8,128)S(1)}, f32[2,64,128]{2,1,0:T(8,128)S(1)}, u32[]{:S(2)}, u32[]{:S(2)}) collective-permute-start(f32[2,64,128]{2,1,0:T(8,128)S(1)} %pad_maximum_fusion.3), channel_id=1, source_target_pairs={{0,8},{1,9},{2,10},{3,11},{4,12},{5,13},{6,14},{7,15},{8,0},{9,1},... | collective-permute-start | bytes 196616 | tf_op jit(solution)/shard_map/ppermute | solution.py:145
  11.8 6.7 %collective-permute-start.2 = (f32[4,64,128]{2,1,0:T(8,128)S(1)}, f32[4,64,128]{2,1,0:T(8,128)S(1)}, u32[]{:S(2)}, u32[]{:S(2)}) collective-permute-start(f32[4,64,128]{2,1,0:T(8,128)S(1)} %pad_maximum_fusion.2), channel_id=1, source_target_pairs={{0,4},{1,5},{2,6},{3,7},{4,0},{5,1},{6,2},{7,3},{8,12},{9,13},{10,... | collective-permute-start | bytes 393224 | tf_op jit(solution)/shard_map/ppermute | solution.py:145
  18.5 6.5 %collective-permute-start.3 = (f32[8,64,128]{2,1,0:T(8,128)S(1)}, f32[8,64,128]{2,1,0:T(8,128)S(1)}, u32[]{:S(2)}, u32[]{:S(2)}) collective-permute-start(f32[8,64,128]{2,1,0:T(8,128)S(1)} %pad_maximum_fusion.1), channel_id=1, source_target_pairs={{0,2},{1,3},{2,0},{3,1},{4,6},{5,7},{6,4},{7,5},{8,10},{9,11},{10,... | collective-permute-start | bytes 786440 | tf_op jit(solution)/shard_map/ppermute | solution.py:145
  25.6 10.5 %collective-permute-start.4 = (f32[16,64,128]{2,1,0:T(8,128)}, f32[16,64,128]{2,1,0:T(8,128)S(1)}, u32[]{:S(2)}, u32[]{:S(2)}) collective-permute-start(f32[16,64,128]{2,1,0:T(8,128)} %constant_dynamic-update-slice_fusion.near_ref), channel_id=1, source_target_pairs={{0,1},{1,0},{2,3},{3,2},{4,5},{5,4},{6,7},{7,6},{8,9},{9,8},{10,11... | collective-permute-start | bytes 1572872 | tf_op jit(solution)/shard_map/ppermute | solution.py:145
  25.7 8.4 %collective-permute-start.7 = (f32[2,16,64]{2,1,0:T(8,128)}, f32[2,16,64]{2,1,0:T(8,128)S(1)}, u32[]{:S(2)}, u32[]{:S(2)}) collective-permute-start(f32[2,16,64]{2,1,0:T(8,128)} %param.6), channel_id=1, source_target_pairs={{0,96},{32,0},{64,32},{96,64},{1,97},{33,1},{65,33},{97,65},{2,98}... | collective-permute-start | bytes 24584 | tf_op jit(solution)/shard_map/ppermute | solution.py:178
  26.2 7.8 %collective-permute-start.6 = (f32[2,16,64]{2,1,0:T(8,128)}, f32[2,16,64]{2,1,0:T(8,128)S(1)}, u32[]{:S(2)}, u32[]{:S(2)}) collective-permute-start(f32[2,16,64]{2,1,0:T(8,128)} %param.6), channel_id=1, source_target_pairs={{0,64},{32,96},{64,0},{96,32},{1,65},{33,97},{65,1},{97,33},{2,66}... | collective-permute-start | bytes 24584 | tf_op jit(solution)/shard_map/ppermute | solution.py:178
  28.8 5.1 %collective-permute-start.5 = (f32[2,16,64]{2,1,0:T(8,128)}, f32[2,16,64]{2,1,0:T(8,128)S(1)}, u32[]{:S(2)}, u32[]{:S(2)}) collective-permute-start(f32[2,16,64]{2,1,0:T(8,128)} %param.6), channel_id=1, source_target_pairs={{0,32},{32,64},{64,96},{96,0},{1,33},{33,65},{65,97},{97,1},{2,34}... | collective-permute-start | bytes 24584 | tf_op jit(solution)/shard_map/ppermute | solution.py:178
  36.1 33.8 %copy-start = (f32[16,64,128]{2,1,0:T(8,128)}, f32[16,64,128]{2,1,0:T(8,128)S(1)}, u32[]{:S(2)}) copy-start(f32[16,64,128]{2,1,0:T(8,128)S(1)} %collective-permute-done.4.far_ref) | copy-start | bytes 1572868
  39.1 26.9 %collective-permute-start.10 = (f32[2,8,64,64]{3,1,2,0:T(8,128)S(1)}, f32[2,8,64,64]{3,1,2,0:T(8,128)S(1)}, u32[]{:S(2)}, u32[]{:S(2)}) collective-permute-start(f32[2,8,64,64]{3,1,2,0:T(8,128)S(1)} %convolution_add_fusion), channel_id=1, source_target_pairs={{0,64},{1,65},{2,66},{3,67},{4,68},{5,69},{6,70},{7,71},{40,104},{... | collective-permute-start | bytes 786440 | tf_op jit(solution)/shard_map/ppermute | solution.py:208
  39.8 26.2 %collective-permute-start.11 = (f32[2,8,64,64]{3,1,2,0:T(8,128)S(1)}, f32[2,8,64,64]{3,1,2,0:T(8,128)S(1)}, u32[]{:S(2)}, u32[]{:S(2)}) collective-permute-start(f32[2,8,64,64]{3,1,2,0:T(8,128)S(1)} %convolution_add_fusion), channel_id=1, source_target_pairs={{0,96},{1,97},{2,98},{3,99},{4,100},{5,101},{6,102},{7,103}} | collective-permute-start | bytes 786440 | tf_op jit(solution)/shard_map/ppermute | solution.py:208
  42.1 20.1 %collective-permute-start.8 = (f32[8,64,64]{2,0,1:T(8,128)S(1)}, f32[8,64,64]{2,0,1:T(8,128)S(1)}, u32[]{:S(2)}, u32[]{:S(2)}) collective-permute-start(f32[8,64,64]{2,0,1:T(8,128)S(1)} %get-tuple-element.19), channel_id=1, source_target_pairs={{0,32},{1,33},{2,34},{3,35},{4,36},{5,37},{6,38},{7,39},{40,72},{4... | collective-permute-start | bytes 393224 | tf_op jit(solution)/shard_map/ppermute | solution.py:208
  43.4 22.7 %collective-permute-start.9 = (f32[8,64,64]{2,0,1:T(8,128)S(1)}, f32[8,64,64]{2,0,1:T(8,128)S(1)}, u32[]{:S(2)}, u32[]{:S(2)}) collective-permute-start(f32[8,64,64]{2,0,1:T(8,128)S(1)} %get-tuple-element.20), channel_id=1, source_target_pairs={{0,32},{1,33},{2,34},{3,35},{4,36},{5,37},{6,38},{7,39},{40,72},{4... | collective-permute-start | bytes 393224 | tf_op jit(solution)/shard_map/ppermute | solution.py:208

commit v12 on v11

--- a/solution.py
+++ b/solution.py
@@ -9,7 +9,7 @@
 from jax.sharding import PartitionSpec as P
 
 HIGHEST = lax.Precision.HIGHEST
-TILE_ROWS = 256
+TILE_ROWS = 1024
 
 
 def split_bf16(value):

time: 85.7 us -> 79.7 us (0.930)
  Pallas kernels: 23 us -> 17.3 us
    pallas_call x1, Pallas kernels: 15 us -> 9.3 us  [apply_update(): pl.pallas_call(kernel, out_shape=jax.ShapeDtypeStruct(front.shape, front....]
  transfers between devices with their start and end apart: 12 -> 12, of which waited for: 5 -> 5; matrix products, arithmetic and copies ran while one was open for 17% -> 18% of each run, Pallas kernels for 9% -> 10%
where the time goes in v12:
time: 79.7 us; the launch traced here: 79.2 us
  waiting for transfers between devices  22.2 us (28%)
  Pallas kernels  17.3 us (22%)
  starting transfers between devices  16.4 us (21%)
  local copies, waits for them, and re-layouts  13.4 us (17%)
  other arithmetic  5.51 us (7%)
  matrix products  4.01 us (5%)
    ppermute x4, waiting for transfers between devices, send(): lax.ppermute(value, ('prow', 'pcol'), [(owner[c] * col_count + c, (owner[...  12 us
    ppermute x5, waiting for transfers between devices, doubling_gather(): other = lax.ppermute(block, axis, [(i, i ^ mask) for i in range(count)])  10.2 us
    pallas_call x1, Pallas kernels, apply_update(): pl.pallas_call(kernel, out_shape=jax.ShapeDtypeStruct(front.shape, front....  9.3 us
    pallas_call x1, Pallas kernels, invert_spd(): pl.pallas_call(inverse_kernel, out_shape=jax.ShapeDtypeStruct(matrix.shap...  8.03 us
    ppermute x5, starting transfers between devices, doubling_gather(): other = lax.ppermute(block, axis, [(i, i ^ mask) for i in range(count)])  7.39 us
    ppermute x3, starting transfers between devices, per_device(): lax.ppermute(diag_blocks, 'prow', [(i, (i + k) % row_count) for i in rang...  5 us
    ppermute x4, starting transfers between devices, send(): lax.ppermute(value, ('prow', 'pcol'), [(owner[c] * col_count + c, (owner[...  3.97 us
    unnamed x9, local copies, waits for them, and re-layouts  3.41 us
  transfers between devices with their start and end apart: 12, of which 5 were waited for; matrix products, arithmetic and copies ran while one was open for 18% of the time, Pallas kernels for 10%

profile of v12, /device:TPU:14, one launch (start us, length us, event | category | flops | bytes accessed | tf_op | source)
XLA Modules:
  0.0 79.2 jit_solution(2507948639907554530)
XLA Ops:
  0.0 0.9 %copy.53 = f32[1,64,128]{2,1,0:T(8,128)S(1)} copy(f32[1,64,128]{1,2,0:T(8,128)} %bitcast.49) | data formatting | bytes 65536 | tf_op jit(solution)/shard_map/broadcast_in_dim;reshape | solution.py:170
  0.9 4.0 %collective-permute-start = (f32[1,64,128]{2,1,0:T(8,128)S(1)}, f32[1,64,128]{2,1,0:T(8,128)S(1)}, u32[]{:S(2)}, u32[]{:S(2)}) collective-permute-start(f32[1,64,128]{2,1,0:T(8,128)S(1)} %copy.53), channel_id=1, source_target_pairs={{0,16},{1,17},{2,18},{3,19},{4,20},{5,21},{6,22},{7,23},{8,24},{9,... | collective-permute-start | bytes 98312 | tf_op jit(solution)/shard_map/ppermute | solution.py:145
  4.9 0.7 constant_dynamic-slice_fusion
  5.8 0.8 compare_reduce_fusion
  6.6 0.7 broadcast_xor_fusion
  7.4 1.1 %collective-permute-start.1 = (f32[2,64,128]{2,1,0:T(8,128)S(1)}, f32[2,64,128]{2,1,0:T(8,128)S(1)}, u32[]{:S(2)}, u32[]{:S(2)}) collective-permute-start(f32[2,64,128]{2,1,0:T(8,128)S(1)} %pad_maximum_fusion.3), channel_id=1, source_target_pairs={{0,8},{1,9},{2,10},{3,11},{4,12},{5,13},{6,14},{7,15},{8,0},{9,1},... | collective-permute-start | bytes 196616 | tf_op jit(solution)/shard_map/ppermute | solution.py:145
  8.5 3.2 %collective-permute-done.1 = f32[2,64,128]{2,1,0:T(8,128)S(1)} collective-permute-done((f32[2,64,128]{2,1,0:T(8,128)S(1)}, f32[2,64,128]{2,1,0:T(8,128)S(1)}, u32[]{:S(2)}, u32[]{:S(2)}) %collective-permute-start.1) | collective-permute-done | bytes 65568 | tf_op jit(solution)/shard_map/ppermute | solution.py:145
  11.8 1.5 %collective-permute-start.2 = (f32[4,64,128]{2,1,0:T(8,128)S(1)}, f32[4,64,128]{2,1,0:T(8,128)S(1)}, u32[]{:S(2)}, u32[]{:S(2)}) collective-permute-start(f32[4,64,128]{2,1,0:T(8,128)S(1)} %pad_maximum_fusion.2), channel_id=1, source_target_pairs={{0,4},{1,5},{2,6},{3,7},{4,0},{5,1},{6,2},{7,3},{8,12},{9,13},{10,... | collective-permute-start | bytes 393224 | tf_op jit(solution)/shard_map/ppermute | solution.py:145
  13.3 1.4 %gather_fusion = s32[32]{0:T(128)S(1)} fusion(s32[32]{0:T(128)} %constant.101.clone, s32[1024]{0:T(1024)S(1)} %pad_clamp_fusion.1), kind=kCustom, calls=%fused_computation | custom fusion | bytes 384 | tf_op jit(solution)/shard_map/jit(_take)/gather | solution.py:175
  15.2 3.2 %collective-permute-done.2 = f32[4,64,128]{2,1,0:T(8,128)S(1)} collective-permute-done((f32[4,64,128]{2,1,0:T(8,128)S(1)}, f32[4,64,128]{2,1,0:T(8,128)S(1)}, u32[]{:S(2)}, u32[]{:S(2)}) %collective-permute-start.2) | collective-permute-done | bytes 131104 | tf_op jit(solution)/shard_map/ppermute | solution.py:145
  18.5 0.9 %collective-permute-start.3 = (f32[8,64,128]{2,1,0:T(8,128)S(1)}, f32[8,64,128]{2,1,0:T(8,128)S(1)}, u32[]{:S(2)}, u32[]{:S(2)}) collective-permute-start(f32[8,64,128]{2,1,0:T(8,128)S(1)} %pad_maximum_fusion.1), channel_id=1, source_target_pairs={{0,2},{1,3},{2,0},{3,1},{4,6},{5,7},{6,4},{7,5},{8,10},{9,11},{10,... | collective-permute-start | bytes 786440 | tf_op jit(solution)/shard_map/ppermute | solution.py:145
  20.6 0.6 constant_dynamic-update-slice_fusion.1
  21.2 3.7 %collective-permute-done.3 = f32[8,64,128]{2,1,0:T(8,128)S(1)} collective-permute-done((f32[8,64,128]{2,1,0:T(8,128)S(1)}, f32[8,64,128]{2,1,0:T(8,128)S(1)}, u32[]{:S(2)}, u32[]{:S(2)}) %collective-permute-start.3) | collective-permute-done | bytes 262176 | tf_op jit(solution)/shard_map/ppermute | solution.py:145
  24.9 0.7 constant_dynamic-update-slice_fusion.near_ref
  26.2 2.6 %collective-permute-start.6 = (f32[2,16,64]{2,1,0:T(8,128)}, f32[2,16,64]{2,1,0:T(8,128)S(1)}, u32[]{:S(2)}, u32[]{:S(2)}) collective-permute-start(f32[2,16,64]{2,1,0:T(8,128)} %param.6), channel_id=1, source_target_pairs={{0,64},{32,96},{64,0},{96,32},{1,65},{33,97},{65,1},{97,33},{2,66}... | collective-permute-start | bytes 24584 | tf_op jit(solution)/shard_map/ppermute | solution.py:178
  28.8 1.9 %collective-permute-start.5 = (f32[2,16,64]{2,1,0:T(8,128)}, f32[2,16,64]{2,1,0:T(8,128)S(1)}, u32[]{:S(2)}, u32[]{:S(2)}) collective-permute-start(f32[2,16,64]{2,1,0:T(8,128)} %param.6), channel_id=1, source_target_pairs={{0,32},{32,64},{64,96},{96,0},{1,33},{33,65},{65,97},{97,1},{2,34}... | collective-permute-start | bytes 24584 | tf_op jit(solution)/shard_map/ppermute | solution.py:178
  30.7 0.7 pad_add_fusion.place_ref
  31.3 0.9 %copy.35 = f32[2,64,64]{1,2,0:T(8,128)S(1)} copy(f32[2,64,64]{2,1,0:T(8,128)} %param.7) | data formatting | bytes 65536 | tf_op args[1]
  32.9 0.7 broadcast_in_dim.122
  36.7 1.1 %fusion = f32[2,8,64,64]{3,1,2,0:T(8,128)S(1)} fusion(f32[16,64,2,64]{3,2,1,0:T(2,128)S(1)} %reshape.86, pred[2,8,32]{2,1,0:T(8,128)(4,1)S(1)} %compare_and_fusion), kind=kOutput, calls=%fused_computation.3 | convolution fusion | flops 12582912 | bytes 786944 | tf_op jit(solution)/shard_map/pjk,kbpa->pjba/dot_general | solution.py:195
  39.1 0.7 collective-permute-start.10
  39.8 0.7 collective-permute-start.11
  40.6 1.2 %gather_fusion.1 = s32[128]{0:T(128)S(1)} fusion(s32[32]{0:T(128)S(1)} %and_select_fusion, s32[1024]{0:T(1024)S(1)} %pad_clamp_fusion), kind=kCustom, calls=%fused_computation.1 | custom fusion | bytes 1536 | tf_op jit(solution)/shard_map/jit(_take)/gather | solution.py:204
  42.1 1.3 %collective-permute-start.8 = (f32[8,64,64]{2,0,1:T(8,128)S(1)}, f32[8,64,64]{2,0,1:T(8,128)S(1)}, u32[]{:S(2)}, u32[]{:S(2)}) collective-permute-start(f32[8,64,64]{2,0,1:T(8,128)S(1)} %get-tuple-element.19), channel_id=1, source_target_pairs={{0,32},{1,33},{2,34},{3,35},{4,36},{5,37},{6,38},{7,39},{40,72},{4... | collective-permute-start | bytes 393224 | tf_op jit(solution)/shard_map/ppermute | solution.py:208
  43.4 1.3 %collective-permute-start.9 = (f32[8,64,64]{2,0,1:T(8,128)S(1)}, f32[8,64,64]{2,0,1:T(8,128)S(1)}, u32[]{:S(2)}, u32[]{:S(2)}) collective-permute-start(f32[8,64,64]{2,0,1:T(8,128)S(1)} %get-tuple-element.20), channel_id=1, source_target_pairs={{0,32},{1,33},{2,34},{3,35},{4,36},{5,37},{6,38},{7,39},{40,72},{4... | collective-permute-start | bytes 393224 | tf_op jit(solution)/shard_map/ppermute | solution.py:208
  44.7 0.7 pad_maximum_fusion.4.system_ref
  45.4 8.0 %shard_map.64 = f32[2,64,64]{2,1,0:T(8,128)} custom-call(f32[2,64,128]{2,1,0:T(8,128)} %pad_maximum_fusion.4.system_ref), custom_call_target="tpu_custom_call" | custom-call | flops 4194304 | bytes 98304 | tf_op jit(solution)/shard_map/pallas_call | solution.py:127
  54.0 8.2 %collective-permute-done.8 = f32[8,64,64]{2,0,1:T(8,128)S(1)} collective-permute-done((f32[8,64,64]{2,0,1:T(8,128)S(1)}, f32[8,64,64]{2,0,1:T(8,128)S(1)}, u32[]{:S(2)}, u32[]{:S(2)}) %collective-permute-start.8) | collective-permute-done | bytes 131104 | tf_op jit(solution)/shard_map/ppermute | solution.py:208
  62.2 3.8 %collective-permute-done.9 = f32[8,64,64]{2,0,1:T(8,128)S(1)} collective-permute-done((f32[8,64,64]{2,0,1:T(8,128)S(1)}, f32[8,64,64]{2,0,1:T(8,128)S(1)}, u32[]{:S(2)}, u32[]{:S(2)}) %collective-permute-start.9) | collective-permute-done | bytes 131104 | tf_op jit(solution)/shard_map/ppermute | solution.py:208
  66.1 2.5 %fusion.3 = f32[2,64,8,64]{3,1,2,0:T(8,128)S(1)} fusion(f32[2,8,64,64]{3,1,2,0:T(8,128)S(1)} %fusion.2, f32[2,64,64]{2,1,0:T(8,128)} %shard_map.64), kind=kOutput, calls=%fused_computation.7 | convolution fusion | flops 50331648 | bytes 557056 | tf_op jit(solution)/shard_map/pxa,pjba->pxjb/dot_general | solution.py:215
  69.1 0.8 pad_maximum_fusion.stack_ref
  69.9 9.3 %shard_map.65 = f32[4096,512]{1,0:T(8,128)} custom-call(s32[2,64]{1,0:T(2,128)} %compare_select_fusion.5.table_ref, s32[2]{0:T(128)} %pad_add_fusion.place_ref, f32[16,64,128]{2,1,0:T(8,128)} %constant_dynamic-update-slice_fusion.near_ref, f32[16,64,128]{2,1,0:T(8,128)} %copy-done, bf16[384,512]{1,0:T(8,128)(2,1)} %pad_maximum_fusion.stack_ref, ...), custom_call_target="tpu_custom_call" | custom-call | flops 1610612736 | bytes 18219008 | tf_op jit(solution)/shard_map/pallas_call | solution.py:78
  (72 shorter events, 9.1 us)
Async XLA Ops:
  0.0 38.3 %copy-start.1 = (s32[2,128]{1,0:T(2,128)S(1)}, s32[2,128]{1,0:T(2,128)}, u32[]{:S(2)}) copy-start(s32[2,128]{1,0:T(2,128)} %param.8) | copy-start | bytes 3076
  0.9 6.5 %collective-permute-start = (f32[1,64,128]{2,1,0:T(8,128)S(1)}, f32[1,64,128]{2,1,0:T(8,128)S(1)}, u32[]{:S(2)}, u32[]{:S(2)}) collective-permute-start(f32[1,64,128]{2,1,0:T(8,128)S(1)} %copy.53), channel_id=1, source_target_pairs={{0,16},{1,17},{2,18},{3,19},{4,20},{5,21},{6,22},{7,23},{8,24},{9,... | collective-permute-start | bytes 98312 | tf_op jit(solution)/shard_map/ppermute | solution.py:145
  7.4 4.3 %collective-permute-start.1 = (f32[2,64,128]{2,1,0:T(8,128)S(1)}, f32[2,64,128]{2,1,0:T(8,128)S(1)}, u32[]{:S(2)}, u32[]{:S(2)}) collective-permute-start(f32[2,64,128]{2,1,0:T(8,128)S(1)} %pad_maximum_fusion.3), channel_id=1, source_target_pairs={{0,8},{1,9},{2,10},{3,11},{4,12},{5,13},{6,14},{7,15},{8,0},{9,1},... | collective-permute-start | bytes 196616 | tf_op jit(solution)/shard_map/ppermute | solution.py:145
  11.8 6.7 %collective-permute-start.2 = (f32[4,64,128]{2,1,0:T(8,128)S(1)}, f32[4,64,128]{2,1,0:T(8,128)S(1)}, u32[]{:S(2)}, u32[]{:S(2)}) collective-permute-start(f32[4,64,128]{2,1,0:T(8,128)S(1)} %pad_maximum_fusion.2), channel_id=1, source_target_pairs={{0,4},{1,5},{2,6},{3,7},{4,0},{5,1},{6,2},{7,3},{8,12},{9,13},{10,... | collective-permute-start | bytes 393224 | tf_op jit(solution)/shard_map/ppermute | solution.py:145
  18.5 6.5 %collective-permute-start.3 = (f32[8,64,128]{2,1,0:T(8,128)S(1)}, f32[8,64,128]{2,1,0:T(8,128)S(1)}, u32[]{:S(2)}, u32[]{:S(2)}) collective-permute-start(f32[8,64,128]{2,1,0:T(8,128)S(1)} %pad_maximum_fusion.1), channel_id=1, source_target_pairs={{0,2},{1,3},{2,0},{3,1},{4,6},{5,7},{6,4},{7,5},{8,10},{9,11},{10,... | collective-permute-start | bytes 786440 | tf_op jit(solution)/shard_map/ppermute | solution.py:145
  25.6 10.5 %collective-permute-start.4 = (f32[16,64,128]{2,1,0:T(8,128)}, f32[16,64,128]{2,1,0:T(8,128)S(1)}, u32[]{:S(2)}, u32[]{:S(2)}) collective-permute-start(f32[16,64,128]{2,1,0:T(8,128)} %constant_dynamic-update-slice_fusion.near_ref), channel_id=1, source_target_pairs={{0,1},{1,0},{2,3},{3,2},{4,5},{5,4},{6,7},{7,6},{8,9},{9,8},{10,11... | collective-permute-start | bytes 1572872 | tf_op jit(solution)/shard_map/ppermute | solution.py:145
  25.7 8.4 %collective-permute-start.7 = (f32[2,16,64]{2,1,0:T(8,128)}, f32[2,16,64]{2,1,0:T(8,128)S(1)}, u32[]{:S(2)}, u32[]{:S(2)}) collective-permute-start(f32[2,16,64]{2,1,0:T(8,128)} %param.6), channel_id=1, source_target_pairs={{0,96},{32,0},{64,32},{96,64},{1,97},{33,1},{65,33},{97,65},{2,98}... | collective-permute-start | bytes 24584 | tf_op jit(solution)/shard_map/ppermute | solution.py:178
  26.2 7.8 %collective-permute-start.6 = (f32[2,16,64]{2,1,0:T(8,128)}, f32[2,16,64]{2,1,0:T(8,128)S(1)}, u32[]{:S(2)}, u32[]{:S(2)}) collective-permute-start(f32[2,16,64]{2,1,0:T(8,128)} %param.6), channel_id=1, source_target_pairs={{0,64},{32,96},{64,0},{96,32},{1,65},{33,97},{65,1},{97,33},{2,66}... | collective-permute-start | bytes 24584 | tf_op jit(solution)/shard_map/ppermute | solution.py:178
  28.8 5.1 %collective-permute-start.5 = (f32[2,16,64]{2,1,0:T(8,128)}, f32[2,16,64]{2,1,0:T(8,128)S(1)}, u32[]{:S(2)}, u32[]{:S(2)}) collective-permute-start(f32[2,16,64]{2,1,0:T(8,128)} %param.6), channel_id=1, source_target_pairs={{0,32},{32,64},{64,96},{96,0},{1,33},{33,65},{65,97},{97,1},{2,34}... | collective-permute-start | bytes 24584 | tf_op jit(solution)/shard_map/ppermute | solution.py:178
  36.1 33.8 %copy-start = (f32[16,64,128]{2,1,0:T(8,128)}, f32[16,64,128]{2,1,0:T(8,128)S(1)}, u32[]{:S(2)}) copy-start(f32[16,64,128]{2,1,0:T(8,128)S(1)} %collective-permute-done.4.far_ref) | copy-start | bytes 1572868
  39.1 26.9 %collective-permute-start.10 = (f32[2,8,64,64]{3,1,2,0:T(8,128)S(1)}, f32[2,8,64,64]{3,1,2,0:T(8,128)S(1)}, u32[]{:S(2)}, u32[]{:S(2)}) collective-permute-start(f32[2,8,64,64]{3,1,2,0:T(8,128)S(1)} %convolution_add_fusion), channel_id=1, source_target_pairs={{0,64},{1,65},{2,66},{3,67},{4,68},{5,69},{6,70},{7,71},{40,104},{... | collective-permute-start | bytes 786440 | tf_op jit(solution)/shard_map/ppermute | solution.py:208
  39.8 26.2 %collective-permute-start.11 = (f32[2,8,64,64]{3,1,2,0:T(8,128)S(1)}, f32[2,8,64,64]{3,1,2,0:T(8,128)S(1)}, u32[]{:S(2)}, u32[]{:S(2)}) collective-permute-start(f32[2,8,64,64]{3,1,2,0:T(8,128)S(1)} %convolution_add_fusion), channel_id=1, source_target_pairs={{0,96},{1,97},{2,98},{3,99},{4,100},{5,101},{6,102},{7,103}} | collective-permute-start | bytes 786440 | tf_op jit(solution)/shard_map/ppermute | solution.py:208
  42.1 20.1 %collective-permute-start.8 = (f32[8,64,64]{2,0,1:T(8,128)S(1)}, f32[8,64,64]{2,0,1:T(8,128)S(1)}, u32[]{:S(2)}, u32[]{:S(2)}) collective-permute-start(f32[8,64,64]{2,0,1:T(8,128)S(1)} %get-tuple-element.19), channel_id=1, source_target_pairs={{0,32},{1,33},{2,34},{3,35},{4,36},{5,37},{6,38},{7,39},{40,72},{4... | collective-permute-start | bytes 393224 | tf_op jit(solution)/shard_map/ppermute | solution.py:208
  43.4 22.7 %collective-permute-start.9 = (f32[8,64,64]{2,0,1:T(8,128)S(1)}, f32[8,64,64]{2,0,1:T(8,128)S(1)}, u32[]{:S(2)}, u32[]{:S(2)}) collective-permute-start(f32[8,64,64]{2,0,1:T(8,128)S(1)} %get-tuple-element.20), channel_id=1, source_target_pairs={{0,32},{1,33},{2,34},{3,35},{4,36},{5,37},{6,38},{7,39},{40,72},{4... | collective-permute-start | bytes 393224 | tf_op jit(solution)/shard_map/ppermute | solution.py:208

commit v13 on v12

--- a/solution.py
+++ b/solution.py
@@ -9,7 +9,7 @@
 from jax.sharding import PartitionSpec as P
 
 HIGHEST = lax.Precision.HIGHEST
-TILE_ROWS = 1024
+TILE_ROWS = 2048
 
 
 def split_bf16(value):

time: 79.7 us -> 78.3 us (0.982)
  Pallas kernels: 17.3 us -> 16 us
    pallas_call x1, Pallas kernels: 9.3 us -> 7.95 us  [apply_update(): pl.pallas_call(kernel, out_shape=jax.ShapeDtypeStruct(front.shape, front....]
  transfers between devices with their start and end apart: 12 -> 12, of which waited for: 5 -> 5; matrix products, arithmetic and copies ran while one was open for 18% -> 19% of each run, Pallas kernels for 10% -> 10%
where the time goes in v13:
time: 78.3 us; the launch traced here: 77.8 us
  waiting for transfers between devices  22 us (28%)
  starting transfers between devices  16.5 us (21%)
  Pallas kernels  16 us (20%)
  local copies, waits for them, and re-layouts  13.4 us (17%)
  other arithmetic  5.51 us (7%)
  matrix products  4.01 us (5%)
    ppermute x4, waiting for transfers between devices, send(): lax.ppermute(value, ('prow', 'pcol'), [(owner[c] * col_count + c, (owner[...  11.8 us
    ppermute x5, waiting for transfers between devices, doubling_gather(): other = lax.ppermute(block, axis, [(i, i ^ mask) for i in range(count)])  10.2 us
    pallas_call x1, Pallas kernels, invert_spd(): pl.pallas_call(inverse_kernel, out_shape=jax.ShapeDtypeStruct(matrix.shap...  8.03 us
    pallas_call x1, Pallas kernels, apply_update(): pl.pallas_call(kernel, out_shape=jax.ShapeDtypeStruct(front.shape, front....  7.95 us
    ppermute x5, starting transfers between devices, doubling_gather(): other = lax.ppermute(block, axis, [(i, i ^ mask) for i in range(count)])  7.39 us
    ppermute x3, starting transfers between devices, per_device(): lax.ppermute(diag_blocks, 'prow', [(i, (i + k) % row_count) for i in rang...  5 us
    ppermute x4, starting transfers between devices, send(): lax.ppermute(value, ('prow', 'pcol'), [(owner[c] * col_count + c, (owner[...  4.15 us
    unnamed x9, local copies, waits for them, and re-layouts  3.41 us
  transfers between devices with their start and end apart: 12, of which 5 were waited for; matrix products, arithmetic and copies ran while one was open for 19% of the time, Pallas kernels for 10%

profile of v13, /device:TPU:14, one launch (start us, length us, event | category | flops | bytes accessed | tf_op | source)
XLA Modules:
  0.0 77.8 jit_solution(17206826528137927342)
XLA Ops:
  0.0 0.9 %copy.53 = f32[1,64,128]{2,1,0:T(8,128)S(1)} copy(f32[1,64,128]{1,2,0:T(8,128)} %bitcast.49) | data formatting | bytes 65536 | tf_op jit(solution)/shard_map/broadcast_in_dim;reshape | solution.py:170
  0.9 4.0 %collective-permute-start = (f32[1,64,128]{2,1,0:T(8,128)S(1)}, f32[1,64,128]{2,1,0:T(8,128)S(1)}, u32[]{:S(2)}, u32[]{:S(2)}) collective-permute-start(f32[1,64,128]{2,1,0:T(8,128)S(1)} %copy.53), channel_id=1, source_target_pairs={{0,16},{1,17},{2,18},{3,19},{4,20},{5,21},{6,22},{7,23},{8,24},{9,... | collective-permute-start | bytes 98312 | tf_op jit(solution)/shard_map/ppermute | solution.py:145
  4.9 0.7 constant_dynamic-slice_fusion
  5.8 0.8 %compare_reduce_fusion = (pred[2,8]{1,0:T(4,128)(4,1)}, s32[2,8]{1,0:T(2,128)S(1)}) fusion(s32[2,32]{1,0:T(2,128)S(1)} %constant_dynamic-slice_fusion, s32[8]{0:T(128)S(1)} %iota_add_fusion), kind=kLoop, calls=%fused_computation.29 | loop fusion | flops 3984 | bytes 368 | tf_op jit(solution)/shard_map/first_match/reduce | solution.py:155
  6.6 0.7 broadcast_xor_fusion
  7.4 1.1 %collective-permute-start.1 = (f32[2,64,128]{2,1,0:T(8,128)S(1)}, f32[2,64,128]{2,1,0:T(8,128)S(1)}, u32[]{:S(2)}, u32[]{:S(2)}) collective-permute-start(f32[2,64,128]{2,1,0:T(8,128)S(1)} %pad_maximum_fusion.3), channel_id=1, source_target_pairs={{0,8},{1,9},{2,10},{3,11},{4,12},{5,13},{6,14},{7,15},{8,0},{9,1},... | collective-permute-start | bytes 196616 | tf_op jit(solution)/shard_map/ppermute | solution.py:145
  8.5 3.2 %collective-permute-done.1 = f32[2,64,128]{2,1,0:T(8,128)S(1)} collective-permute-done((f32[2,64,128]{2,1,0:T(8,128)S(1)}, f32[2,64,128]{2,1,0:T(8,128)S(1)}, u32[]{:S(2)}, u32[]{:S(2)}) %collective-permute-start.1) | collective-permute-done | bytes 65568 | tf_op jit(solution)/shard_map/ppermute | solution.py:145
  11.8 1.5 %collective-permute-start.2 = (f32[4,64,128]{2,1,0:T(8,128)S(1)}, f32[4,64,128]{2,1,0:T(8,128)S(1)}, u32[]{:S(2)}, u32[]{:S(2)}) collective-permute-start(f32[4,64,128]{2,1,0:T(8,128)S(1)} %pad_maximum_fusion.2), channel_id=1, source_target_pairs={{0,4},{1,5},{2,6},{3,7},{4,0},{5,1},{6,2},{7,3},{8,12},{9,13},{10,... | collective-permute-start | bytes 393224 | tf_op jit(solution)/shard_map/ppermute | solution.py:145
  13.3 1.4 %gather_fusion = s32[32]{0:T(128)S(1)} fusion(s32[32]{0:T(128)} %constant.101.clone, s32[1024]{0:T(1024)S(1)} %pad_clamp_fusion.1), kind=kCustom, calls=%fused_computation | custom fusion | bytes 384 | tf_op jit(solution)/shard_map/jit(_take)/gather | solution.py:175
  15.2 3.2 %collective-permute-done.2 = f32[4,64,128]{2,1,0:T(8,128)S(1)} collective-permute-done((f32[4,64,128]{2,1,0:T(8,128)S(1)}, f32[4,64,128]{2,1,0:T(8,128)S(1)}, u32[]{:S(2)}, u32[]{:S(2)}) %collective-permute-start.2) | collective-permute-done | bytes 131104 | tf_op jit(solution)/shard_map/ppermute | solution.py:145
  18.5 0.9 %collective-permute-start.3 = (f32[8,64,128]{2,1,0:T(8,128)S(1)}, f32[8,64,128]{2,1,0:T(8,128)S(1)}, u32[]{:S(2)}, u32[]{:S(2)}) collective-permute-start(f32[8,64,128]{2,1,0:T(8,128)S(1)} %pad_maximum_fusion.1), channel_id=1, source_target_pairs={{0,2},{1,3},{2,0},{3,1},{4,6},{5,7},{6,4},{7,5},{8,10},{9,11},{10,... | collective-permute-start | bytes 786440 | tf_op jit(solution)/shard_map/ppermute | solution.py:145
  20.6 0.6 constant_dynamic-update-slice_fusion.1
  21.2 3.7 %collective-permute-done.3 = f32[8,64,128]{2,1,0:T(8,128)S(1)} collective-permute-done((f32[8,64,128]{2,1,0:T(8,128)S(1)}, f32[8,64,128]{2,1,0:T(8,128)S(1)}, u32[]{:S(2)}, u32[]{:S(2)}) %collective-permute-start.3) | collective-permute-done | bytes 262176 | tf_op jit(solution)/shard_map/ppermute | solution.py:145
  24.9 0.7 constant_dynamic-update-slice_fusion.near_ref
  26.2 2.6 %collective-permute-start.6 = (f32[2,16,64]{2,1,0:T(8,128)}, f32[2,16,64]{2,1,0:T(8,128)S(1)}, u32[]{:S(2)}, u32[]{:S(2)}) collective-permute-start(f32[2,16,64]{2,1,0:T(8,128)} %param.6), channel_id=1, source_target_pairs={{0,64},{32,96},{64,0},{96,32},{1,65},{33,97},{65,1},{97,33},{2,66}... | collective-permute-start | bytes 24584 | tf_op jit(solution)/shard_map/ppermute | solution.py:178
  28.8 1.9 %collective-permute-start.5 = (f32[2,16,64]{2,1,0:T(8,128)}, f32[2,16,64]{2,1,0:T(8,128)S(1)}, u32[]{:S(2)}, u32[]{:S(2)}) collective-permute-start(f32[2,16,64]{2,1,0:T(8,128)} %param.6), channel_id=1, source_target_pairs={{0,32},{32,64},{64,96},{96,0},{1,33},{33,65},{65,97},{97,1},{2,34}... | collective-permute-start | bytes 24584 | tf_op jit(solution)/shard_map/ppermute | solution.py:178
  30.7 0.7 pad_add_fusion.place_ref
  31.3 0.9 %copy.35 = f32[2,64,64]{1,2,0:T(8,128)S(1)} copy(f32[2,64,64]{2,1,0:T(8,128)} %param.7) | data formatting | bytes 65536 | tf_op args[1]
  32.9 0.7 broadcast_in_dim.122
  36.7 1.1 %fusion = f32[2,8,64,64]{3,1,2,0:T(8,128)S(1)} fusion(f32[16,64,2,64]{3,2,1,0:T(2,128)S(1)} %reshape.86, pred[2,8,32]{2,1,0:T(8,128)(4,1)S(1)} %compare_and_fusion), kind=kOutput, calls=%fused_computation.3 | convolution fusion | flops 12582912 | bytes 786944 | tf_op jit(solution)/shard_map/pjk,kbpa->pjba/dot_general | solution.py:195
  39.1 0.7 collective-permute-start.10
  39.8 0.7 collective-permute-start.11
  40.6 1.2 %gather_fusion.1 = s32[128]{0:T(128)S(1)} fusion(s32[32]{0:T(128)S(1)} %and_select_fusion, s32[1024]{0:T(1024)S(1)} %pad_clamp_fusion), kind=kCustom, calls=%fused_computation.1 | custom fusion | bytes 1536 | tf_op jit(solution)/shard_map/jit(_take)/gather | solution.py:204
  42.1 1.3 %collective-permute-start.8 = (f32[8,64,64]{2,0,1:T(8,128)S(1)}, f32[8,64,64]{2,0,1:T(8,128)S(1)}, u32[]{:S(2)}, u32[]{:S(2)}) collective-permute-start(f32[8,64,64]{2,0,1:T(8,128)S(1)} %get-tuple-element.19), channel_id=1, source_target_pairs={{0,32},{1,33},{2,34},{3,35},{4,36},{5,37},{6,38},{7,39},{40,72},{4... | collective-permute-start | bytes 393224 | tf_op jit(solution)/shard_map/ppermute | solution.py:208
  43.4 1.5 %collective-permute-start.9 = (f32[8,64,64]{2,0,1:T(8,128)S(1)}, f32[8,64,64]{2,0,1:T(8,128)S(1)}, u32[]{:S(2)}, u32[]{:S(2)}) collective-permute-start(f32[8,64,64]{2,0,1:T(8,128)S(1)} %get-tuple-element.20), channel_id=1, source_target_pairs={{0,32},{1,33},{2,34},{3,35},{4,36},{5,37},{6,38},{7,39},{40,72},{4... | collective-permute-start | bytes 393224 | tf_op jit(solution)/shard_map/ppermute | solution.py:208
  44.9 0.7 pad_maximum_fusion.4.system_ref
  45.6 8.0 %shard_map.64 = f32[2,64,64]{2,1,0:T(8,128)} custom-call(f32[2,64,128]{2,1,0:T(8,128)} %pad_maximum_fusion.4.system_ref), custom_call_target="tpu_custom_call" | custom-call | flops 4194304 | bytes 98304 | tf_op jit(solution)/shard_map/pallas_call | solution.py:127
  54.2 8.0 %collective-permute-done.8 = f32[8,64,64]{2,0,1:T(8,128)S(1)} collective-permute-done((f32[8,64,64]{2,0,1:T(8,128)S(1)}, f32[8,64,64]{2,0,1:T(8,128)S(1)}, u32[]{:S(2)}, u32[]{:S(2)}) %collective-permute-start.8) | collective-permute-done | bytes 131104 | tf_op jit(solution)/shard_map/ppermute | solution.py:208
  62.2 3.8 %collective-permute-done.9 = f32[8,64,64]{2,0,1:T(8,128)S(1)} collective-permute-done((f32[8,64,64]{2,0,1:T(8,128)S(1)}, f32[8,64,64]{2,0,1:T(8,128)S(1)}, u32[]{:S(2)}, u32[]{:S(2)}) %collective-permute-start.9) | collective-permute-done | bytes 131104 | tf_op jit(solution)/shard_map/ppermute | solution.py:208
  66.1 2.5 %fusion.3 = f32[2,64,8,64]{3,1,2,0:T(8,128)S(1)} fusion(f32[2,8,64,64]{3,1,2,0:T(8,128)S(1)} %fusion.2, f32[2,64,64]{2,1,0:T(8,128)} %shard_map.64), kind=kOutput, calls=%fused_computation.7 | convolution fusion | flops 50331648 | bytes 557056 | tf_op jit(solution)/shard_map/pxa,pjba->pxjb/dot_general | solution.py:215
  69.1 0.8 pad_maximum_fusion.stack_ref
  69.9 7.9 %shard_map.65 = f32[4096,512]{1,0:T(8,128)} custom-call(s32[2,64]{1,0:T(2,128)} %compare_select_fusion.5.table_ref, s32[2]{0:T(128)} %pad_add_fusion.place_ref, f32[16,64,128]{2,1,0:T(8,128)} %constant_dynamic-update-slice_fusion.near_ref, f32[16,64,128]{2,1,0:T(8,128)} %copy-done, bf16[384,512]{1,0:T(8,128)(2,1)} %pad_maximum_fusion.stack_ref, ...), custom_call_target="tpu_custom_call" | custom-call | flops 1610612736 | bytes 18219008 | tf_op jit(solution)/shard_map/pallas_call | solution.py:78
  (72 shorter events, 9.1 us)
Async XLA Ops:
  0.0 38.3 %copy-start.1 = (s32[2,128]{1,0:T(2,128)S(1)}, s32[2,128]{1,0:T(2,128)}, u32[]{:S(2)}) copy-start(s32[2,128]{1,0:T(2,128)} %param.8) | copy-start | bytes 3076
  0.9 6.5 %collective-permute-start = (f32[1,64,128]{2,1,0:T(8,128)S(1)}, f32[1,64,128]{2,1,0:T(8,128)S(1)}, u32[]{:S(2)}, u32[]{:S(2)}) collective-permute-start(f32[1,64,128]{2,1,0:T(8,128)S(1)} %copy.53), channel_id=1, source_target_pairs={{0,16},{1,17},{2,18},{3,19},{4,20},{5,21},{6,22},{7,23},{8,24},{9,... | collective-permute-start | bytes 98312 | tf_op jit(solution)/shard_map/ppermute | solution.py:145
  7.4 4.3 %collective-permute-start.1 = (f32[2,64,128]{2,1,0:T(8,128)S(1)}, f32[2,64,128]{2,1,0:T(8,128)S(1)}, u32[]{:S(2)}, u32[]{:S(2)}) collective-permute-start(f32[2,64,128]{2,1,0:T(8,128)S(1)} %pad_maximum_fusion.3), channel_id=1, source_target_pairs={{0,8},{1,9},{2,10},{3,11},{4,12},{5,13},{6,14},{7,15},{8,0},{9,1},... | collective-permute-start | bytes 196616 | tf_op jit(solution)/shard_map/ppermute | solution.py:145
  11.8 6.7 %collective-permute-start.2 = (f32[4,64,128]{2,1,0:T(8,128)S(1)}, f32[4,64,128]{2,1,0:T(8,128)S(1)}, u32[]{:S(2)}, u32[]{:S(2)}) collective-permute-start(f32[4,64,128]{2,1,0:T(8,128)S(1)} %pad_maximum_fusion.2), channel_id=1, source_target_pairs={{0,4},{1,5},{2,6},{3,7},{4,0},{5,1},{6,2},{7,3},{8,12},{9,13},{10,... | collective-permute-start | bytes 393224 | tf_op jit(solution)/shard_map/ppermute | solution.py:145
  18.5 6.5 %collective-permute-start.3 = (f32[8,64,128]{2,1,0:T(8,128)S(1)}, f32[8,64,128]{2,1,0:T(8,128)S(1)}, u32[]{:S(2)}, u32[]{:S(2)}) collective-permute-start(f32[8,64,128]{2,1,0:T(8,128)S(1)} %pad_maximum_fusion.1), channel_id=1, source_target_pairs={{0,2},{1,3},{2,0},{3,1},{4,6},{5,7},{6,4},{7,5},{8,10},{9,11},{10,... | collective-permute-start | bytes 786440 | tf_op jit(solution)/shard_map/ppermute | solution.py:145
  25.6 10.5 %collective-permute-start.4 = (f32[16,64,128]{2,1,0:T(8,128)}, f32[16,64,128]{2,1,0:T(8,128)S(1)}, u32[]{:S(2)}, u32[]{:S(2)}) collective-permute-start(f32[16,64,128]{2,1,0:T(8,128)} %constant_dynamic-update-slice_fusion.near_ref), channel_id=1, source_target_pairs={{0,1},{1,0},{2,3},{3,2},{4,5},{5,4},{6,7},{7,6},{8,9},{9,8},{10,11... | collective-permute-start | bytes 1572872 | tf_op jit(solution)/shard_map/ppermute | solution.py:145
  25.7 8.4 %collective-permute-start.7 = (f32[2,16,64]{2,1,0:T(8,128)}, f32[2,16,64]{2,1,0:T(8,128)S(1)}, u32[]{:S(2)}, u32[]{:S(2)}) collective-permute-start(f32[2,16,64]{2,1,0:T(8,128)} %param.6), channel_id=1, source_target_pairs={{0,96},{32,0},{64,32},{96,64},{1,97},{33,1},{65,33},{97,65},{2,98}... | collective-permute-start | bytes 24584 | tf_op jit(solution)/shard_map/ppermute | solution.py:178
  26.2 7.8 %collective-permute-start.6 = (f32[2,16,64]{2,1,0:T(8,128)}, f32[2,16,64]{2,1,0:T(8,128)S(1)}, u32[]{:S(2)}, u32[]{:S(2)}) collective-permute-start(f32[2,16,64]{2,1,0:T(8,128)} %param.6), channel_id=1, source_target_pairs={{0,64},{32,96},{64,0},{96,32},{1,65},{33,97},{65,1},{97,33},{2,66}... | collective-permute-start | bytes 24584 | tf_op jit(solution)/shard_map/ppermute | solution.py:178
  28.8 5.1 %collective-permute-start.5 = (f32[2,16,64]{2,1,0:T(8,128)}, f32[2,16,64]{2,1,0:T(8,128)S(1)}, u32[]{:S(2)}, u32[]{:S(2)}) collective-permute-start(f32[2,16,64]{2,1,0:T(8,128)} %param.6), channel_id=1, source_target_pairs={{0,32},{32,64},{64,96},{96,0},{1,33},{33,65},{65,97},{97,1},{2,34}... | collective-permute-start | bytes 24584 | tf_op jit(solution)/shard_map/ppermute | solution.py:178
  36.1 33.8 %copy-start = (f32[16,64,128]{2,1,0:T(8,128)}, f32[16,64,128]{2,1,0:T(8,128)S(1)}, u32[]{:S(2)}) copy-start(f32[16,64,128]{2,1,0:T(8,128)S(1)} %collective-permute-done.4.far_ref) | copy-start | bytes 1572868
  39.1 26.9 %collective-permute-start.10 = (f32[2,8,64,64]{3,1,2,0:T(8,128)S(1)}, f32[2,8,64,64]{3,1,2,0:T(8,128)S(1)}, u32[]{:S(2)}, u32[]{:S(2)}) collective-permute-start(f32[2,8,64,64]{3,1,2,0:T(8,128)S(1)} %convolution_add_fusion), channel_id=1, source_target_pairs={{0,64},{1,65},{2,66},{3,67},{4,68},{5,69},{6,70},{7,71},{40,104},{... | collective-permute-start | bytes 786440 | tf_op jit(solution)/shard_map/ppermute | solution.py:208
  39.8 26.2 %collective-permute-start.11 = (f32[2,8,64,64]{3,1,2,0:T(8,128)S(1)}, f32[2,8,64,64]{3,1,2,0:T(8,128)S(1)}, u32[]{:S(2)}, u32[]{:S(2)}) collective-permute-start(f32[2,8,64,64]{3,1,2,0:T(8,128)S(1)} %convolution_add_fusion), channel_id=1, source_target_pairs={{0,96},{1,97},{2,98},{3,99},{4,100},{5,101},{6,102},{7,103}} | collective-permute-start | bytes 786440 | tf_op jit(solution)/shard_map/ppermute | solution.py:208
  42.1 20.1 %collective-permute-start.8 = (f32[8,64,64]{2,0,1:T(8,128)S(1)}, f32[8,64,64]{2,0,1:T(8,128)S(1)}, u32[]{:S(2)}, u32[]{:S(2)}) collective-permute-start(f32[8,64,64]{2,0,1:T(8,128)S(1)} %get-tuple-element.19), channel_id=1, source_target_pairs={{0,32},{1,33},{2,34},{3,35},{4,36},{5,37},{6,38},{7,39},{40,72},{4... | collective-permute-start | bytes 393224 | tf_op jit(solution)/shard_map/ppermute | solution.py:208
  43.4 22.7 %collective-permute-start.9 = (f32[8,64,64]{2,0,1:T(8,128)S(1)}, f32[8,64,64]{2,0,1:T(8,128)S(1)}, u32[]{:S(2)}, u32[]{:S(2)}) collective-permute-start(f32[8,64,64]{2,0,1:T(8,128)S(1)} %get-tuple-element.20), channel_id=1, source_target_pairs={{0,32},{1,33},{2,34},{3,35},{4,36},{5,37},{6,38},{7,39},{40,72},{4... | collective-permute-start | bytes 393224 | tf_op jit(solution)/shard_map/ppermute | solution.py:208

commit v14 on v13

--- a/solution.py
+++ b/solution.py
@@ -210,8 +210,10 @@
             for c in range(col_count) if owner[c] + k < row_count
         ])
 
-    nearest = jnp.stack([send(window[panel], 1) for panel in range(window.shape[0])])
-    window = window + nearest + sum(send(window, k) for k in range(2, row_count))
+    window = window + sum(
+        jnp.stack([send(window[panel], k) for panel in range(window.shape[0])])
+        for k in range(1, row_count)
+    )
     right = jnp.einsum("pxa,pjba->pxjb", inverse, window, precision=HIGHEST)
     right = right.reshape(2 * width, col_blocks * width)
 

time: 78.3 us -> 79.7 us (1.018)
  starting transfers between devices: 16.5 us -> 17.9 us
    ppermute x4 -> x6, starting transfers between devices: 4.15 us -> 5.46 us  [send(): lax.ppermute(value, ('prow', 'pcol'), [(owner[c] * col_count + c, (owner[...]
    ppermute x4 -> x6, waiting for transfers between devices: 11.8 us -> 11.9 us  [send(): lax.ppermute(value, ('prow', 'pcol'), [(owner[c] * col_count + c, (owner[...]
  transfers between devices with their start and end apart: 12 -> 14, of which waited for: 5 -> 5; matrix products, arithmetic and copies ran while one was open for 19% -> 18% of each run, Pallas kernels for 10% -> 10%
where the time goes in v14:
time: 79.7 us; the launch traced here: 79.2 us
  waiting for transfers between devices  22.1 us (28%)
  starting transfers between devices  17.9 us (22%)
  Pallas kernels  16 us (20%)
  local copies, waits for them, and re-layouts  13.4 us (17%)
  other arithmetic  5.51 us (7%)
  matrix products  4.01 us (5%)
    ppermute x6, waiting for transfers between devices, send(): lax.ppermute(value, ('prow', 'pcol'), [(owner[c] * col_count + c, (owner[...  11.9 us
    ppermute x5, waiting for transfers between devices, doubling_gather(): other = lax.ppermute(block, axis, [(i, i ^ mask) for i in range(count)])  10.2 us
    pallas_call x1, Pallas kernels, invert_spd(): pl.pallas_call(inverse_kernel, out_shape=jax.ShapeDtypeStruct(matrix.shap...  8.03 us
    pallas_call x1, Pallas kernels, apply_update(): pl.pallas_call(kernel, out_shape=jax.ShapeDtypeStruct(front.shape, front....  7.94 us
    ppermute x5, starting transfers between devices, doubling_gather(): other = lax.ppermute(block, axis, [(i, i ^ mask) for i in range(count)])  7.39 us
    ppermute x6, starting transfers between devices, send(): lax.ppermute(value, ('prow', 'pcol'), [(owner[c] * col_count + c, (owner[...  5.46 us
    ppermute x3, starting transfers between devices, per_device(): lax.ppermute(diag_blocks, 'prow', [(i, (i + k) % row_count) for i in rang...  5 us
    unnamed x9, local copies, waits for them, and re-layouts  3.41 us
  transfers between devices with their start and end apart: 14, of which 5 were waited for; matrix products, arithmetic and copies ran while one was open for 18% of the time, Pallas kernels for 10%

profile of v14, /device:TPU:14, one launch (start us, length us, event | category | flops | bytes accessed | tf_op | source)
XLA Modules:
  0.0 79.2 jit_solution(8753699304600326183)
XLA Ops:
  0.0 0.9 %copy.53 = f32[1,64,128]{2,1,0:T(8,128)S(1)} copy(f32[1,64,128]{1,2,0:T(8,128)} %bitcast.57) | data formatting | bytes 65536 | tf_op jit(solution)/shard_map/broadcast_in_dim;reshape | solution.py:170
  0.9 4.0 %collective-permute-start = (f32[1,64,128]{2,1,0:T(8,128)S(1)}, f32[1,64,128]{2,1,0:T(8,128)S(1)}, u32[]{:S(2)}, u32[]{:S(2)}) collective-permute-start(f32[1,64,128]{2,1,0:T(8,128)S(1)} %copy.53), channel_id=1, source_target_pairs={{0,16},{1,17},{2,18},{3,19},{4,20},{5,21},{6,22},{7,23},{8,24},{9,... | collective-permute-start | bytes 98312 | tf_op jit(solution)/shard_map/ppermute | solution.py:145
  4.9 0.7 constant_dynamic-slice_fusion
  5.8 0.8 compare_reduce_fusion
  6.6 0.7 broadcast_xor_fusion
  7.4 1.1 %collective-permute-start.1 = (f32[2,64,128]{2,1,0:T(8,128)S(1)}, f32[2,64,128]{2,1,0:T(8,128)S(1)}, u32[]{:S(2)}, u32[]{:S(2)}) collective-permute-start(f32[2,64,128]{2,1,0:T(8,128)S(1)} %pad_maximum_fusion.3), channel_id=1, source_target_pairs={{0,8},{1,9},{2,10},{3,11},{4,12},{5,13},{6,14},{7,15},{8,0},{9,1},... | collective-permute-start | bytes 196616 | tf_op jit(solution)/shard_map/ppermute | solution.py:145
  8.5 3.2 %collective-permute-done.1 = f32[2,64,128]{2,1,0:T(8,128)S(1)} collective-permute-done((f32[2,64,128]{2,1,0:T(8,128)S(1)}, f32[2,64,128]{2,1,0:T(8,128)S(1)}, u32[]{:S(2)}, u32[]{:S(2)}) %collective-permute-start.1) | collective-permute-done | bytes 65568 | tf_op jit(solution)/shard_map/ppermute | solution.py:145
  11.8 1.5 %collective-permute-start.2 = (f32[4,64,128]{2,1,0:T(8,128)S(1)}, f32[4,64,128]{2,1,0:T(8,128)S(1)}, u32[]{:S(2)}, u32[]{:S(2)}) collective-permute-start(f32[4,64,128]{2,1,0:T(8,128)S(1)} %pad_maximum_fusion.2), channel_id=1, source_target_pairs={{0,4},{1,5},{2,6},{3,7},{4,0},{5,1},{6,2},{7,3},{8,12},{9,13},{10,... | collective-permute-start | bytes 393224 | tf_op jit(solution)/shard_map/ppermute | solution.py:145
  13.3 1.4 %gather_fusion = s32[32]{0:T(128)S(1)} fusion(s32[32]{0:T(128)} %constant.101.clone, s32[1024]{0:T(1024)S(1)} %pad_clamp_fusion.1), kind=kCustom, calls=%fused_computation | custom fusion | bytes 384 | tf_op jit(solution)/shard_map/jit(_take)/gather | solution.py:175
  15.2 3.2 %collective-permute-done.2 = f32[4,64,128]{2,1,0:T(8,128)S(1)} collective-permute-done((f32[4,64,128]{2,1,0:T(8,128)S(1)}, f32[4,64,128]{2,1,0:T(8,128)S(1)}, u32[]{:S(2)}, u32[]{:S(2)}) %collective-permute-start.2) | collective-permute-done | bytes 131104 | tf_op jit(solution)/shard_map/ppermute | solution.py:145
  18.5 0.9 %collective-permute-start.3 = (f32[8,64,128]{2,1,0:T(8,128)S(1)}, f32[8,64,128]{2,1,0:T(8,128)S(1)}, u32[]{:S(2)}, u32[]{:S(2)}) collective-permute-start(f32[8,64,128]{2,1,0:T(8,128)S(1)} %pad_maximum_fusion.1), channel_id=1, source_target_pairs={{0,2},{1,3},{2,0},{3,1},{4,6},{5,7},{6,4},{7,5},{8,10},{9,11},{10,... | collective-permute-start | bytes 786440 | tf_op jit(solution)/shard_map/ppermute | solution.py:145
  21.2 3.7 %collective-permute-done.3 = f32[8,64,128]{2,1,0:T(8,128)S(1)} collective-permute-done((f32[8,64,128]{2,1,0:T(8,128)S(1)}, f32[8,64,128]{2,1,0:T(8,128)S(1)}, u32[]{:S(2)}, u32[]{:S(2)}) %collective-permute-start.3) | collective-permute-done | bytes 262176 | tf_op jit(solution)/shard_map/ppermute | solution.py:145
  24.9 0.7 constant_dynamic-update-slice_fusion.near_ref
  26.2 2.6 %collective-permute-start.6 = (f32[2,16,64]{2,1,0:T(8,128)}, f32[2,16,64]{2,1,0:T(8,128)S(1)}, u32[]{:S(2)}, u32[]{:S(2)}) collective-permute-start(f32[2,16,64]{2,1,0:T(8,128)} %param.6), channel_id=1, source_target_pairs={{0,64},{32,96},{64,0},{96,32},{1,65},{33,97},{65,1},{97,33},{2,66}... | collective-permute-start | bytes 24584 | tf_op jit(solution)/shard_map/ppermute | solution.py:178
  28.8 1.9 %collective-permute-start.5 = (f32[2,16,64]{2,1,0:T(8,128)}, f32[2,16,64]{2,1,0:T(8,128)S(1)}, u32[]{:S(2)}, u32[]{:S(2)}) collective-permute-start(f32[2,16,64]{2,1,0:T(8,128)} %param.6), channel_id=1, source_target_pairs={{0,32},{32,64},{64,96},{96,0},{1,33},{33,65},{65,97},{97,1},{2,34}... | collective-permute-start | bytes 24584 | tf_op jit(solution)/shard_map/ppermute | solution.py:178
  31.3 0.9 %copy.35 = f32[2,64,64]{1,2,0:T(8,128)S(1)} copy(f32[2,64,64]{2,1,0:T(8,128)} %param.7) | data formatting | bytes 65536 | tf_op args[1]
  32.9 0.7 broadcast_in_dim.122
  36.7 1.1 %fusion = f32[2,8,64,64]{3,1,2,0:T(8,128)S(1)} fusion(f32[16,64,2,64]{3,2,1,0:T(2,128)S(1)} %reshape.86, pred[2,8,32]{2,1,0:T(8,128)(4,1)S(1)} %compare_and_fusion), kind=kOutput, calls=%fused_computation.3 | convolution fusion | flops 12582912 | bytes 786944 | tf_op jit(solution)/shard_map/pjk,kbpa->pjba/dot_general | solution.py:195
  39.1 0.7 collective-permute-start.12
  39.8 0.7 collective-permute-start.10
  40.5 1.3 %collective-permute-start.8 = (f32[8,64,64]{2,0,1:T(8,128)S(1)}, f32[8,64,64]{2,0,1:T(8,128)S(1)}, u32[]{:S(2)}, u32[]{:S(2)}) collective-permute-start(f32[8,64,64]{2,0,1:T(8,128)S(1)} %get-tuple-element.19), channel_id=1, source_target_pairs={{0,32},{1,33},{2,34},{3,35},{4,36},{5,37},{6,38},{7,39},{40,72},{4... | collective-permute-start | bytes 393224 | tf_op jit(solution)/shard_map/ppermute | solution.py:208
  41.8 0.7 collective-permute-start.13
  42.5 0.7 collective-permute-start.11
  43.4 1.2 %gather_fusion.1 = s32[128]{0:T(128)S(1)} fusion(s32[32]{0:T(128)S(1)} %and_select_fusion, s32[1024]{0:T(1024)S(1)} %pad_clamp_fusion), kind=kCustom, calls=%fused_computation.1 | custom fusion | bytes 1536 | tf_op jit(solution)/shard_map/jit(_take)/gather | solution.py:204
  44.7 0.7 pad_maximum_fusion.4.system_ref
  45.4 8.0 %shard_map.64 = f32[2,64,64]{2,1,0:T(8,128)} custom-call(f32[2,64,128]{2,1,0:T(8,128)} %pad_maximum_fusion.4.system_ref), custom_call_target="tpu_custom_call" | custom-call | flops 4194304 | bytes 98304 | tf_op jit(solution)/shard_map/pallas_call | solution.py:127
  53.5 1.5 %collective-permute-start.9 = (f32[8,64,64]{2,0,1:T(8,128)S(1)}, f32[8,64,64]{2,0,1:T(8,128)S(1)}, u32[]{:S(2)}, u32[]{:S(2)}) collective-permute-start(f32[8,64,64]{2,0,1:T(8,128)S(1)} %get-tuple-element.20), channel_id=1, source_target_pairs={{0,32},{1,33},{2,34},{3,35},{4,36},{5,37},{6,38},{7,39},{40,72},{4... | collective-permute-start | bytes 393224 | tf_op jit(solution)/shard_map/ppermute | solution.py:208
  55.5 2.0 %collective-permute-done.8 = f32[8,64,64]{2,0,1:T(8,128)S(1)} collective-permute-done((f32[8,64,64]{2,0,1:T(8,128)S(1)}, f32[8,64,64]{2,0,1:T(8,128)S(1)}, u32[]{:S(2)}, u32[]{:S(2)}) %collective-permute-start.8) | collective-permute-done | bytes 131104 | tf_op jit(solution)/shard_map/ppermute | solution.py:208
  57.5 9.9 %collective-permute-done.9 = f32[8,64,64]{2,0,1:T(8,128)S(1)} collective-permute-done((f32[8,64,64]{2,0,1:T(8,128)S(1)}, f32[8,64,64]{2,0,1:T(8,128)S(1)}, u32[]{:S(2)}, u32[]{:S(2)}) %collective-permute-start.9) | collective-permute-done | bytes 131104 | tf_op jit(solution)/shard_map/ppermute | solution.py:208
  67.5 2.5 %fusion.4 = f32[2,64,8,64]{3,1,2,0:T(8,128)S(1)} fusion(f32[2,8,64,64]{3,1,2,0:T(8,128)S(1)} %fusion.3, f32[2,64,64]{2,1,0:T(8,128)} %shard_map.64), kind=kOutput, calls=%fused_computation.8 | convolution fusion | flops 50331648 | bytes 557056 | tf_op jit(solution)/shard_map/pxa,pjba->pxjb/dot_general | solution.py:217
  70.5 0.8 pad_maximum_fusion.stack_ref
  71.3 7.9 %shard_map.65 = f32[4096,512]{1,0:T(8,128)} custom-call(s32[2,64]{1,0:T(2,128)} %compare_select_fusion.5.table_ref, s32[2]{0:T(128)} %pad_add_fusion.place_ref, f32[16,64,128]{2,1,0:T(8,128)} %constant_dynamic-update-slice_fusion.near_ref, f32[16,64,128]{2,1,0:T(8,128)} %copy-done, bf16[384,512]{1,0:T(8,128)(2,1)} %pad_maximum_fusion.stack_ref, ...), custom_call_target="tpu_custom_call" | custom-call | flops 1610612736 | bytes 18219008 | tf_op jit(solution)/shard_map/pallas_call | solution.py:78
  (76 shorter events, 10.4 us)
Async XLA Ops:
  0.0 38.3 %copy-start.1 = (s32[2,128]{1,0:T(2,128)S(1)}, s32[2,128]{1,0:T(2,128)}, u32[]{:S(2)}) copy-start(s32[2,128]{1,0:T(2,128)} %param.8) | copy-start | bytes 3076
  0.9 6.5 %collective-permute-start = (f32[1,64,128]{2,1,0:T(8,128)S(1)}, f32[1,64,128]{2,1,0:T(8,128)S(1)}, u32[]{:S(2)}, u32[]{:S(2)}) collective-permute-start(f32[1,64,128]{2,1,0:T(8,128)S(1)} %copy.53), channel_id=1, source_target_pairs={{0,16},{1,17},{2,18},{3,19},{4,20},{5,21},{6,22},{7,23},{8,24},{9,... | collective-permute-start | bytes 98312 | tf_op jit(solution)/shard_map/ppermute | solution.py:145
  7.4 4.3 %collective-permute-start.1 = (f32[2,64,128]{2,1,0:T(8,128)S(1)}, f32[2,64,128]{2,1,0:T(8,128)S(1)}, u32[]{:S(2)}, u32[]{:S(2)}) collective-permute-start(f32[2,64,128]{2,1,0:T(8,128)S(1)} %pad_maximum_fusion.3), channel_id=1, source_target_pairs={{0,8},{1,9},{2,10},{3,11},{4,12},{5,13},{6,14},{7,15},{8,0},{9,1},... | collective-permute-start | bytes 196616 | tf_op jit(solution)/shard_map/ppermute | solution.py:145
  11.8 6.7 %collective-permute-start.2 = (f32[4,64,128]{2,1,0:T(8,128)S(1)}, f32[4,64,128]{2,1,0:T(8,128)S(1)}, u32[]{:S(2)}, u32[]{:S(2)}) collective-permute-start(f32[4,64,128]{2,1,0:T(8,128)S(1)} %pad_maximum_fusion.2), channel_id=1, source_target_pairs={{0,4},{1,5},{2,6},{3,7},{4,0},{5,1},{6,2},{7,3},{8,12},{9,13},{10,... | collective-permute-start | bytes 393224 | tf_op jit(solution)/shard_map/ppermute | solution.py:145
  18.5 6.5 %collective-permute-start.3 = (f32[8,64,128]{2,1,0:T(8,128)S(1)}, f32[8,64,128]{2,1,0:T(8,128)S(1)}, u32[]{:S(2)}, u32[]{:S(2)}) collective-permute-start(f32[8,64,128]{2,1,0:T(8,128)S(1)} %pad_maximum_fusion.1), channel_id=1, source_target_pairs={{0,2},{1,3},{2,0},{3,1},{4,6},{5,7},{6,4},{7,5},{8,10},{9,11},{10,... | collective-permute-start | bytes 786440 | tf_op jit(solution)/shard_map/ppermute | solution.py:145
  25.6 10.5 %collective-permute-start.4 = (f32[16,64,128]{2,1,0:T(8,128)}, f32[16,64,128]{2,1,0:T(8,128)S(1)}, u32[]{:S(2)}, u32[]{:S(2)}) collective-permute-start(f32[16,64,128]{2,1,0:T(8,128)} %constant_dynamic-update-slice_fusion.near_ref), channel_id=1, source_target_pairs={{0,1},{1,0},{2,3},{3,2},{4,5},{5,4},{6,7},{7,6},{8,9},{9,8},{10,11... | collective-permute-start | bytes 1572872 | tf_op jit(solution)/shard_map/ppermute | solution.py:145
  25.7 8.4 %collective-permute-start.7 = (f32[2,16,64]{2,1,0:T(8,128)}, f32[2,16,64]{2,1,0:T(8,128)S(1)}, u32[]{:S(2)}, u32[]{:S(2)}) collective-permute-start(f32[2,16,64]{2,1,0:T(8,128)} %param.6), channel_id=1, source_target_pairs={{0,96},{32,0},{64,32},{96,64},{1,97},{33,1},{65,33},{97,65},{2,98}... | collective-permute-start | bytes 24584 | tf_op jit(solution)/shard_map/ppermute | solution.py:178
  26.2 7.8 %collective-permute-start.6 = (f32[2,16,64]{2,1,0:T(8,128)}, f32[2,16,64]{2,1,0:T(8,128)S(1)}, u32[]{:S(2)}, u32[]{:S(2)}) collective-permute-start(f32[2,16,64]{2,1,0:T(8,128)} %param.6), channel_id=1, source_target_pairs={{0,64},{32,96},{64,0},{96,32},{1,65},{33,97},{65,1},{97,33},{2,66}... | collective-permute-start | bytes 24584 | tf_op jit(solution)/shard_map/ppermute | solution.py:178
  28.8 5.1 %collective-permute-start.5 = (f32[2,16,64]{2,1,0:T(8,128)}, f32[2,16,64]{2,1,0:T(8,128)S(1)}, u32[]{:S(2)}, u32[]{:S(2)}) collective-permute-start(f32[2,16,64]{2,1,0:T(8,128)} %param.6), channel_id=1, source_target_pairs={{0,32},{32,64},{64,96},{96,0},{1,33},{33,65},{65,97},{97,1},{2,34}... | collective-permute-start | bytes 24584 | tf_op jit(solution)/shard_map/ppermute | solution.py:178
  36.1 35.1 %copy-start = (f32[16,64,128]{2,1,0:T(8,128)}, f32[16,64,128]{2,1,0:T(8,128)S(1)}, u32[]{:S(2)}) copy-start(f32[16,64,128]{2,1,0:T(8,128)S(1)} %collective-permute-done.4.far_ref) | copy-start | bytes 1572868
  39.1 14.3 %collective-permute-start.12 = (f32[8,64,64]{2,0,1:T(8,128)S(1)}, f32[8,64,64]{2,0,1:T(8,128)S(1)}, u32[]{:S(2)}, u32[]{:S(2)}) collective-permute-start(f32[8,64,64]{2,0,1:T(8,128)S(1)} %get-tuple-element.19), channel_id=1, source_target_pairs={{0,96},{1,97},{2,98},{3,99},{4,100},{5,101},{6,102},{7,103}} | collective-permute-start | bytes 393224 | tf_op jit(solution)/shard_map/ppermute | solution.py:208
  39.8 15.7 %collective-permute-start.10 = (f32[8,64,64]{2,0,1:T(8,128)S(1)}, f32[8,64,64]{2,0,1:T(8,128)S(1)}, u32[]{:S(2)}, u32[]{:S(2)}) collective-permute-start(f32[8,64,64]{2,0,1:T(8,128)S(1)} %get-tuple-element.19), channel_id=1, source_target_pairs={{0,64},{1,65},{2,66},{3,67},{4,68},{5,69},{6,70},{7,71},{40,104},{... | collective-permute-start | bytes 393224 | tf_op jit(solution)/shard_map/ppermute | solution.py:208
  40.5 17.0 %collective-permute-start.8 = (f32[8,64,64]{2,0,1:T(8,128)S(1)}, f32[8,64,64]{2,0,1:T(8,128)S(1)}, u32[]{:S(2)}, u32[]{:S(2)}) collective-permute-start(f32[8,64,64]{2,0,1:T(8,128)S(1)} %get-tuple-element.19), channel_id=1, source_target_pairs={{0,32},{1,33},{2,34},{3,35},{4,36},{5,37},{6,38},{7,39},{40,72},{4... | collective-permute-start | bytes 393224 | tf_op jit(solution)/shard_map/ppermute | solution.py:208
  41.8 15.7 %collective-permute-start.13 = (f32[8,64,64]{2,0,1:T(8,128)S(1)}, f32[8,64,64]{2,0,1:T(8,128)S(1)}, u32[]{:S(2)}, u32[]{:S(2)}) collective-permute-start(f32[8,64,64]{2,0,1:T(8,128)S(1)} %get-tuple-element.20), channel_id=1, source_target_pairs={{0,96},{1,97},{2,98},{3,99},{4,100},{5,101},{6,102},{7,103}} | collective-permute-start | bytes 393224 | tf_op jit(solution)/shard_map/ppermute | solution.py:208
  42.5 15.0 %collective-permute-start.11 = (f32[8,64,64]{2,0,1:T(8,128)S(1)}, f32[8,64,64]{2,0,1:T(8,128)S(1)}, u32[]{:S(2)}, u32[]{:S(2)}) collective-permute-start(f32[8,64,64]{2,0,1:T(8,128)S(1)} %get-tuple-element.20), channel_id=1, source_target_pairs={{0,64},{1,65},{2,66},{3,67},{4,68},{5,69},{6,70},{7,71},{40,104},{... | collective-permute-start | bytes 393224 | tf_op jit(solution)/shard_map/ppermute | solution.py:208
  53.5 13.9 %collective-permute-start.9 = (f32[8,64,64]{2,0,1:T(8,128)S(1)}, f32[8,64,64]{2,0,1:T(8,128)S(1)}, u32[]{:S(2)}, u32[]{:S(2)}) collective-permute-start(f32[8,64,64]{2,0,1:T(8,128)S(1)} %get-tuple-element.20), channel_id=1, source_target_pairs={{0,32},{1,33},{2,34},{3,35},{4,36},{5,37},{6,38},{7,39},{40,72},{4... | collective-permute-start | bytes 393224 | tf_op jit(solution)/shard_map/ppermute | solution.py:208

commit v15 on v13

--- a/solution.py
+++ b/solution.py
@@ -9,7 +9,7 @@
 from jax.sharding import PartitionSpec as P
 
 HIGHEST = lax.Precision.HIGHEST
-TILE_ROWS = 2048
+TILE_ROWS = 4096
 
 
 def split_bf16(value):

time: 78.3 us -> 80.7 us (1.031)
  Pallas kernels: 16 us -> 18.3 us
    pallas_call x1, Pallas kernels: 7.95 us -> 10.3 us  [apply_update(): pl.pallas_call(kernel, out_shape=jax.ShapeDtypeStruct(front.shape, front....]
  transfers between devices with their start and end apart: 12 -> 12, of which waited for: 5 -> 5; matrix products, arithmetic and copies ran while one was open for 19% -> 18% of each run, Pallas kernels for 10% -> 10%
where the time goes in v15:
time: 80.7 us; the launch traced here: 80.2 us
  waiting for transfers between devices  22.2 us (28%)
  Pallas kernels  18.3 us (23%)
  starting transfers between devices  16.4 us (20%)
  local copies, waits for them, and re-layouts  13.4 us (17%)
  other arithmetic  5.51 us (7%)
  matrix products  4.01 us (5%)
    ppermute x4, waiting for transfers between devices, send(): lax.ppermute(value, ('prow', 'pcol'), [(owner[c] * col_count + c, (owner[...  12 us
    pallas_call x1, Pallas kernels, apply_update(): pl.pallas_call(kernel, out_shape=jax.ShapeDtypeStruct(front.shape, front....  10.3 us
    ppermute x5, waiting for transfers between devices, doubling_gather(): other = lax.ppermute(block, axis, [(i, i ^ mask) for i in range(count)])  10.2 us
    pallas_call x1, Pallas kernels, invert_spd(): pl.pallas_call(inverse_kernel, out_shape=jax.ShapeDtypeStruct(matrix.shap...  8.03 us
    ppermute x5, starting transfers between devices, doubling_gather(): other = lax.ppermute(block, axis, [(i, i ^ mask) for i in range(count)])  7.39 us
    ppermute x3, starting transfers between devices, per_device(): lax.ppermute(diag_blocks, 'prow', [(i, (i + k) % row_count) for i in rang...  5 us
    ppermute x4, starting transfers between devices, send(): lax.ppermute(value, ('prow', 'pcol'), [(owner[c] * col_count + c, (owner[...  3.97 us
    unnamed x9, local copies, waits for them, and re-layouts  3.41 us
  transfers between devices with their start and end apart: 12, of which 5 were waited for; matrix products, arithmetic and copies ran while one was open for 18% of the time, Pallas kernels for 10%

profile of v15, /device:TPU:14, one launch (start us, length us, event | category | flops | bytes accessed | tf_op | source)
XLA Modules:
  0.0 80.2 jit_solution(4591271411669334074)
XLA Ops:
  0.0 0.9 %copy.53 = f32[1,64,128]{2,1,0:T(8,128)S(1)} copy(f32[1,64,128]{1,2,0:T(8,128)} %bitcast.49) | data formatting | bytes 65536 | tf_op jit(solution)/shard_map/broadcast_in_dim;reshape | solution.py:170
  0.9 4.0 %collective-permute-start = (f32[1,64,128]{2,1,0:T(8,128)S(1)}, f32[1,64,128]{2,1,0:T(8,128)S(1)}, u32[]{:S(2)}, u32[]{:S(2)}) collective-permute-start(f32[1,64,128]{2,1,0:T(8,128)S(1)} %copy.53), channel_id=1, source_target_pairs={{0,16},{1,17},{2,18},{3,19},{4,20},{5,21},{6,22},{7,23},{8,24},{9,... | collective-permute-start | bytes 98312 | tf_op jit(solution)/shard_map/ppermute | solution.py:145
  4.9 0.7 constant_dynamic-slice_fusion
  5.8 0.8 compare_reduce_fusion
  6.6 0.7 broadcast_xor_fusion
  7.4 1.1 %collective-permute-start.1 = (f32[2,64,128]{2,1,0:T(8,128)S(1)}, f32[2,64,128]{2,1,0:T(8,128)S(1)}, u32[]{:S(2)}, u32[]{:S(2)}) collective-permute-start(f32[2,64,128]{2,1,0:T(8,128)S(1)} %pad_maximum_fusion.3), channel_id=1, source_target_pairs={{0,8},{1,9},{2,10},{3,11},{4,12},{5,13},{6,14},{7,15},{8,0},{9,1},... | collective-permute-start | bytes 196616 | tf_op jit(solution)/shard_map/ppermute | solution.py:145
  8.5 3.2 %collective-permute-done.1 = f32[2,64,128]{2,1,0:T(8,128)S(1)} collective-permute-done((f32[2,64,128]{2,1,0:T(8,128)S(1)}, f32[2,64,128]{2,1,0:T(8,128)S(1)}, u32[]{:S(2)}, u32[]{:S(2)}) %collective-permute-start.1) | collective-permute-done | bytes 65568 | tf_op jit(solution)/shard_map/ppermute | solution.py:145
  11.8 1.5 %collective-permute-start.2 = (f32[4,64,128]{2,1,0:T(8,128)S(1)}, f32[4,64,128]{2,1,0:T(8,128)S(1)}, u32[]{:S(2)}, u32[]{:S(2)}) collective-permute-start(f32[4,64,128]{2,1,0:T(8,128)S(1)} %pad_maximum_fusion.2), channel_id=1, source_target_pairs={{0,4},{1,5},{2,6},{3,7},{4,0},{5,1},{6,2},{7,3},{8,12},{9,13},{10,... | collective-permute-start | bytes 393224 | tf_op jit(solution)/shard_map/ppermute | solution.py:145
  13.3 1.4 %gather_fusion = s32[32]{0:T(128)S(1)} fusion(s32[32]{0:T(128)} %constant.101.clone, s32[1024]{0:T(1024)S(1)} %pad_clamp_fusion.1), kind=kCustom, calls=%fused_computation | custom fusion | bytes 384 | tf_op jit(solution)/shard_map/jit(_take)/gather | solution.py:175
  15.2 3.2 %collective-permute-done.2 = f32[4,64,128]{2,1,0:T(8,128)S(1)} collective-permute-done((f32[4,64,128]{2,1,0:T(8,128)S(1)}, f32[4,64,128]{2,1,0:T(8,128)S(1)}, u32[]{:S(2)}, u32[]{:S(2)}) %collective-permute-start.2) | collective-permute-done | bytes 131104 | tf_op jit(solution)/shard_map/ppermute | solution.py:145
  18.5 0.9 %collective-permute-start.3 = (f32[8,64,128]{2,1,0:T(8,128)S(1)}, f32[8,64,128]{2,1,0:T(8,128)S(1)}, u32[]{:S(2)}, u32[]{:S(2)}) collective-permute-start(f32[8,64,128]{2,1,0:T(8,128)S(1)} %pad_maximum_fusion.1), channel_id=1, source_target_pairs={{0,2},{1,3},{2,0},{3,1},{4,6},{5,7},{6,4},{7,5},{8,10},{9,11},{10,... | collective-permute-start | bytes 786440 | tf_op jit(solution)/shard_map/ppermute | solution.py:145
  20.6 0.6 constant_dynamic-update-slice_fusion.1
  21.2 3.7 %collective-permute-done.3 = f32[8,64,128]{2,1,0:T(8,128)S(1)} collective-permute-done((f32[8,64,128]{2,1,0:T(8,128)S(1)}, f32[8,64,128]{2,1,0:T(8,128)S(1)}, u32[]{:S(2)}, u32[]{:S(2)}) %collective-permute-start.3) | collective-permute-done | bytes 262176 | tf_op jit(solution)/shard_map/ppermute | solution.py:145
  24.9 0.7 constant_dynamic-update-slice_fusion.near_ref
  26.2 2.6 %collective-permute-start.6 = (f32[2,16,64]{2,1,0:T(8,128)}, f32[2,16,64]{2,1,0:T(8,128)S(1)}, u32[]{:S(2)}, u32[]{:S(2)}) collective-permute-start(f32[2,16,64]{2,1,0:T(8,128)} %param.6), channel_id=1, source_target_pairs={{0,64},{32,96},{64,0},{96,32},{1,65},{33,97},{65,1},{97,33},{2,66}... | collective-permute-start | bytes 24584 | tf_op jit(solution)/shard_map/ppermute | solution.py:178
  28.8 1.9 %collective-permute-start.5 = (f32[2,16,64]{2,1,0:T(8,128)}, f32[2,16,64]{2,1,0:T(8,128)S(1)}, u32[]{:S(2)}, u32[]{:S(2)}) collective-permute-start(f32[2,16,64]{2,1,0:T(8,128)} %param.6), channel_id=1, source_target_pairs={{0,32},{32,64},{64,96},{96,0},{1,33},{33,65},{65,97},{97,1},{2,34}... | collective-permute-start | bytes 24584 | tf_op jit(solution)/shard_map/ppermute | solution.py:178
  30.7 0.7 pad_add_fusion.place_ref
  31.3 0.9 %copy.35 = f32[2,64,64]{1,2,0:T(8,128)S(1)} copy(f32[2,64,64]{2,1,0:T(8,128)} %param.7) | data formatting | bytes 65536 | tf_op args[1]
  32.9 0.7 broadcast_in_dim.122
  36.7 1.1 %fusion = f32[2,8,64,64]{3,1,2,0:T(8,128)S(1)} fusion(f32[16,64,2,64]{3,2,1,0:T(2,128)S(1)} %reshape.86, pred[2,8,32]{2,1,0:T(8,128)(4,1)S(1)} %compare_and_fusion), kind=kOutput, calls=%fused_computation.3 | convolution fusion | flops 12582912 | bytes 786944 | tf_op jit(solution)/shard_map/pjk,kbpa->pjba/dot_general | solution.py:195
  39.1 0.7 collective-permute-start.10
  39.8 0.7 collective-permute-start.11
  40.6 1.2 %gather_fusion.1 = s32[128]{0:T(128)S(1)} fusion(s32[32]{0:T(128)S(1)} %and_select_fusion, s32[1024]{0:T(1024)S(1)} %pad_clamp_fusion), kind=kCustom, calls=%fused_computation.1 | custom fusion | bytes 1536 | tf_op jit(solution)/shard_map/jit(_take)/gather | solution.py:204
  42.1 1.3 %collective-permute-start.8 = (f32[8,64,64]{2,0,1:T(8,128)S(1)}, f32[8,64,64]{2,0,1:T(8,128)S(1)}, u32[]{:S(2)}, u32[]{:S(2)}) collective-permute-start(f32[8,64,64]{2,0,1:T(8,128)S(1)} %get-tuple-element.19), channel_id=1, source_target_pairs={{0,32},{1,33},{2,34},{3,35},{4,36},{5,37},{6,38},{7,39},{40,72},{4... | collective-permute-start | bytes 393224 | tf_op jit(solution)/shard_map/ppermute | solution.py:208
  43.4 1.3 %collective-permute-start.9 = (f32[8,64,64]{2,0,1:T(8,128)S(1)}, f32[8,64,64]{2,0,1:T(8,128)S(1)}, u32[]{:S(2)}, u32[]{:S(2)}) collective-permute-start(f32[8,64,64]{2,0,1:T(8,128)S(1)} %get-tuple-element.20), channel_id=1, source_target_pairs={{0,32},{1,33},{2,34},{3,35},{4,36},{5,37},{6,38},{7,39},{40,72},{4... | collective-permute-start | bytes 393224 | tf_op jit(solution)/shard_map/ppermute | solution.py:208
  44.7 0.7 pad_maximum_fusion.4.system_ref
  45.4 8.0 %shard_map.64 = f32[2,64,64]{2,1,0:T(8,128)} custom-call(f32[2,64,128]{2,1,0:T(8,128)} %pad_maximum_fusion.4.system_ref), custom_call_target="tpu_custom_call" | custom-call | flops 4194304 | bytes 98304 | tf_op jit(solution)/shard_map/pallas_call | solution.py:127
  54.0 8.2 %collective-permute-done.8 = f32[8,64,64]{2,0,1:T(8,128)S(1)} collective-permute-done((f32[8,64,64]{2,0,1:T(8,128)S(1)}, f32[8,64,64]{2,0,1:T(8,128)S(1)}, u32[]{:S(2)}, u32[]{:S(2)}) %collective-permute-start.8) | collective-permute-done | bytes 131104 | tf_op jit(solution)/shard_map/ppermute | solution.py:208
  62.2 3.8 %collective-permute-done.9 = f32[8,64,64]{2,0,1:T(8,128)S(1)} collective-permute-done((f32[8,64,64]{2,0,1:T(8,128)S(1)}, f32[8,64,64]{2,0,1:T(8,128)S(1)}, u32[]{:S(2)}, u32[]{:S(2)}) %collective-permute-start.9) | collective-permute-done | bytes 131104 | tf_op jit(solution)/shard_map/ppermute | solution.py:208
  66.1 2.5 %fusion.3 = f32[2,64,8,64]{3,1,2,0:T(8,128)S(1)} fusion(f32[2,8,64,64]{3,1,2,0:T(8,128)S(1)} %fusion.2, f32[2,64,64]{2,1,0:T(8,128)} %shard_map.64), kind=kOutput, calls=%fused_computation.7 | convolution fusion | flops 50331648 | bytes 557056 | tf_op jit(solution)/shard_map/pxa,pjba->pxjb/dot_general | solution.py:215
  69.1 0.8 pad_maximum_fusion.stack_ref
  69.9 10.3 %shard_map.65 = f32[4096,512]{1,0:T(8,128)} custom-call(s32[2,64]{1,0:T(2,128)} %compare_select_fusion.5.table_ref, s32[2]{0:T(128)} %pad_add_fusion.place_ref, f32[16,64,128]{2,1,0:T(8,128)} %constant_dynamic-update-slice_fusion.near_ref, f32[16,64,128]{2,1,0:T(8,128)} %copy-done, bf16[384,512]{1,0:T(8,128)(2,1)} %pad_maximum_fusion.stack_ref, ...), custom_call_target="tpu_custom_call" | custom-call | flops 1610612736 | bytes 18219008 | tf_op jit(solution)/shard_map/pallas_call | solution.py:78
  (72 shorter events, 9.1 us)
Async XLA Ops:
  0.0 38.3 %copy-start.1 = (s32[2,128]{1,0:T(2,128)S(1)}, s32[2,128]{1,0:T(2,128)}, u32[]{:S(2)}) copy-start(s32[2,128]{1,0:T(2,128)} %param.8) | copy-start | bytes 3076
  0.9 6.5 %collective-permute-start = (f32[1,64,128]{2,1,0:T(8,128)S(1)}, f32[1,64,128]{2,1,0:T(8,128)S(1)}, u32[]{:S(2)}, u32[]{:S(2)}) collective-permute-start(f32[1,64,128]{2,1,0:T(8,128)S(1)} %copy.53), channel_id=1, source_target_pairs={{0,16},{1,17},{2,18},{3,19},{4,20},{5,21},{6,22},{7,23},{8,24},{9,... | collective-permute-start | bytes 98312 | tf_op jit(solution)/shard_map/ppermute | solution.py:145
  7.4 4.3 %collective-permute-start.1 = (f32[2,64,128]{2,1,0:T(8,128)S(1)}, f32[2,64,128]{2,1,0:T(8,128)S(1)}, u32[]{:S(2)}, u32[]{:S(2)}) collective-permute-start(f32[2,64,128]{2,1,0:T(8,128)S(1)} %pad_maximum_fusion.3), channel_id=1, source_target_pairs={{0,8},{1,9},{2,10},{3,11},{4,12},{5,13},{6,14},{7,15},{8,0},{9,1},... | collective-permute-start | bytes 196616 | tf_op jit(solution)/shard_map/ppermute | solution.py:145
  11.8 6.7 %collective-permute-start.2 = (f32[4,64,128]{2,1,0:T(8,128)S(1)}, f32[4,64,128]{2,1,0:T(8,128)S(1)}, u32[]{:S(2)}, u32[]{:S(2)}) collective-permute-start(f32[4,64,128]{2,1,0:T(8,128)S(1)} %pad_maximum_fusion.2), channel_id=1, source_target_pairs={{0,4},{1,5},{2,6},{3,7},{4,0},{5,1},{6,2},{7,3},{8,12},{9,13},{10,... | collective-permute-start | bytes 393224 | tf_op jit(solution)/shard_map/ppermute | solution.py:145
  18.5 6.5 %collective-permute-start.3 = (f32[8,64,128]{2,1,0:T(8,128)S(1)}, f32[8,64,128]{2,1,0:T(8,128)S(1)}, u32[]{:S(2)}, u32[]{:S(2)}) collective-permute-start(f32[8,64,128]{2,1,0:T(8,128)S(1)} %pad_maximum_fusion.1), channel_id=1, source_target_pairs={{0,2},{1,3},{2,0},{3,1},{4,6},{5,7},{6,4},{7,5},{8,10},{9,11},{10,... | collective-permute-start | bytes 786440 | tf_op jit(solution)/shard_map/ppermute | solution.py:145
  25.6 10.5 %collective-permute-start.4 = (f32[16,64,128]{2,1,0:T(8,128)}, f32[16,64,128]{2,1,0:T(8,128)S(1)}, u32[]{:S(2)}, u32[]{:S(2)}) collective-permute-start(f32[16,64,128]{2,1,0:T(8,128)} %constant_dynamic-update-slice_fusion.near_ref), channel_id=1, source_target_pairs={{0,1},{1,0},{2,3},{3,2},{4,5},{5,4},{6,7},{7,6},{8,9},{9,8},{10,11... | collective-permute-start | bytes 1572872 | tf_op jit(solution)/shard_map/ppermute | solution.py:145
  25.7 8.4 %collective-permute-start.7 = (f32[2,16,64]{2,1,0:T(8,128)}, f32[2,16,64]{2,1,0:T(8,128)S(1)}, u32[]{:S(2)}, u32[]{:S(2)}) collective-permute-start(f32[2,16,64]{2,1,0:T(8,128)} %param.6), channel_id=1, source_target_pairs={{0,96},{32,0},{64,32},{96,64},{1,97},{33,1},{65,33},{97,65},{2,98}... | collective-permute-start | bytes 24584 | tf_op jit(solution)/shard_map/ppermute | solution.py:178
  26.2 7.8 %collective-permute-start.6 = (f32[2,16,64]{2,1,0:T(8,128)}, f32[2,16,64]{2,1,0:T(8,128)S(1)}, u32[]{:S(2)}, u32[]{:S(2)}) collective-permute-start(f32[2,16,64]{2,1,0:T(8,128)} %param.6), channel_id=1, source_target_pairs={{0,64},{32,96},{64,0},{96,32},{1,65},{33,97},{65,1},{97,33},{2,66}... | collective-permute-start | bytes 24584 | tf_op jit(solution)/shard_map/ppermute | solution.py:178
  28.8 5.1 %collective-permute-start.5 = (f32[2,16,64]{2,1,0:T(8,128)}, f32[2,16,64]{2,1,0:T(8,128)S(1)}, u32[]{:S(2)}, u32[]{:S(2)}) collective-permute-start(f32[2,16,64]{2,1,0:T(8,128)} %param.6), channel_id=1, source_target_pairs={{0,32},{32,64},{64,96},{96,0},{1,33},{33,65},{65,97},{97,1},{2,34}... | collective-permute-start | bytes 24584 | tf_op jit(solution)/shard_map/ppermute | solution.py:178
  36.1 33.8 %copy-start = (f32[16,64,128]{2,1,0:T(8,128)}, f32[16,64,128]{2,1,0:T(8,128)S(1)}, u32[]{:S(2)}) copy-start(f32[16,64,128]{2,1,0:T(8,128)S(1)} %collective-permute-done.4.far_ref) | copy-start | bytes 1572868
  39.1 26.9 %collective-permute-start.10 = (f32[2,8,64,64]{3,1,2,0:T(8,128)S(1)}, f32[2,8,64,64]{3,1,2,0:T(8,128)S(1)}, u32[]{:S(2)}, u32[]{:S(2)}) collective-permute-start(f32[2,8,64,64]{3,1,2,0:T(8,128)S(1)} %convolution_add_fusion), channel_id=1, source_target_pairs={{0,64},{1,65},{2,66},{3,67},{4,68},{5,69},{6,70},{7,71},{40,104},{... | collective-permute-start | bytes 786440 | tf_op jit(solution)/shard_map/ppermute | solution.py:208
  39.8 26.2 %collective-permute-start.11 = (f32[2,8,64,64]{3,1,2,0:T(8,128)S(1)}, f32[2,8,64,64]{3,1,2,0:T(8,128)S(1)}, u32[]{:S(2)}, u32[]{:S(2)}) collective-permute-start(f32[2,8,64,64]{3,1,2,0:T(8,128)S(1)} %convolution_add_fusion), channel_id=1, source_target_pairs={{0,96},{1,97},{2,98},{3,99},{4,100},{5,101},{6,102},{7,103}} | collective-permute-start | bytes 786440 | tf_op jit(solution)/shard_map/ppermute | solution.py:208
  42.1 20.1 %collective-permute-start.8 = (f32[8,64,64]{2,0,1:T(8,128)S(1)}, f32[8,64,64]{2,0,1:T(8,128)S(1)}, u32[]{:S(2)}, u32[]{:S(2)}) collective-permute-start(f32[8,64,64]{2,0,1:T(8,128)S(1)} %get-tuple-element.19), channel_id=1, source_target_pairs={{0,32},{1,33},{2,34},{3,35},{4,36},{5,37},{6,38},{7,39},{40,72},{4... | collective-permute-start | bytes 393224 | tf_op jit(solution)/shard_map/ppermute | solution.py:208
  43.4 22.7 %collective-permute-start.9 = (f32[8,64,64]{2,0,1:T(8,128)S(1)}, f32[8,64,64]{2,0,1:T(8,128)S(1)}, u32[]{:S(2)}, u32[]{:S(2)}) collective-permute-start(f32[8,64,64]{2,0,1:T(8,128)S(1)} %get-tuple-element.20), channel_id=1, source_target_pairs={{0,32},{1,33},{2,34},{3,35},{4,36},{5,37},{6,38},{7,39},{40,72},{4... | collective-permute-start | bytes 393224 | tf_op jit(solution)/shard_map/ppermute | solution.py:208
